TPU v7x, 512 devices: a whole 4x4x16 slice. The times are simulated.
512 devices in a mesh: tensor: 4 (over x), request: 128 (over z, y, core).
Axes of the slice: x: 4, y: 4, z: 16, core: 2. Of those that a mesh axis runs over, the one named last changes fastest.
Arguments:
- hidden: bfloat16 [1024, 2048], P('request'), may hold values from -6 to 6
- norm_gain: float32 [2048], replicated, may hold values from 0.1 to 1.9
- w_query: bfloat16 [2048, 2048], P(None, 'tensor'), may hold values from -0.125 to 0.125
- w_keyval: bfloat16 [2048, 512], P(None, 'tensor'), may hold values from -0.125 to 0.125
- w_output: bfloat16 [2048, 2048], P('tensor'), may hold values from -0.125 to 0.125
- node_cache: bfloat16 [128, 4, 512, 128], P('request', 'tensor'), may hold values from -300 to 300
- leaf_cache: bfloat16 [1024, 4, 128, 128], P('request', 'tensor'), may hold values from -300 to 300
- leaf_branch: int32 [1024], replicated, may hold values from 0 to 63
- branch_root: int32 [64], replicated, may hold values from 0 to 7
- root_owner: int32 [8], replicated, may hold values from 0 to 127, as said below
- branch_owner: int32 [64], replicated, may hold values from 1 to 126, as said below
- root_len: int32 [8], replicated, may hold values from 1 to 512, as said below
- branch_len: int32 [64], replicated, may hold values from 1 to 512, as said below
- leaf_len: int32 [1024], P('request'), may hold values from 0 to 127, as said below
Outputs:
- mixed: bfloat16 [1024, 2048], P('request', 'tensor')
- new_entries: bfloat16 [1024, 4, 128], P('request', 'tensor')
Inputs may be any that keep to these rules, and one draw needn't show every extreme that they name: The 8 entries of root_owner are all different slots. `branch_owner`: different from every entry of root_owner and from one another. `root_len`: some root has exactly 512 positions. `branch_len`: some branch has exactly 512 positions. `leaf_len`: some leaf has exactly 127 positions.
All inputs are finite; a program needn't handle non-finite values.
Results may differ from a plain program's by a relative error of at most 0.029.
Values may be sent and summed in bfloat16 or wider, within the bound.
No kernel may reach another device: no remote copies, remote signals or barrier semaphores. Data moves between devices by JAX's collectives and lax.ppermute only.
A program may use at most 128 MiB of HBM per device.

v0:
```python
import jax
import jax.numpy as jnp
from jax import lax
from jax.sharding import PartitionSpec as P

FLOOR = -1e30


def rotate(values_in, positions):
    half_dim = values_in.shape[-1] // 2
    inverse_freq = 10000.0 ** (
        -(jnp.arange(half_dim, dtype=jnp.float32) * 2.0 / values_in.shape[-1])
    )
    angles = positions.astype(jnp.float32)[..., None] * inverse_freq
    angles = jnp.concatenate([angles, angles], -1)
    turned = jnp.concatenate([-values_in[..., half_dim:], values_in[..., :half_dim]], -1)
    return values_in * jnp.cos(angles) + turned * jnp.sin(angles)


def soft_part(scores, usable, value_rows, pattern):
    scores = jnp.where(usable, scores, FLOOR)
    peak = jnp.max(scores, -1)
    weights = jnp.where(usable, jnp.exp(scores - peak[..., None]), 0.0).astype(jnp.bfloat16)
    summed = jnp.einsum(pattern, weights, value_rows, preferred_element_type=jnp.float32)
    weight_sum = jnp.sum(weights.astype(jnp.float32), -1)
    return (summed, weight_sum, peak)


def local(
    hidden,
    norm_gain,
    w_query,
    w_keyval,
    w_output,
    node_cache,
    leaf_cache,
    leaf_branch,
    branch_root,
    root_owner,
    branch_owner,
    root_len,
    branch_len,
    leaf_len,
):
    head_dim = w_keyval.shape[1] // 2
    local_leaves = hidden.shape[0]
    group = w_query.shape[1] // head_dim
    factor = head_dim ** (-0.5)
    device = lax.axis_index("request")
    offset = device * local_leaves
    widened = hidden.astype(jnp.float32)
    normed = (
        widened * lax.rsqrt(jnp.mean(widened * widened, -1, keepdims=True) + 1e-05) * norm_gain
    ).astype(jnp.bfloat16)
    branch_ids = jnp.arange(branch_root.shape[0], dtype=jnp.int32)
    root_ids = jnp.arange(root_owner.shape[0], dtype=jnp.int32)
    branch_hits = leaf_branch[:, None] == branch_ids[None, :]
    leaf_root = jnp.sum(jnp.where(branch_hits, branch_root[None, :], 0), 1)
    root_hits = leaf_root[:, None] == root_ids[None, :]
    prefix_all = jnp.sum(jnp.where(root_hits, root_len[None, :], 0), 1) + jnp.sum(
        jnp.where(branch_hits, branch_len[None, :], 0), 1
    )
    positions = lax.dynamic_slice_in_dim(prefix_all, offset, local_leaves) + leaf_len
    raw_query = jnp.dot(normed, w_query, preferred_element_type=jnp.float32).reshape(
        local_leaves, group, head_dim
    )
    queries = rotate(raw_query, positions[:, None]).astype(jnp.bfloat16)
    raw_entry = jnp.dot(normed, w_keyval, preferred_element_type=jnp.float32)
    new_entry = jnp.concatenate(
        [rotate(raw_entry[:, :head_dim], positions), raw_entry[:, head_dim:]], -1
    ).astype(jnp.bfloat16)
    leaf_rows = leaf_cache[:, 0]
    slot_index = jnp.arange(leaf_rows.shape[1], dtype=jnp.int32)
    appended = jnp.where(
        (slot_index[None, :] == leaf_len[:, None])[:, :, None], new_entry[:, None, :], leaf_rows
    )
    leaf_scores = (
        jnp.einsum(
            "lgd,lkd->lgk", queries, appended[:, :, :head_dim], preferred_element_type=jnp.float32
        )
        * factor
    )
    leaf_usable = (slot_index[None, :] <= leaf_len[:, None])[:, None, :]
    leaf_sum, leaf_weight, leaf_peak = soft_part(
        leaf_scores, leaf_usable, appended[:, :, head_dim:], "lgk,lkd->lgd"
    )
    everyone = lax.all_gather(
        queries.reshape(local_leaves, group * head_dim), "request", axis=0, tiled=True
    )
    total_leaves = everyone.shape[0]
    mine_all = jnp.any(branch_hits & (branch_owner == device)[None, :], 1) | jnp.any(
        root_hits & (root_owner == device)[None, :], 1
    )
    my_length = jnp.sum(jnp.where(root_owner == device, root_len, 0)) + jnp.sum(
        jnp.where(branch_owner == device, branch_len, 0)
    )
    node_rows = node_cache[0, 0]
    node_usable = jnp.arange(node_rows.shape[0], dtype=jnp.int32) < my_length
    block_rows = 128
    block_count = total_leaves // block_rows

    def owner_block(stacked_in):
        rows_query, rows_mine = stacked_in
        scores = (
            jnp.einsum(
                "ngd,kd->ngk",
                rows_query,
                node_rows[:, :head_dim],
                preferred_element_type=jnp.float32,
            )
            * factor
        )
        usable = rows_mine[:, None, None] & node_usable[None, None, :]
        return soft_part(scores, usable, node_rows[:, head_dim:], "ngk,kd->ngd")

    results = lax.map(
        owner_block,
        (
            everyone.reshape(block_count, block_rows, group, head_dim),
            mine_all.reshape(block_count, block_rows),
        ),
    )
    own_sum = results[0].reshape(total_leaves, group, head_dim)
    own_weight = results[1].reshape(total_leaves, group)
    own_peak = results[2].reshape(total_leaves, group)
    global_peak = lax.pmax(own_peak.astype(jnp.bfloat16), "request").astype(own_peak.dtype)
    scaled = jnp.exp(own_peak - global_peak)
    shared_sum, remote_weight = (
        lax.psum_scatter(
            (scaled[..., None] * own_sum).reshape(total_leaves, group * head_dim),
            "request",
            scatter_dimension=0,
            tiled=True,
        ),
        lax.psum_scatter(scaled * own_weight, "request", scatter_dimension=0, tiled=True),
    )
    remote_sum = shared_sum.reshape(local_leaves, group, head_dim)
    remote_peak = lax.dynamic_slice_in_dim(global_peak, offset, local_leaves)
    peak = jnp.maximum(remote_peak, leaf_peak)
    remote_scale = jnp.exp(remote_peak - peak)
    leaf_scale = jnp.exp(leaf_peak - peak)
    numerator = remote_scale[..., None] * remote_sum + leaf_scale[..., None] * leaf_sum
    denominator = remote_scale * remote_weight + leaf_scale * leaf_weight
    attended = (
        (numerator / denominator[..., None])
        .astype(jnp.bfloat16)
        .reshape(local_leaves, group * head_dim)
    )
    term = jnp.dot(attended, w_output, preferred_element_type=jnp.float32)
    mixed = lax.psum_scatter(term, "tensor", scatter_dimension=1, tiled=True).astype(jnp.bfloat16)
    return (mixed, new_entry[:, None, :])


def solution(mesh):
    in_specs = (
        P("request", None),
        P(),
        P(None, "tensor"),
        P(None, "tensor"),
        P("tensor", None),
        P("request", "tensor", None, None),
        P("request", "tensor", None, None),
        P(),
        P(),
        P(),
        P(),
        P(),
        P(),
        P("request"),
    )
    out_specs = (P("request", "tensor"), P("request", "tensor", None))
    return jax.shard_map(local, mesh=mesh, in_specs=in_specs, out_specs=out_specs, check_vma=False)
```

profile of v0, /device:TPU:24, one launch (start us, length us, event | category | flops | bytes accessed | tf_op | source)
XLA Modules:
  0.0 1273.7 jit_solution(6114707259069529670)
XLA Ops:
  7.3 1.0 fusion.20
  8.4 1.3 fusion.27
  9.7 2.1 fusion.29
  12.7 0.6 add_convert_fusion.2
  13.6 0.6 select_reduce_fusion.4
  14.2 0.6 select_reduce_fusion.3
  16.3 0.6 or_bitcast_fusion
  16.9 131.9 %all-gather.2.cloned.1.call-done = bf16[1024,512]{1,0:T(8,128)(2,1)} async-done(((bf16[8,512]{1,0:T(8,128)(2,1)}), bf16[1024,512]{1,0:T(8,128)(2,1)}) %all-gather.2.cloned.1.call-update) | async-done | bytes 1048592 | tf_op jit(solution)/shard_map/all_gather | solution.py:87
  148.7 3.9 reshape.275
  152.6 2.3 copy.55
  154.9 88.6 %while.15 = (s32[]{:T(128)}, f32[8,128,8,64]{1,0,3,2:T(8,128)}, f32[8,128,8]{1,2,0:T(8,128)}, f32[8,128,8]{1,2,0:T(8,128)}, pred[8,128]{1,0:T(8,128)(4,1)}, /*in...) while((s32[]{:T(128)}, f32[8,128,8,64]{1,0,3,2:T(8,128)}, ...), condition=%wide.region_11.12_spmd.clone, body=%wide.region_8.11_spmd.clone.sunk | while | flops 142146048 | bytes 7636981 | solution.py:116
  154.9 0.7 dynamic-slice_bitcast_fusion.2
  156.3 0.7 convert_reduce_fusion.3
  157.0 0.6 bitcast_dynamic-update-slice_fusion.3
  157.6 0.7 fusion.52
  158.3 7.7 dynamic_update_slice.19
  166.0 0.7 dynamic-slice_bitcast_fusion.2
  167.4 0.7 convert_reduce_fusion.3
  168.1 0.6 bitcast_dynamic-update-slice_fusion.3
  168.7 0.7 fusion.52
  169.4 7.7 dynamic_update_slice.19
  177.1 0.7 dynamic-slice_bitcast_fusion.2
  178.4 0.7 convert_reduce_fusion.3
  179.1 0.6 bitcast_dynamic-update-slice_fusion.3
  179.7 0.7 fusion.52
  180.4 7.7 dynamic_update_slice.19
  188.2 0.7 dynamic-slice_bitcast_fusion.2
  189.5 0.7 convert_reduce_fusion.3
  190.2 0.6 bitcast_dynamic-update-slice_fusion.3
  190.8 0.7 fusion.52
  191.5 7.7 dynamic_update_slice.19
  199.2 0.7 dynamic-slice_bitcast_fusion.2
  200.6 0.7 convert_reduce_fusion.3
  201.3 0.6 bitcast_dynamic-update-slice_fusion.3
  201.9 0.7 fusion.52
  202.6 7.7 dynamic_update_slice.19
  210.3 0.7 dynamic-slice_bitcast_fusion.2
  211.7 0.7 convert_reduce_fusion.3
  212.4 0.6 bitcast_dynamic-update-slice_fusion.3
  213.0 0.7 fusion.52
  213.7 7.7 dynamic_update_slice.19
  221.4 0.7 dynamic-slice_bitcast_fusion.2
  222.7 0.7 convert_reduce_fusion.3
  223.4 0.6 bitcast_dynamic-update-slice_fusion.3
  224.0 0.7 fusion.52
  224.7 7.7 dynamic_update_slice.19
  232.5 0.7 dynamic-slice_bitcast_fusion.2
  233.8 0.7 convert_reduce_fusion.3
  234.5 0.6 bitcast_dynamic-update-slice_fusion.3
  235.1 0.7 fusion.52
  235.8 7.7 dynamic_update_slice.19
  243.5 0.8 bitcast_convert_fusion
  244.3 480.1 %pmax.7 = bf16[1024,8]{0,1:T(8,128)(2,1)S(1)} all-reduce(bf16[1024,8]{0,1:T(8,128)(2,1)S(1)} %bitcast_convert_fusion), channel_id=1, replica_groups=mesh['tensor'=4,'request'=128] {'request'}, use_global_device_ids=true, to_apply=%region_12.13 | all-reduce | flops 8192 | bytes 32768 | tf_op jit(solution)/shard_map/pmax | solution.py:126
  724.4 0.8 bitcast_multiply_fusion.1
  725.2 3.4 bitcast_multiply_fusion
  728.6 2.9 copy.68
  731.7 0.8 copy-done.5
  733.6 1.3 dynamic-slice
  735.5 491.0 %all-reduce = f32[1024,8]{0,1:T(8,128)S(1)} all-reduce(f32[1024,8]{0,1:T(8,128)S(1)} %get-tuple-element.129), channel_id=3, replica_groups=mesh['tensor'=4,'request'=128] {'request'}, use_global_device_ids=true, to_apply=%region_15.16.clone | all-reduce | flops 8192 | bytes 65536
  1226.8 0.8 copy.69
  1228.1 1.0 fusion.42
  1229.3 0.7 pad_maximum_fusion.2
  1229.9 36.0 %reduce-scatter.6.cloned.1.call-done = f32[8,512]{1,0:T(8,128)} async-done(((f32[8,2048]{1,0:T(8,128)}), f32[8,512]{1,0:T(8,128)}) %reduce-scatter.6.cloned.1.call-update) | async-done | bytes 16400 | tf_op jit(solution)/shard_map/reduce_scatter | solution.py:150
  1265.9 1.3 convert_element_type.60
  (96 shorter events, 8.7 us)
Async XLA Ops:
  7.2 1221.0 %copy-start = (bf16[512,2048]{1,0:T(8,128)(2,1)S(1)}, bf16[512,2048]{1,0:T(8,128)(2,1)}, u32[]{:S(2)}) copy-start(bf16[512,2048]{1,0:T(8,128)(2,1)} %param.20) | copy-start | bytes 6291460
  7.2 4.7 copy-start.7
  7.2 4.7 copy-start.13
  7.2 4.7 copy-start.10
  7.2 4.9 copy-start.8
  7.2 5.0 copy-start.9
  7.2 6.2 copy-start.6
  7.2 6.3 copy-start.11
  7.3 6.9 copy-start.12
  7.3 141.5 %all-gather.2.cloned.1.call-start = ((), (), s32[]{:S(2)}) async-start(), calls=%async_computation.2 | async-start | bytes 1056768 | tf_op jit(solution)/shard_map/all_gather | solution.py:87
  11.8 136.9 %copy-start.1 = (f32[8,8,64]{2,1,0:T(8,128)}, f32[8,8,64]{2,1,0:T(8,128)S(1)}, u32[]{:S(2)}) copy-start(f32[8,8,64]{2,1,0:T(8,128)S(1)} %reshape.266) | copy-start | bytes 49156
  12.5 136.2 %copy-start.3 = (f32[8,8,64]{2,1,0:T(8,128)}, f32[8,8,64]{2,1,0:T(8,128)S(1)}, u32[]{:S(2)}) copy-start(f32[8,8,64]{2,1,0:T(8,128)S(1)} %maximum_multiply_fusion) | copy-start | bytes 49156
  13.3 1213.5 %reduce-scatter.8.cloned.1.call-start = ((), (), s32[]{:S(2)}) async-start(), calls=%async_computation.4 | async-start | bytes 2113536
  731.5 0.9 copy-start.5
  731.5 1.5 copy-start.2
  731.5 1.5 copy-start.4
  731.6 534.3 %reduce-scatter.6.cloned.1.call-start = ((), (), s32[]{:S(2)}) async-start(), calls=%async_computation.3 | async-start | bytes 81920 | tf_op jit(solution)/shard_map/reduce_scatter | solution.py:150
Sparse Core Ops, SparseCore 0:
  13.5 135.2 all-gather.1
  731.7 270.8 reduce-scatter.7
  1229.3 36.5 reduce-scatter.5
where the time goes:
time: 1280 us; the launch traced here: 1270 us
  blocking collectives  971 us (76%)
  waiting for transfers between devices  168 us (13%)
  local copies, waits for them, and re-layouts  85.3 us (7%)
  other arithmetic  18.2 us (1%)
  between operations  15.9 us (1%)
  matrix products  15 us (1%)
    unnamed x1, blocking collectives  491 us
    pmax x1, blocking collectives, local(): lax.pmax(own_peak.astype(jnp.bfloat16), 'request').astype(own_peak.dtype)  480 us
    all_gather x1, waiting for transfers between devices, local(): lax.all_gather(queries.reshape(local_leaves, group * head_dim), 'request'...  132 us
    dynamic_update_slice x16, local copies, waits for them, and re-layouts, local(): lax.map(owner_block, (everyone.reshape(block_count, block_rows, group, he...  66.5 us
    reduce_scatter x1, waiting for transfers between devices, local(): lax.psum_scatter(term, 'tensor', scatter_dimension=1, tiled=True)  36 us
  transfers between devices with their start and end apart: 3, of which 2 were waited for; matrix products, arithmetic and copies ran while one was open for 0% of the time, Pallas kernels for 0%

commit v1 on v0

v1 whole, which is shorter than its diff:
```python
import jax
import jax.numpy as jnp
from jax import lax
from jax.sharding import PartitionSpec as P

FLOOR = -1e30


def rotate(values_in, positions):
    half_dim = values_in.shape[-1] // 2
    inverse_freq = 10000.0 ** (
        -(jnp.arange(half_dim, dtype=jnp.float32) * 2.0 / values_in.shape[-1])
    )
    angles = positions.astype(jnp.float32)[..., None] * inverse_freq
    angles = jnp.concatenate([angles, angles], -1)
    turned = jnp.concatenate([-values_in[..., half_dim:], values_in[..., :half_dim]], -1)
    return values_in * jnp.cos(angles) + turned * jnp.sin(angles)


def soft_part(scores, usable, value_rows, pattern):
    scores = jnp.where(usable, scores, FLOOR)
    peak = jnp.max(scores, -1)
    weights = jnp.where(usable, jnp.exp(scores - peak[..., None]), 0.0).astype(jnp.bfloat16)
    summed = jnp.einsum(pattern, weights, value_rows, preferred_element_type=jnp.float32)
    weight_sum = jnp.sum(weights.astype(jnp.float32), -1)
    return (summed, weight_sum, peak)


def split_two(values):
    high = values.astype(jnp.bfloat16)
    low = (values - high.astype(jnp.float32)).astype(jnp.bfloat16)
    return [high, low]


def split_three(values):
    high = values.astype(jnp.bfloat16)
    rest = values - high.astype(jnp.float32)
    middle = rest.astype(jnp.bfloat16)
    low = (rest - middle.astype(jnp.float32)).astype(jnp.bfloat16)
    return [high, middle, low]


def join(pieces):
    total = pieces[0].astype(jnp.float32)
    for piece in pieces[1:]:
        total = total + piece.astype(jnp.float32)
    return total


def local(
    hidden,
    norm_gain,
    w_query,
    w_keyval,
    w_output,
    node_cache,
    leaf_cache,
    leaf_branch,
    branch_root,
    root_owner,
    branch_owner,
    root_len,
    branch_len,
    leaf_len,
):
    head_dim = w_keyval.shape[1] // 2
    local_leaves = hidden.shape[0]
    group = w_query.shape[1] // head_dim
    factor = head_dim ** (-0.5)
    device = lax.axis_index("request")
    offset = device * local_leaves
    widened = hidden.astype(jnp.float32)
    normed = (
        widened * lax.rsqrt(jnp.mean(widened * widened, -1, keepdims=True) + 1e-05) * norm_gain
    ).astype(jnp.bfloat16)
    leaf_root = branch_root[leaf_branch]
    prefix_all = root_len[leaf_root] + branch_len[leaf_branch]
    positions = lax.dynamic_slice_in_dim(prefix_all, offset, local_leaves) + leaf_len
    raw_query = jnp.dot(normed, w_query, preferred_element_type=jnp.float32).reshape(
        local_leaves, group, head_dim
    )
    queries = rotate(raw_query, positions[:, None]).astype(jnp.bfloat16)
    everyone = lax.all_gather(
        queries.reshape(local_leaves, group * head_dim), "request", axis=0, tiled=True
    )
    raw_entry = jnp.dot(normed, w_keyval, preferred_element_type=jnp.float32)
    new_entry = jnp.concatenate(
        [rotate(raw_entry[:, :head_dim], positions), raw_entry[:, head_dim:]], -1
    ).astype(jnp.bfloat16)
    leaf_rows = leaf_cache[:, 0]
    slot_index = jnp.arange(leaf_rows.shape[1], dtype=jnp.int32)
    appended = jnp.where(
        (slot_index[None, :] == leaf_len[:, None])[:, :, None], new_entry[:, None, :], leaf_rows
    )
    leaf_scores = (
        jnp.einsum(
            "lgd,lkd->lgk", queries, appended[:, :, :head_dim], preferred_element_type=jnp.float32
        )
        * factor
    )
    leaf_usable = (slot_index[None, :] <= leaf_len[:, None])[:, None, :]
    leaf_sum, leaf_weight, leaf_peak = soft_part(
        leaf_scores, leaf_usable, appended[:, :, head_dim:], "lgk,lkd->lgd"
    )

    total_leaves = everyone.shape[0]
    root_mine = root_owner[leaf_root] == device
    branch_mine = branch_owner[leaf_branch] == device
    mine_all = root_mine | branch_mine
    my_length = jnp.sum(jnp.where(root_owner == device, root_len, 0)) + jnp.sum(
        jnp.where(branch_owner == device, branch_len, 0)
    )
    node_rows = node_cache[0, 0]
    node_usable = jnp.arange(node_rows.shape[0], dtype=jnp.int32) < my_length
    rows_query = everyone.reshape(total_leaves, group, head_dim)
    scores = (
        jnp.einsum(
            "ngd,kd->ngk", rows_query, node_rows[:, :head_dim], preferred_element_type=jnp.float32
        )
        * factor
    )
    usable = mine_all[:, None, None] & node_usable[None, None, :]
    own_sum, own_weight, own_peak = soft_part(scores, usable, node_rows[:, head_dim:], "ngk,kd->ngd")
    own_peak = jnp.where(mine_all[:, None], own_peak, 0.0)
    packet = jnp.concatenate(
        [own_sum.reshape(total_leaves, group * head_dim).astype(jnp.bfloat16)]
        + split_two(own_weight)
        + split_three(own_peak),
        -1,
    )
    zeros = jnp.zeros_like(packet)
    packet = jnp.stack(
        [
            jnp.where(root_mine[:, None], packet, zeros),
            jnp.where(branch_mine[:, None], packet, zeros),
        ],
        1,
    )
    width = packet.shape[-1]
    gathered = lax.psum_scatter(
        packet.reshape(total_leaves * 2, width), "request", scatter_dimension=0, tiled=True
    ).reshape(local_leaves, 2, width)
    sums = []
    weights = []
    peaks = []
    for part in range(2):
        piece = gathered[:, part]
        sums.append(
            piece[:, : group * head_dim].astype(jnp.float32).reshape(local_leaves, group, head_dim)
        )
        base = group * head_dim
        weights.append(join([piece[:, base + k * group : base + (k + 1) * group] for k in range(2)]))
        base = base + 2 * group
        peaks.append(join([piece[:, base + k * group : base + (k + 1) * group] for k in range(3)]))
    sums.append(leaf_sum)
    weights.append(leaf_weight)
    peaks.append(leaf_peak)
    peak = jnp.maximum(jnp.maximum(peaks[0], peaks[1]), peaks[2])
    numerator = jnp.zeros_like(leaf_sum)
    denominator = jnp.zeros_like(leaf_weight)
    for summed, weight_sum, part_peak in zip(sums, weights, peaks):
        scaled = jnp.exp(part_peak - peak)
        numerator = numerator + scaled[..., None] * summed
        denominator = denominator + scaled * weight_sum
    attended = (
        (numerator / denominator[..., None])
        .astype(jnp.bfloat16)
        .reshape(local_leaves, group * head_dim)
    )
    term = jnp.dot(attended, w_output, preferred_element_type=jnp.float32)
    mixed = lax.psum_scatter(term, "tensor", scatter_dimension=1, tiled=True).astype(jnp.bfloat16)
    return (mixed, new_entry[:, None, :])


def solution(mesh):
    in_specs = (
        P("request", None),
        P(),
        P(None, "tensor"),
        P(None, "tensor"),
        P("tensor", None),
        P("request", "tensor", None, None),
        P("request", "tensor", None, None),
        P(),
        P(),
        P(),
        P(),
        P(),
        P(),
        P("request"),
    )
    out_specs = (P("request", "tensor"), P("request", "tensor", None))
    return jax.shard_map(local, mesh=mesh, in_specs=in_specs, out_specs=out_specs, check_vma=False)
```

time: 1280 us -> 573 us (0.45)
  blocking collectives: 971 us -> 0 us
  waiting for transfers between devices: 168 us -> 357 us
  other arithmetic: 18.2 us -> 143 us
  local copies, waits for them, and re-layouts: 85.3 us -> 40.7 us
    unnamed x1 -> x0, blocking collectives: 491 us -> none
    pmax x1 -> x0, blocking collectives: 480 us -> none  [local(): lax.pmax(own_peak.astype(jnp.bfloat16), 'request').astype(own_peak.dtype)]
    reduce_scatter x0 -> x1, waiting for transfers between devices: none -> 242 us  [local(): lax.psum_scatter(packet.reshape(total_leaves * 2, width), 'request', scat...]
    dynamic_update_slice x16 -> x0, local copies, waits for them, and re-layouts: 66.5 us -> none  [local(): lax.map(owner_block, (everyone.reshape(block_count, block_rows, group, he...]
    gather x0 -> x3, other arithmetic: none -> 49.6 us  [the longest x1 40.9 us: local(): leaf_root = branch_root[leaf_branch]]
    all_gather x1, waiting for transfers between devices: 132 us -> 88.7 us  [local(): lax.all_gather(queries.reshape(local_leaves, group * head_dim), 'request'...]
    add x2, other arithmetic: 0.08 us -> 40.7 us  [the longest x1 40.6 us: local(): prefix_all = root_len[leaf_root] + branch_len[leaf_branch]]
    or x1, other arithmetic: 0.57 us -> 40.6 us  [local(): mine_all = root_mine | branch_mine]
  transfers between devices with their start and end apart: 3 -> 3, of which waited for: 2 -> 3; matrix products, arithmetic and copies ran while one was open for 0% -> 8% of each run, Pallas kernels for 0% -> 0%
where the time goes in v1:
time: 573 us; the launch traced here: 570 us
  waiting for transfers between devices  357 us (62%)
  other arithmetic  143 us (25%)
  local copies, waits for them, and re-layouts  40.7 us (7%)
  between operations  15.4 us (3%)
  matrix products  13.6 us (2%)
    reduce_scatter x1, waiting for transfers between devices, local(): lax.psum_scatter(packet.reshape(total_leaves * 2, width), 'request', scat...  242 us
    all_gather x1, waiting for transfers between devices, local(): lax.all_gather(queries.reshape(local_leaves, group * head_dim), 'request'...  88.7 us
    gather x1, other arithmetic, local(): leaf_root = branch_root[leaf_branch]  40.9 us
    add x1, other arithmetic, local(): prefix_all = root_len[leaf_root] + branch_len[leaf_branch]  40.6 us
    or x1, other arithmetic, local(): mine_all = root_mine | branch_mine  40.6 us
    reduce_scatter x1, waiting for transfers between devices, local(): lax.psum_scatter(term, 'tensor', scatter_dimension=1, tiled=True)  26.1 us
  transfers between devices with their start and end apart: 3, of which 3 were waited for; matrix products, arithmetic and copies ran while one was open for 8% of the time, Pallas kernels for 0%

profile of v1, /device:TPU:24, one launch (start us, length us, event | category | flops | bytes accessed | tf_op | source)
XLA Modules:
  0.0 570.0 jit_solution(10782272740981139692)
XLA Ops:
  7.2 2.1 fusion.43
  9.3 2.1 fusion.44
  11.4 2.1 fusion.45
  13.5 1.6 fusion.46
  15.1 2.1 fusion.39
  17.1 2.1 fusion.40
  19.2 2.1 fusion.41
  21.3 1.6 fusion.42
  22.9 1.6 fusion.38
  24.6 1.6 fusion.33
  26.2 40.9 %select_select_fusion = (s32[1024]{0:T(1024)S(1)}, pred[1024]{0:T(1024)(128)(4,1)S(1)}, pred[1024]{0:T(1024)(128)(4,1)S(1)}, pred[1024]{0:T(1024)(128)(4,1)S(1)}...) fusion(s32[]{:T(128)} %bitcast, s32[]{:T(128)} %bitcast.1, ...), kind=kLoop, calls=%fused_computation.76 | loop fusion | flops 132096 | bytes 72960 | tf_op jit(solution)/shard_map/gather | solution.py:76
  67.1 0.9 fusion.7
  68.0 1.3 fusion.21
  69.3 2.1 fusion.23
  71.3 0.1 reshape.516
  71.4 0.1 slice_negate_fusion
  71.5 8.8 %compare_select_fusion.2 = (s32[1024,1]{0,1:T(1,128)S(1)}, s32[1024,1]{0,1:T(1,128)S(1)}) fusion(s32[]{:T(128)} %bitcast.66, s32[]{:T(128)} %bitcast.67, s32[]{:T(128)} %bitcast.68, s32[]{:T(128)} %bitcast.69, s32[]{:T(128)} %bitcast.70, s32[]{:T(128)} %bitcast.72, s32[]{:T(128)} %bitcast.71, s32[1024,1]{0,1:T(1,128)S(1)} %bitcast.267, s32[]{:T(128)} %bitcast.145, ...), kind=kLoop, calls=%fused_computation.53 | loop fusion | flops 21504 | bytes 12344 | tf_op jit(solution)/shard_map/gather | solution.py:107
  80.3 40.6 %select_add_fusion = s32[1024]{0:T(1024)S(1)} fusion(pred[1024]{0:T(1024)(128)(4,1)S(1)} %get-tuple-element.72, pred[1024]{0:T(1024)(128)(4,1)S(1)} %get-tuple-element.71, pred[1024]{0:T(1024)(128)(4,1)S(1)} %get-tuple-element.70, pred[1024]{0:T(1024)(128)(4,1)S(1)} %get-tuple-element.69, pred[1024]{0:T(1024)(128)(4,1)S(1)} %get-tuple-element.68, ...), kind=kLoop, calls=%fused_computation.73 | loop fusion | flops 66560 | bytes 73988 | tf_op jit(solution)/shard_map/add | solution.py:77
  120.9 0.1 add_convert_fusion.3
  121.0 0.1 slice_negate_fusion.1
  121.1 0.1 fusion.28
  121.2 0.1 maximum_multiply_fusion
  121.3 0.1 mul.147
  121.4 0.1 mul.143
  121.4 0.6 add_convert_fusion.2
  122.1 0.1 copy.51
  122.3 0.6 fusion.29
  122.9 0.7 fusion.30
  125.0 0.7 fusion.37
  125.7 0.7 fusion.35
  126.4 0.7 fusion.36
  127.1 0.7 fusion.34
  127.8 40.6 %fusion.31 = (pred[1024]{0:T(1024)(128)(4,1)S(1)}, pred[1024]{0:T(1024)(128)(4,1)S(1)}, pred[1024]{0:T(1024)(128)(4,1)S(1)}) fusion(s32[]{:T(128)S(6)} %axis_index.12, pred[1024]{0:T(1024)(128)(4,1)S(1)} %get-tuple-element.72, pred[1024]{0:T(1024)(128)(4,1)S(1)} %get-tuple-element.71, pred[1024]{0:T(1024)(128)(4,1)S(1)} %get-tuple-element.70, ...), kind=kLoop, calls=%fused_computation.164 | loop fusion | flops 68608 | bytes 72968 | tf_op jit(solution)/shard_map/or | solution.py:109
  168.5 0.3 broadcast_and_fusion
  168.8 88.7 %all-gather.2.cloned.1.call-done = bf16[1024,512]{1,0:T(8,128)(2,1)} async-done(((bf16[8,512]{1,0:T(8,128)(2,1)}), bf16[1024,512]{1,0:T(8,128)(2,1)}) %all-gather.2.cloned.1.call-update) | async-done | bytes 1048592 | tf_op jit(solution)/shard_map/all_gather | solution.py:83
  257.5 2.3 copy.50
  259.8 4.1 fusion
  263.9 4.1 convert_reduce_fusion
  268.0 4.7 convolution_convert_fusion
  272.6 0.1 bitcast_dynamic-update-slice_fusion
  272.8 0.2 broadcast_select_fusion.1
  273.0 1.6 pad_maximum_fusion
  274.6 7.5 %copy.53 = bf16[1024,2,552]{2,1,0:T(2,128)(2,1)} copy(bf16[1024,2,552]{0,2,1:T(8,128)(2,1)} %pad_maximum_fusion) | data formatting | bytes 4521984 | tf_op jit(solution)/shard_map/stack | solution.py:132
  282.0 6.7 %reshape.518 = bf16[2048,552]{1,0:T(8,128)(2,1)} reshape(bf16[1024,2,552]{2,1,0:T(2,128)(2,1)} %copy.53) | data formatting | bytes 4521984 | tf_op jit(solution)/shard_map/reshape | solution.py:141
  288.7 0.1 slice.361
  288.8 0.8 copy-done.3
  289.6 0.2 copy.54
  289.8 0.1 pad_maximum_fusion.2
  289.9 0.1 iota_compare_fusion.1
  289.9 0.2 bitcast_select_fusion
  290.2 0.2 fusion.47
  290.4 0.2 convert_reduce_fusion.1
  290.6 242.3 %reduce-scatter.3.cloned.1.call-done = bf16[16,552]{1,0:T(8,128)(2,1)} async-done(((bf16[2048,552]{1,0:T(8,128)(2,1)}), bf16[16,552]{1,0:T(8,128)(2,1)}) %reduce-scatter.3.cloned.1.call-update) | async-done | bytes 17680 | tf_op jit(solution)/shard_map/reduce_scatter | solution.py:140
  532.9 0.7 reshape.519
  533.7 0.1 multiply_add_fusion
  533.8 0.1 reshape.526
  533.9 0.1 reshape.528
  533.9 0.2 fusion.4
  534.2 0.1 reshape.524
  534.3 1.0 fusion.48
  535.3 0.1 slice_bitcast_fusion.4
  535.4 0.7 pad_maximum_fusion.3
  536.0 26.1 %reduce-scatter.5.cloned.1.call-done = f32[8,512]{1,0:T(8,128)} async-done(((f32[8,2048]{1,0:T(8,128)}), f32[8,512]{1,0:T(8,128)}) %reduce-scatter.5.cloned.1.call-update) | async-done | bytes 16400 | tf_op jit(solution)/shard_map/reduce_scatter | solution.py:171
  562.1 1.3 convert_element_type.259
  (36 shorter events, 0.4 us)
Async XLA Ops:
  7.2 527.1 %copy-start = (bf16[512,2048]{1,0:T(8,128)(2,1)S(1)}, bf16[512,2048]{1,0:T(8,128)(2,1)}, u32[]{:S(2)}) copy-start(bf16[512,2048]{1,0:T(8,128)(2,1)} %param.18) | copy-start | bytes 6291460
  7.2 113.7 %copy-start.7 = (s32[8]{0:T(128)S(1)}, s32[8]{0:T(128)}, u32[]{:S(2)}) copy-start(s32[8]{0:T(128)} %param.27) | copy-start | bytes 100
  7.2 114.9 %copy-start.4 = (bf16[1,1,512,128]{3,2,1,0:T(8,128)(2,1)S(1)}, bf16[1,1,512,128]{3,2,1,0:T(8,128)(2,1)}, u32[]{:S(2)}) copy-start(bf16[1,1,512,128]{3,2,1,0:T(8,128)(2,1)} %param.19) | copy-start | bytes 393220
  7.2 250.3 %all-gather.2.cloned.1.call-start = ((), (), s32[]{:S(2)}) async-start(), calls=%async_computation.2 | async-start | bytes 1056768 | tf_op jit(solution)/shard_map/all_gather | solution.py:83
  22.9 99.4 %copy-start.5 = (s32[8]{0:T(128)S(1)}, s32[8]{0:T(128)}, u32[]{:S(2)}) copy-start(s32[8]{0:T(128)} %param.23) | copy-start | bytes 100
  22.9 99.4 %copy-start.6 = (s32[8]{0:T(128)S(1)}, s32[8]{0:T(128)}, u32[]{:S(2)}) copy-start(s32[8]{0:T(128)} %param.25) | copy-start | bytes 100
  22.9 100.0 %copy-start.1 = (s32[64]{0:T(128)S(1)}, s32[64]{0:T(128)}, u32[]{:S(2)}) copy-start(s32[64]{0:T(128)} %param.26) | copy-start | bytes 772
  22.9 100.0 %copy-start.2 = (s32[64]{0:T(128)S(1)}, s32[64]{0:T(128)}, u32[]{:S(2)}) copy-start(s32[64]{0:T(128)} %param.24) | copy-start | bytes 772
  122.1 410.8 %reduce-scatter.3.cloned.1.call-start = ((), (), s32[]{:S(2)}) async-start(), calls=%async_computation.3 | async-start | bytes 2641920 | tf_op jit(solution)/shard_map/reduce_scatter | solution.py:140
  288.7 0.9 copy-start.3
  288.7 273.4 %reduce-scatter.5.cloned.1.call-start = ((), (), s32[]{:S(2)}) async-start(), calls=%async_computation.4 | async-start | bytes 81920 | tf_op jit(solution)/shard_map/reduce_scatter | solution.py:171
Sparse Core Ops, SparseCore 0:
  122.2 135.2 all-gather.1
  288.8 243.9 reduce-scatter.2
  535.7 26.4 reduce-scatter.4

commit v2 on v1

--- a/solution.py
+++ b/solution.py
@@ -1,7 +1,7 @@
 import jax
 import jax.numpy as jnp
 from jax import lax
-from jax.sharding import PartitionSpec as P
+from jax.sharding import Mesh, PartitionSpec as P
 
 FLOOR = -1e30
 
@@ -67,21 +67,37 @@
     local_leaves = hidden.shape[0]
     group = w_query.shape[1] // head_dim
     factor = head_dim ** (-0.5)
-    device = lax.axis_index("request")
+    device = (
+        lax.axis_index("z") * (lax.axis_size("y") * lax.axis_size("core"))
+        + lax.axis_index("y") * lax.axis_size("core")
+        + lax.axis_index("core")
+    )
     offset = device * local_leaves
     widened = hidden.astype(jnp.float32)
     normed = (
         widened * lax.rsqrt(jnp.mean(widened * widened, -1, keepdims=True) + 1e-05) * norm_gain
     ).astype(jnp.bfloat16)
-    leaf_root = branch_root[leaf_branch]
-    prefix_all = root_len[leaf_root] + branch_len[leaf_branch]
-    positions = lax.dynamic_slice_in_dim(prefix_all, offset, local_leaves) + leaf_len
+    branch_ids = jnp.arange(branch_root.shape[0], dtype=jnp.int32)
+    root_ids = jnp.arange(root_owner.shape[0], dtype=jnp.int32)
+    own_branch = lax.dynamic_slice_in_dim(leaf_branch, offset, local_leaves)
+    own_hits = own_branch[:, None] == branch_ids[None, :]
+    own_root = jnp.sum(jnp.where(own_hits, branch_root[None, :], 0), 1)
+    positions = (
+        jnp.sum(jnp.where(own_root[:, None] == root_ids[None, :], root_len[None, :], 0), 1)
+        + jnp.sum(jnp.where(own_hits, branch_len[None, :], 0), 1)
+        + leaf_len
+    )
     raw_query = jnp.dot(normed, w_query, preferred_element_type=jnp.float32).reshape(
         local_leaves, group, head_dim
     )
     queries = rotate(raw_query, positions[:, None]).astype(jnp.bfloat16)
     everyone = lax.all_gather(
-        queries.reshape(local_leaves, group * head_dim), "request", axis=0, tiled=True
+        lax.all_gather(
+            queries.reshape(local_leaves, group * head_dim), "z", axis=0, tiled=True
+        ),
+        ("y", "core"),
+        axis=0,
+        tiled=True,
     )
     raw_entry = jnp.dot(normed, w_keyval, preferred_element_type=jnp.float32)
     new_entry = jnp.concatenate(
@@ -104,8 +120,17 @@
     )
 
     total_leaves = everyone.shape[0]
-    root_mine = root_owner[leaf_root] == device
-    branch_mine = branch_owner[leaf_branch] == device
+    z_size = lax.axis_size("z")
+    row_branch = (
+        leaf_branch.reshape(z_size, total_leaves // (z_size * local_leaves), local_leaves)
+        .transpose(1, 0, 2)
+        .reshape(total_leaves)
+    )
+    branch_root_hits = branch_root[:, None] == root_ids[None, :]
+    root_mine_by_branch = jnp.any(branch_root_hits & (root_owner == device)[None, :], 1)
+    row_hits = row_branch[:, None] == branch_ids[None, :]
+    root_mine = jnp.any(row_hits & root_mine_by_branch[None, :], 1)
+    branch_mine = jnp.any(row_hits & (branch_owner == device)[None, :], 1)
     mine_all = root_mine | branch_mine
     my_length = jnp.sum(jnp.where(root_owner == device, root_len, 0)) + jnp.sum(
         jnp.where(branch_owner == device, branch_len, 0)
@@ -138,7 +163,12 @@
     )
     width = packet.shape[-1]
     gathered = lax.psum_scatter(
-        packet.reshape(total_leaves * 2, width), "request", scatter_dimension=0, tiled=True
+        lax.psum_scatter(
+            packet.reshape(total_leaves * 2, width), ("y", "core"), scatter_dimension=0, tiled=True
+        ),
+        "z",
+        scatter_dimension=0,
+        tiled=True,
     ).reshape(local_leaves, 2, width)
     sums = []
     weights = []
@@ -173,21 +203,31 @@
 
 
 def solution(mesh):
+    tensor_size = mesh.shape["tensor"]
+    request_size = mesh.shape["request"]
+    core_size = 2
+    y_size = 4
+    z_size = request_size // (y_size * core_size)
+    fine = Mesh(
+        mesh.devices.reshape(tensor_size, z_size, y_size, core_size),
+        ("tensor", "z", "y", "core"),
+    )
+    request = ("z", "y", "core")
     in_specs = (
-        P("request", None),
+        P(request, None),
         P(),
         P(None, "tensor"),
         P(None, "tensor"),
         P("tensor", None),
-        P("request", "tensor", None, None),
-        P("request", "tensor", None, None),
-        P(),
-        P(),
-        P(),
-        P(),
-        P(),
-        P(),
-        P("request"),
-    )
-    out_specs = (P("request", "tensor"), P("request", "tensor", None))
-    return jax.shard_map(local, mesh=mesh, in_specs=in_specs, out_specs=out_specs, check_vma=False)
+        P(request, "tensor", None, None),
+        P(request, "tensor", None, None),
+        P(),
+        P(),
+        P(),
+        P(),
+        P(),
+        P(),
+        P(request),
+    )
+    out_specs = (P(request, "tensor"), P(request, "tensor", None))
+    return jax.shard_map(local, mesh=fine, in_specs=in_specs, out_specs=out_specs, check_vma=False)

time: 573 us -> 261 us (0.46)
  waiting for transfers between devices: 357 us -> 161 us
  other arithmetic: 143 us -> 12 us
  blocking collectives: 0 us -> 38.4 us
  local copies, waits for them, and re-layouts: 40.7 us -> 19.3 us
    reduce_scatter x1 -> x2, waiting for transfers between devices: 242 us -> 114 us  [the longest x1 74.3 us: local(): lax.psum_scatter(lax.psum_scatter(packet.reshape(total_leaves * 2, width)...]
    all_gather x1, waiting for transfers between devices: 88.7 us -> 21.9 us  [local(): lax.all_gather(lax.all_gather(queries.reshape(local_leaves, group * head_...]
    gather x3 -> x0, other arithmetic: 49.6 us -> none  [the longest x1 40.9 us: local(): leaf_root = branch_root[leaf_branch]]
    add x1 -> x0, other arithmetic: 40.6 us -> none  [local(): prefix_all = root_len[leaf_root] + branch_len[leaf_branch]]
    or x1, other arithmetic: 40.6 us -> 0.01 us  [local(): mine_all = root_mine | branch_mine]
    all_gather x0 -> x1, blocking collectives: none -> 38.4 us  [local(): lax.all_gather(queries.reshape(local_leaves, group * head_dim), 'z', axis...]
    gather x14 -> x0, local copies, waits for them, and re-layouts: 21.7 us -> none  [the longest x5 9.44 us: local(): prefix_all = root_len[leaf_root] + branch_len[leaf_branch]]
  transfers between devices with their start and end apart: 3 -> 4, of which waited for: 3 -> 4; matrix products, arithmetic and copies ran while one was open for 8% -> 1% of each run, Pallas kernels for 0% -> 0%
where the time goes in v2:
time: 261 us; the launch traced here: 260 us
  waiting for transfers between devices  161 us (62%)
  blocking collectives  38.4 us (15%)
  local copies, waits for them, and re-layouts  19.3 us (7%)
  between operations  15.4 us (6%)
  matrix products  13.6 us (5%)
  other arithmetic  12 us (5%)
    reduce_scatter x1, waiting for transfers between devices, local(): lax.psum_scatter(lax.psum_scatter(packet.reshape(total_leaves * 2, width)...  74.3 us
    reduce_scatter x1, waiting for transfers between devices, local(): lax.psum_scatter(packet.reshape(total_leaves * 2, width), ('y', 'core'),...  39.7 us
    all_gather x1, blocking collectives, local(): lax.all_gather(queries.reshape(local_leaves, group * head_dim), 'z', axis...  38.4 us
    reduce_scatter x1, waiting for transfers between devices, local(): lax.psum_scatter(term, 'tensor', scatter_dimension=1, tiled=True)  25.3 us
    all_gather x1, waiting for transfers between devices, local(): lax.all_gather(lax.all_gather(queries.reshape(local_leaves, group * head_...  21.9 us
    another operation x1, local copies, waits for them, and re-layouts, local(): jnp.stack([jnp.where(root_mine[:, None], packet, zeros), jnp.where(branch...  7.46 us
    reshape x1, local copies, waits for them, and re-layouts, local(): packet.reshape(total_leaves * 2, width)  6.68 us
  transfers between devices with their start and end apart: 4, of which 4 were waited for; matrix products, arithmetic and copies ran while one was open for 1% of the time, Pallas kernels for 0%

profile of v2, /device:TPU:24, one launch (start us, length us, event | category | flops | bytes accessed | tf_op | source)
XLA Modules:
  0.0 260.2 jit_solution(3833507069731562670)
XLA Ops:
  7.2 0.0 copy-start
  7.3 0.0 all-gather.2.cloned.1.call-start
  7.3 1.0 fusion.11
  8.4 1.3 fusion.25
  9.7 2.1 fusion.27
  11.8 0.1 reshape.509
  11.8 0.1 slice_negate_fusion
  11.9 0.1 dynamic_slice.3
  12.0 0.0 copy-done.4
  12.0 0.2 select_reduce_fusion
  12.2 0.2 select_reduce_fusion.1
  12.4 0.1 slice_negate_fusion.1
  12.5 0.1 fusion.34
  12.6 0.1 maximum_multiply_fusion
  12.7 0.1 mul.155
  12.7 0.1 mul.151
  12.8 38.4 %all_gather.6 = bf16[128,512]{1,0:T(8,128)(2,1)} all-gather(bf16[8,512]{1,0:T(8,128)(2,1)S(1)} %add_convert_fusion.2), channel_id=1, replica_groups=mesh['tensor'=4,'z'=16,'y'=4,'core'=2] {'z'}, dimensions={0}, use_global_device_ids=true | all-gather | bytes 139264 | tf_op jit(solution)/shard_map/all_gather | solution.py:95
  51.2 0.0 all-gather.2.cloned.1.call-update
  51.3 0.0 reduce-scatter.4.cloned.1.call-start
  51.3 0.1 reshape.508
  51.4 0.1 eq.40
  51.5 0.1 copy.61
  51.6 0.0 copy-done.7
  51.7 0.6 select_reduce_fusion.4
  52.3 0.1 fusion.32
  52.4 0.6 select_reduce_fusion.3
  53.0 0.1 fusion.8
  54.5 0.3 broadcast_and_fusion
  54.8 21.9 %all-gather.2.cloned.1.call-done = bf16[1024,512]{1,0:T(8,128)(2,1)} async-done(((bf16[128,512]{1,0:T(8,128)(2,1)}), bf16[1024,512]{1,0:T(8,128)(2,1)}) %all-gather.2.cloned.1.call-update) | async-done | bytes 1048592 | tf_op jit(solution)/shard_map/all_gather | solution.py:94
  76.7 2.3 copy.60
  79.0 4.1 %fusion = (f32[1024,8]{0,1:T(8,128)S(1)}, f32[1024,8,512]{0,2,1:T(8,128)S(1)}) fusion(pred[1024,512]{0,1:T(8,128)(4,1)S(1)} %broadcast_and_fusion, bf16[1024,8,64]{0,2,1:T(8,128)(2,1)} %bitcast.48, bf16[512,128]{0,1:T(8,128)(2,1)S(1)} %bitcast.50), kind=kOutput, calls=%fused_computation.3 | convolution fusion | flops 549445632 | bytes 18448384 | tf_op jit(solution)/shard_map/ngd,kd->ngk/dot_general | solution.py:142
  83.1 4.1 %convert_reduce_fusion = f32[1024,8]{0,1:T(8,128)S(1)} fusion(f32[1024,8]{0,1:T(8,128)S(1)} %get-tuple-element.27, f32[1024,8,512]{0,2,1:T(8,128)S(1)} %get-tuple-element.28, pred[1024,512]{0,1:T(8,128)(4,1)S(1)} %broadcast_and_fusion), kind=kLoop, calls=%fused_computation | loop fusion | flops 29351936 | bytes 17367040 | tf_op jit(solution)/shard_map/reduce_sum | solution.py:25
  87.1 4.7 %convolution_convert_fusion = bf16[1024,8,64]{0,2,1:T(8,128)(2,1)S(1)} fusion(bf16[512,128]{0,1:T(8,128)(2,1)S(1)} %bitcast.51, f32[1024,8,512]{0,2,1:T(8,128)S(1)} %get-tuple-element.28, f32[1024,8]{0,1:T(8,128)S(1)} %get-tuple-element.27, pred[1024,512]{0,1:T(8,128)(4,1)S(1)} %broadcast_and_fusion), kind=kOutput, calls=%fused_computation.5 | convolution fusion | flops 558366720 | bytes 18448384 | tf_op jit(solution)/shard_map/ngk,kd->ngd/dot_general | solution.py:24
  91.8 0.1 bitcast_dynamic-update-slice_fusion
  92.0 0.2 broadcast_select_fusion.1
  92.1 1.6 pad_maximum_fusion
  93.7 7.5 %copy.63 = bf16[1024,2,552]{2,1,0:T(2,128)(2,1)} copy(bf16[1024,2,552]{0,2,1:T(8,128)(2,1)} %pad_maximum_fusion) | data formatting | bytes 4521984 | tf_op jit(solution)/shard_map/stack | solution.py:157
  101.2 6.7 %reshape.511 = bf16[2048,552]{1,0:T(8,128)(2,1)} reshape(bf16[1024,2,552]{2,1,0:T(2,128)(2,1)} %copy.63) | data formatting | bytes 4521984 | tf_op jit(solution)/shard_map/reshape | solution.py:167
  107.9 0.0 reduce-scatter.4.cloned.1.call-update
  107.9 0.0 reduce-scatter.6.cloned.1.call-start
  107.9 0.1 slice.148
  108.0 0.8 copy-done.1
  108.8 0.2 copy.64
  109.0 0.1 pad_maximum_fusion.2
  109.1 0.1 iota_compare_fusion.2
  109.1 39.7 %reduce-scatter.4.cloned.1.call-done = bf16[256,552]{1,0:T(8,128)(2,1)} async-done(((bf16[2048,552]{1,0:T(8,128)(2,1)}), bf16[256,552]{1,0:T(8,128)(2,1)}) %reduce-scatter.4.cloned.1.call-update) | async-done | bytes 282640 | tf_op jit(solution)/shard_map/reduce_scatter | solution.py:166
  148.8 0.0 reduce-scatter.6.cloned.1.call-update
  148.8 0.0 reduce-scatter.8.cloned.1.call-start
  148.9 0.2 bitcast_select_fusion
  149.1 0.2 fusion.36
  149.3 0.2 convert_reduce_fusion.1
  149.5 74.3 %reduce-scatter.6.cloned.1.call-done = bf16[16,552]{1,0:T(8,128)(2,1)} async-done(((bf16[256,552]{1,0:T(8,128)(2,1)}), bf16[16,552]{1,0:T(8,128)(2,1)}) %reduce-scatter.6.cloned.1.call-update) | async-done | bytes 17680 | tf_op jit(solution)/shard_map/reduce_scatter | solution.py:165
  223.8 0.7 reshape.512
  224.6 0.1 multiply_add_fusion
  224.7 0.1 reshape.519
  224.8 0.1 reshape.521
  224.9 0.2 fusion.4
  225.1 0.1 reshape.517
  225.2 1.0 fusion.37
  226.2 0.0 reduce-scatter.8.cloned.1.call-update
  226.2 0.1 slice_bitcast_fusion.4
  226.3 0.7 pad_maximum_fusion.3
  227.0 25.3 %reduce-scatter.8.cloned.1.call-done = f32[8,512]{1,0:T(8,128)} async-done(((f32[8,2048]{1,0:T(8,128)}), f32[8,512]{1,0:T(8,128)}) %reduce-scatter.8.cloned.1.call-update) | async-done | bytes 16400 | tf_op jit(solution)/shard_map/reduce_scatter | solution.py:201
  252.3 1.3 convert_element_type.259
  (34 shorter events, 0.2 us)
Async XLA Ops:
  7.2 218.0 %copy-start = (bf16[512,2048]{1,0:T(8,128)(2,1)S(1)}, bf16[512,2048]{1,0:T(8,128)(2,1)}, u32[]{:S(2)}) copy-start(bf16[512,2048]{1,0:T(8,128)(2,1)} %param.18) | copy-start | bytes 6291460
  7.2 4.7 %copy-start.3 = (s32[1024]{0:T(1024)S(1)}, s32[1024]{0:T(1024)}, u32[]{:S(2)}) copy-start(s32[1024]{0:T(1024)} %param.21) | copy-start | bytes 12292
  7.2 4.8 %copy-start.8 = (s32[64]{0:T(128)S(1)}, s32[64]{0:T(128)}, u32[]{:S(2)}) copy-start(s32[64]{0:T(128)} %param.22) | copy-start | bytes 772
  7.2 4.8 %copy-start.4 = (s32[64]{0:T(128)S(1)}, s32[64]{0:T(128)}, u32[]{:S(2)}) copy-start(s32[64]{0:T(128)} %param.26) | copy-start | bytes 772
  7.2 5.0 %copy-start.6 = (s32[8]{0:T(128)S(1)}, s32[8]{0:T(128)}, u32[]{:S(2)}) copy-start(s32[8]{0:T(128)} %param.25) | copy-start | bytes 100
  7.2 5.1 %copy-start.5 = (s32[8]{0:T(128)S(1)}, s32[8]{0:T(128)}, u32[]{:S(2)}) copy-start(s32[8]{0:T(128)} %param.27) | copy-start | bytes 100
  7.2 44.3 %copy-start.2 = (bf16[1,1,512,128]{3,2,1,0:T(8,128)(2,1)S(1)}, bf16[1,1,512,128]{3,2,1,0:T(8,128)(2,1)}, u32[]{:S(2)}) copy-start(bf16[1,1,512,128]{3,2,1,0:T(8,128)(2,1)} %param.19) | copy-start | bytes 393220
  7.2 44.4 %copy-start.7 = (s32[8]{0:T(128)S(1)}, s32[8]{0:T(128)}, u32[]{:S(2)}) copy-start(s32[8]{0:T(128)} %param.23) | copy-start | bytes 100
  7.3 45.1 %copy-start.9 = (s32[64]{0:T(128)S(1)}, s32[64]{0:T(128)}, u32[]{:S(2)}) copy-start(s32[64]{0:T(128)} %param.24) | copy-start | bytes 772
  7.3 69.4 %all-gather.2.cloned.1.call-start = ((), (), s32[]{:S(2)}) async-start(), calls=%async_computation.3 | async-start | bytes 1179648 | tf_op jit(solution)/shard_map/all_gather | solution.py:94
  51.3 97.5 %reduce-scatter.4.cloned.1.call-start = ((), (), s32[]{:S(2)}) async-start(), calls=%async_computation.4 | async-start | bytes 2949120 | tf_op jit(solution)/shard_map/reduce_scatter | solution.py:166
  107.8 0.9 copy-start.1
  107.9 115.9 %reduce-scatter.6.cloned.1.call-start = ((), (), s32[]{:S(2)}) async-start(), calls=%async_computation.5 | async-start | bytes 348160 | tf_op jit(solution)/shard_map/reduce_scatter | solution.py:165
  148.8 103.5 %reduce-scatter.8.cloned.1.call-start = ((), (), s32[]{:S(2)}) async-start(), calls=%async_computation.6 | async-start | bytes 81920 | tf_op jit(solution)/shard_map/reduce_scatter | solution.py:201
Sparse Core Ops, SparseCore 0:
  51.4 25.2 all-gather.1
  108.0 40.7 reduce-scatter.3
  151.6 72.1 reduce-scatter.5
  226.4 25.8 reduce-scatter.7

commit v3 on v2

--- a/solution.py
+++ b/solution.py
@@ -45,6 +45,27 @@
     for piece in pieces[1:]:
         total = total + piece.astype(jnp.float32)
     return total
+
+
+def group_size(axes):
+    size = 1
+    for axis in axes if isinstance(axes, tuple) else (axes,):
+        size = size * lax.axis_size(axis)
+    return size
+
+
+def gather_rows(values, axes):
+    count = group_size(axes)
+    spread = jnp.broadcast_to(values[None], (count,) + values.shape)
+    received = lax.all_to_all(spread, axes, 0, 0, tiled=False)
+    return received.reshape(count * values.shape[0], values.shape[1])
+
+
+def scatter_rows(values, axes):
+    count = group_size(axes)
+    blocks = values.reshape(count, values.shape[0] // count, values.shape[1])
+    received = lax.all_to_all(blocks, axes, 0, 0, tiled=False)
+    return jnp.sum(received.astype(jnp.float32), 0).astype(values.dtype)
 
 
 def local(
@@ -91,13 +112,8 @@
         local_leaves, group, head_dim
     )
     queries = rotate(raw_query, positions[:, None]).astype(jnp.bfloat16)
-    everyone = lax.all_gather(
-        lax.all_gather(
-            queries.reshape(local_leaves, group * head_dim), "z", axis=0, tiled=True
-        ),
-        ("y", "core"),
-        axis=0,
-        tiled=True,
+    everyone = gather_rows(
+        gather_rows(queries.reshape(local_leaves, group * head_dim), "z"), ("y", "core")
     )
     raw_entry = jnp.dot(normed, w_keyval, preferred_element_type=jnp.float32)
     new_entry = jnp.concatenate(
@@ -162,13 +178,8 @@
         1,
     )
     width = packet.shape[-1]
-    gathered = lax.psum_scatter(
-        lax.psum_scatter(
-            packet.reshape(total_leaves * 2, width), ("y", "core"), scatter_dimension=0, tiled=True
-        ),
-        "z",
-        scatter_dimension=0,
-        tiled=True,
+    gathered = scatter_rows(
+        scatter_rows(packet.reshape(total_leaves * 2, width), ("y", "core")), "z"
     ).reshape(local_leaves, 2, width)
     sums = []
     weights = []
@@ -198,7 +209,15 @@
         .reshape(local_leaves, group * head_dim)
     )
     term = jnp.dot(attended, w_output, preferred_element_type=jnp.float32)
-    mixed = lax.psum_scatter(term, "tensor", scatter_dimension=1, tiled=True).astype(jnp.bfloat16)
+    tensor_size = lax.axis_size("tensor")
+    pieces = lax.all_to_all(
+        term.reshape(local_leaves, tensor_size, term.shape[1] // tensor_size),
+        "tensor",
+        1,
+        1,
+        tiled=False,
+    )
+    mixed = jnp.sum(pieces, 1).astype(jnp.bfloat16)
     return (mixed, new_entry[:, None, :])
 
 

time: 261 us -> 170 us (0.65)
  waiting for transfers between devices: 161 us -> 57.9 us
  starting transfers between devices: 0.16 us -> 19.1 us
  between operations: 15.4 us -> 2.26 us
  local copies, waits for them, and re-layouts: 19.3 us -> 31.2 us
  blocking collectives: 38.4 us -> 29.8 us
    reduce_scatter x3 -> x0, waiting for transfers between devices: 139 us -> none  [the longest x1 74.3 us: local(): lax.psum_scatter(lax.psum_scatter(packet.reshape(total_leaves * 2, width)...]
    all_to_all x0 -> x4, waiting for transfers between devices: none -> 57.9 us  [the longest x2 42.4 us: scatter_rows(): received = lax.all_to_all(blocks, axes, 0, 0, tiled=False)]
    all_gather x1 -> x0, blocking collectives: 38.4 us -> none  [local(): lax.all_gather(queries.reshape(local_leaves, group * head_dim), 'z', axis...]
    all_to_all x0 -> x1, blocking collectives: none -> 29.8 us  [gather_rows(): received = lax.all_to_all(spread, axes, 0, 0, tiled=False)]
    all_gather x1 -> x0, waiting for transfers between devices: 21.9 us -> none  [local(): lax.all_gather(lax.all_gather(queries.reshape(local_leaves, group * head_...]
    all_to_all x0 -> x4, starting transfers between devices: none -> 19.1 us  [the longest x2 10.1 us: scatter_rows(): received = lax.all_to_all(blocks, axes, 0, 0, tiled=False)]
    another operation x0 -> x3, local copies, waits for them, and re-layouts: none -> 13.3 us  [the longest x2 11 us: scatter_rows(): blocks = values.reshape(count, values.shape[0] // count, values.shape[1])]
    reshape x2 -> x1, local copies, waits for them, and re-layouts: 7.43 us -> 0.02 us  [local(): gathered = scatter_rows(scatter_rows(packet.reshape(total_leaves * 2, wid...]
  transfers between devices with their start and end apart: 4 -> 4, of which waited for: 4 -> 4; matrix products, arithmetic and copies ran while one was open for 1% -> 5% of each run, Pallas kernels for 0% -> 0%
where the time goes in v3:
time: 170 us; the launch traced here: 168 us
  waiting for transfers between devices  57.9 us (34%)
  local copies, waits for them, and re-layouts  31.2 us (18%)
  blocking collectives  29.8 us (18%)
  starting transfers between devices  19.1 us (11%)
  matrix products  14.6 us (9%)
  other arithmetic  13.4 us (8%)
  between operations  2.26 us (1%)
    all_to_all x2, waiting for transfers between devices, scatter_rows(): received = lax.all_to_all(blocks, axes, 0, 0, tiled=False)  42.4 us
    all_to_all x1, blocking collectives, gather_rows(): received = lax.all_to_all(spread, axes, 0, 0, tiled=False)  29.8 us
    another operation x2, local copies, waits for them, and re-layouts, scatter_rows(): blocks = values.reshape(count, values.shape[0] // count, values.shape[1])  11 us
    all_to_all x1, waiting for transfers between devices, gather_rows(): received = lax.all_to_all(spread, axes, 0, 0, tiled=False)  10.5 us
    all_to_all x2, starting transfers between devices, scatter_rows(): received = lax.all_to_all(blocks, axes, 0, 0, tiled=False)  10.1 us
    another operation x1, local copies, waits for them, and re-layouts, local(): jnp.stack([jnp.where(root_mine[:, None], packet, zeros), jnp.where(branch...  7.46 us
    all_to_all x1, waiting for transfers between devices, local(): lax.all_to_all(term.reshape(local_leaves, tensor_size, term.shape[1] // t...  4.97 us
    dot_general x2, matrix products, soft_part(): jnp.einsum(pattern, weights, value_rows, preferred_element_type=jnp.float32)  4.9 us
  transfers between devices with their start and end apart: 4, of which 4 were waited for; matrix products, arithmetic and copies ran while one was open for 5% of the time, Pallas kernels for 0%

profile of v3, /device:TPU:24, one launch (start us, length us, event | category | flops | bytes accessed | tf_op | source)
XLA Modules:
  0.0 168.2 jit_solution(14212703738745783999)
XLA Ops:
  0.6 0.0 copy-start
  0.7 1.0 fusion.11
  1.8 1.3 fusion.25
  3.1 1.2 fusion.27
  4.3 0.1 reshape.521
  4.3 0.1 slice_negate_fusion
  4.4 0.1 dynamic_slice.3
  4.5 0.2 select_reduce_fusion
  4.7 0.2 select_reduce_fusion.1
  4.9 0.1 slice_negate_fusion.1
  5.0 0.1 fusion.34
  5.1 0.1 maximum_multiply_fusion
  5.2 0.1 mul.157
  5.3 0.1 mul.153
  5.4 29.8 %all_to_all.25 = bf16[16,8,512]{2,1,0:T(8,128)(2,1)S(1)} all-to-all(bf16[16,8,512]{2,1,0:T(8,128)(2,1)S(1)} %broadcast_in_dim.178), channel_id=1, replica_groups=mesh['tensor'=4,'z'=16,'y'=4,'core'=2] {'z'}, dimensions={0} | all-to-all | bytes 262144 | tf_op jit(solution)/shard_map/all_to_all | solution.py:60
  35.1 0.1 copy.86
  35.3 1.2 broadcast_in_dim.180
  36.4 4.7 %all-to-all-start.1 = ((bf16[8,128,512]{1,2,0:T(8,128)(2,1)}), bf16[8,128,512]{1,2,0:T(8,128)(2,1)}, u32[]{:S(2)}, u32[]{:S(2)}) async-start(bf16[8,128,512]{1,2,0:T(8,128)(2,1)} %broadcast_in_dim.180), calls=%async_computation.1 | async-start | bytes 2097152 | tf_op jit(solution)/shard_map/all_to_all | solution.py:60
  41.1 0.6 select_reduce_fusion.4
  41.8 0.1 reshape.520
  41.9 0.1 eq.40
  42.0 0.1 copy.88
  42.1 0.1 fusion.32
  42.2 0.6 select_reduce_fusion.3
  42.8 0.1 fusion.8
  44.3 0.3 broadcast_and_fusion
  44.6 10.5 %all-to-all-done.1 = bf16[8,128,512]{1,2,0:T(8,128)(2,1)} async-done(((bf16[8,128,512]{1,2,0:T(8,128)(2,1)}), bf16[8,128,512]{1,2,0:T(8,128)(2,1)}, u32[]{:S(2)}, u32[]{:S(2)}) %all-to-all-start.1) | async-done | bytes 1048608 | tf_op jit(solution)/shard_map/all_to_all | solution.py:60
  55.1 2.9 %copy.87 = bf16[8,128,512]{1,0,2:T(8,128)(2,1)} copy(bf16[8,128,512]{1,2,0:T(8,128)(2,1)} %all-to-all-done.1) | data formatting | bytes 2097152 | tf_op jit(solution)/shard_map/all_to_all | solution.py:60
  58.0 2.3 %reshape_reshape.6 = bf16[1024,8,64]{0,2,1:T(8,128)(2,1)} reshape(bf16[8,128,512]{1,0,2:T(8,128)(2,1)} %copy.87) | data formatting | bytes 2097152 | tf_op jit(solution)/shard_map/reshape;reshape | solution.py:156
  60.4 4.1 %fusion = (f32[1024,8]{0,1:T(8,128)S(1)}, f32[1024,8,512]{0,2,1:T(8,128)S(1)}) fusion(pred[1024,512]{0,1:T(8,128)(4,1)S(1)} %broadcast_and_fusion, bf16[1024,8,64]{0,2,1:T(8,128)(2,1)} %reshape_reshape.6, bf16[512,128]{0,1:T(8,128)(2,1)S(1)} %bitcast.57), kind=kOutput, calls=%fused_computation.3 | convolution fusion | flops 549445632 | bytes 18448384 | tf_op jit(solution)/shard_map/ngd,kd->ngk/dot_general | solution.py:158
  64.4 4.1 %convert_reduce_fusion = f32[1024,8]{0,1:T(8,128)S(1)} fusion(f32[1024,8]{0,1:T(8,128)S(1)} %get-tuple-element.27, f32[1024,8,512]{0,2,1:T(8,128)S(1)} %get-tuple-element.28, pred[1024,512]{0,1:T(8,128)(4,1)S(1)} %broadcast_and_fusion), kind=kLoop, calls=%fused_computation | loop fusion | flops 29351936 | bytes 17367040 | tf_op jit(solution)/shard_map/reduce_sum | solution.py:25
  68.5 4.7 %convolution_convert_fusion = bf16[1024,8,64]{0,2,1:T(8,128)(2,1)S(1)} fusion(bf16[512,128]{0,1:T(8,128)(2,1)S(1)} %bitcast.58, f32[1024,8,512]{0,2,1:T(8,128)S(1)} %get-tuple-element.28, f32[1024,8]{0,1:T(8,128)S(1)} %get-tuple-element.27, pred[1024,512]{0,1:T(8,128)(4,1)S(1)} %broadcast_and_fusion), kind=kOutput, calls=%fused_computation.5 | convolution fusion | flops 558366720 | bytes 18448384 | tf_op jit(solution)/shard_map/ngk,kd->ngd/dot_general | solution.py:24
  73.2 0.1 bitcast_dynamic-update-slice_fusion
  73.3 0.2 broadcast_select_fusion.1
  73.5 1.6 pad_maximum_fusion
  75.1 7.5 %copy.90 = bf16[1024,2,552]{2,1,0:T(2,128)(2,1)} copy(bf16[1024,2,552]{0,2,1:T(8,128)(2,1)} %pad_maximum_fusion) | data formatting | bytes 4521984 | tf_op jit(solution)/shard_map/stack | solution.py:173
  82.5 6.7 %reshape_reshape.7 = bf16[8,256,552]{2,1,0:T(8,128)(2,1)} reshape(bf16[1024,2,552]{2,1,0:T(2,128)(2,1)} %copy.90) | data formatting | bytes 4521984 | tf_op jit(solution)/shard_map/reshape;reshape | solution.py:66
  89.2 4.3 %copy.91 = bf16[8,256,552]{1,2,0:T(8,128)(2,1)} copy(bf16[8,256,552]{2,1,0:T(8,128)(2,1)} %reshape_reshape.7) | data formatting | bytes 4521984 | tf_op jit(solution)/shard_map/reshape;reshape | solution.py:66
  93.5 6.3 %all-to-all-start.2 = ((bf16[8,256,552]{1,2,0:T(8,128)(2,1)}), bf16[8,256,552]{1,2,0:T(8,128)(2,1)}, u32[]{:S(2)}, u32[]{:S(2)}) async-start(bf16[8,256,552]{1,2,0:T(8,128)(2,1)} %copy.91), calls=%async_computation.2 | async-start | bytes 4521984 | tf_op jit(solution)/shard_map/all_to_all | solution.py:67
  99.9 0.1 slice.148
  99.9 26.9 %all-to-all-done.2 = bf16[8,256,552]{1,2,0:T(8,128)(2,1)} async-done(((bf16[8,256,552]{1,2,0:T(8,128)(2,1)}), bf16[8,256,552]{1,2,0:T(8,128)(2,1)}, u32[]{:S(2)}, u32[]{:S(2)}) %all-to-all-start.2) | async-done | bytes 2261024 | tf_op jit(solution)/shard_map/all_to_all | solution.py:67
  126.8 2.0 %reduce_sum.112 = bf16[256,552]{0,1:T(8,128)(2,1)S(1)} reduce(bf16[8,256,552]{1,2,0:T(8,128)(2,1)} %all-to-all-done.2, bf16[]{:T(256)} %constant.48.clone.1), dimensions={0}, to_apply=%region_11.12 | reduce | flops 989184 | bytes 2543618 | tf_op jit(solution)/shard_map/reduce_sum | solution.py:68
  128.9 0.9 copy.92
  129.8 3.7 %all-to-all-start.3 = ((bf16[16,16,552]{2,1,0:T(8,128)(2,1)}), bf16[16,16,552]{2,1,0:T(8,128)(2,1)S(1)}, u32[]{:S(2)}, u32[]{:S(2)}) async-start(bf16[16,16,552]{2,1,0:T(8,128)(2,1)} %bitcast.11), calls=%async_computation.3 | async-start | bytes 655360 | tf_op jit(solution)/shard_map/all_to_all | solution.py:67
  133.5 0.1 pad_maximum_fusion.2
  133.6 0.2 copy.93
  133.8 3.9 %copy.96 = bf16[2048,512]{1,0:T(8,128)(2,1)} copy(bf16[2048,512]{0,1:T(8,128)(2,1)} %bitcast.54) | data formatting | bytes 4194304 | tf_op jit(solution)/shard_map/dot_general | solution.py:211
  137.8 0.1 iota_compare_fusion.2
  137.8 0.2 bitcast_select_fusion
  138.0 0.2 fusion.36
  138.3 0.2 convert_reduce_fusion.1
  138.4 0.1 slice_bitcast_fusion.4
  138.5 15.6 %all-to-all-done.3 = bf16[16,16,552]{2,1,0:T(8,128)(2,1)S(1)} async-done(((bf16[16,16,552]{2,1,0:T(8,128)(2,1)}), bf16[16,16,552]{2,1,0:T(8,128)(2,1)S(1)}, u32[]{:S(2)}, u32[]{:S(2)}) %all-to-all-start.3) | async-done | bytes 282656 | tf_op jit(solution)/shard_map/all_to_all | solution.py:67
  154.1 0.1 reduce_sum.113
  154.2 0.1 multiply_add_fusion
  154.3 0.1 reshape.530
  154.4 0.1 reshape.532
  154.5 0.2 fusion.4
  154.7 0.1 reshape.535
  154.8 2.9 %fusion.37 = f32[8,4,512]{2,0,1:T(8,128)} fusion(bf16[8,512,1]{1,0,2:T(8,128)(2,1)S(1)} %reshape.535, bf16[4,512,512]{2,1,0:T(8,128)(2,1)} %bitcast.53), kind=kOutput, calls=%fused_computation.98 | convolution fusion | flops 16777216 | bytes 2170880 | tf_op jit(solution)/shard_map/dot_general | solution.py:211
  157.7 4.3 %all-to-all-start.4 = ((f32[8,4,512]{2,0,1:T(8,128)}), f32[8,4,512]{2,0,1:T(8,128)S(1)}, u32[]{:S(2)}, u32[]{:S(2)}) async-start(f32[8,4,512]{2,0,1:T(8,128)} %fusion.37), calls=%async_computation.4 | async-start | bytes 131072 | tf_op jit(solution)/shard_map/all_to_all | solution.py:213
  162.0 0.7 pad_maximum_fusion.3
  162.6 5.0 %all-to-all-done.4 = f32[8,4,512]{2,0,1:T(8,128)S(1)} async-done(((f32[8,4,512]{2,0,1:T(8,128)}), f32[8,4,512]{2,0,1:T(8,128)S(1)}, u32[]{:S(2)}, u32[]{:S(2)}) %all-to-all-start.4) | async-done | bytes 65568 | tf_op jit(solution)/shard_map/all_to_all | solution.py:213
  167.6 0.6 reduce_sum.115
  (39 shorter events, 0.2 us)
Async XLA Ops:
  0.6 2.4 %copy-start = (bf16[2048,512]{1,0:T(8,128)(2,1)S(1)}, bf16[2048,512]{1,0:T(8,128)(2,1)}, u32[]{:S(2)}) copy-start(bf16[2048,512]{1,0:T(8,128)(2,1)} %param.16) | copy-start | bytes 6291460
  0.6 3.8 %copy-start.3 = (s32[1024]{0:T(1024)S(1)}, s32[1024]{0:T(1024)}, u32[]{:S(2)}) copy-start(s32[1024]{0:T(1024)} %param.21) | copy-start | bytes 12292
  0.7 3.8 %copy-start.8 = (s32[64]{0:T(128)S(1)}, s32[64]{0:T(128)}, u32[]{:S(2)}) copy-start(s32[64]{0:T(128)} %param.22) | copy-start | bytes 772
  0.7 3.8 %copy-start.4 = (s32[64]{0:T(128)S(1)}, s32[64]{0:T(128)}, u32[]{:S(2)}) copy-start(s32[64]{0:T(128)} %param.26) | copy-start | bytes 772
  0.7 4.0 %copy-start.6 = (s32[8]{0:T(128)S(1)}, s32[8]{0:T(128)}, u32[]{:S(2)}) copy-start(s32[8]{0:T(128)} %param.25) | copy-start | bytes 100
  0.7 4.2 %copy-start.5 = (s32[8]{0:T(128)S(1)}, s32[8]{0:T(128)}, u32[]{:S(2)}) copy-start(s32[8]{0:T(128)} %param.27) | copy-start | bytes 100
  4.3 36.9 %copy-start.7 = (s32[8]{0:T(128)S(1)}, s32[8]{0:T(128)}, u32[]{:S(2)}) copy-start(s32[8]{0:T(128)} %param.23) | copy-start | bytes 100
  5.1 36.9 %copy-start.2 = (bf16[1,1,512,128]{3,2,1,0:T(8,128)(2,1)S(1)}, bf16[1,1,512,128]{3,2,1,0:T(8,128)(2,1)}, u32[]{:S(2)}) copy-start(bf16[1,1,512,128]{3,2,1,0:T(8,128)(2,1)} %param.19) | copy-start | bytes 393220
  5.3 36.9 %copy-start.9 = (s32[64]{0:T(128)S(1)}, s32[64]{0:T(128)}, u32[]{:S(2)}) copy-start(s32[64]{0:T(128)} %param.24) | copy-start | bytes 772
  36.4 18.7 %all-to-all-start.1 = ((bf16[8,128,512]{1,2,0:T(8,128)(2,1)}), bf16[8,128,512]{1,2,0:T(8,128)(2,1)}, u32[]{:S(2)}, u32[]{:S(2)}) async-start(bf16[8,128,512]{1,2,0:T(8,128)(2,1)} %broadcast_in_dim.180), calls=%async_computation.1 | async-start | bytes 2097152 | tf_op jit(solution)/shard_map/all_to_all | solution.py:60
  93.5 33.3 %all-to-all-start.2 = ((bf16[8,256,552]{1,2,0:T(8,128)(2,1)}), bf16[8,256,552]{1,2,0:T(8,128)(2,1)}, u32[]{:S(2)}, u32[]{:S(2)}) async-start(bf16[8,256,552]{1,2,0:T(8,128)(2,1)} %copy.91), calls=%async_computation.2 | async-start | bytes 4521984 | tf_op jit(solution)/shard_map/all_to_all | solution.py:67
  99.9 33.8 %copy-start.1 = (bf16[8,1,128,128]{3,2,1,0:T(8,128)(2,1)S(1)}, bf16[8,1,128,128]{3,2,1,0:T(8,128)(2,1)}, u32[]{:S(2)}) copy-start(bf16[8,1,128,128]{3,2,1,0:T(8,128)(2,1)} %param.20) | copy-start | bytes 786436
  129.8 24.3 %all-to-all-start.3 = ((bf16[16,16,552]{2,1,0:T(8,128)(2,1)}), bf16[16,16,552]{2,1,0:T(8,128)(2,1)S(1)}, u32[]{:S(2)}, u32[]{:S(2)}) async-start(bf16[16,16,552]{2,1,0:T(8,128)(2,1)} %bitcast.11), calls=%async_computation.3 | async-start | bytes 655360 | tf_op jit(solution)/shard_map/all_to_all | solution.py:67
  157.7 9.9 %all-to-all-start.4 = ((f32[8,4,512]{2,0,1:T(8,128)}), f32[8,4,512]{2,0,1:T(8,128)S(1)}, u32[]{:S(2)}, u32[]{:S(2)}) async-start(f32[8,4,512]{2,0,1:T(8,128)} %fusion.37), calls=%async_computation.4 | async-start | bytes 131072 | tf_op jit(solution)/shard_map/all_to_all | solution.py:213

commit v4 on v3

--- a/solution.py
+++ b/solution.py
@@ -163,36 +163,36 @@
     usable = mine_all[:, None, None] & node_usable[None, None, :]
     own_sum, own_weight, own_peak = soft_part(scores, usable, node_rows[:, head_dim:], "ngk,kd->ngd")
     own_peak = jnp.where(mine_all[:, None], own_peak, 0.0)
+    own_values = own_sum.reshape(total_leaves, group * head_dim).astype(jnp.bfloat16)
+    own_stats = jnp.concatenate(split_two(own_weight) + split_three(own_peak), -1)
+    stat_width = own_stats.shape[1]
+    pad_width = (-(2 * group * head_dim + 2 * stat_width)) % 128
+    zeros_values = jnp.zeros_like(own_values)
+    zeros_stats = jnp.zeros_like(own_stats)
     packet = jnp.concatenate(
-        [own_sum.reshape(total_leaves, group * head_dim).astype(jnp.bfloat16)]
-        + split_two(own_weight)
-        + split_three(own_peak),
+        [
+            jnp.where(root_mine[:, None], own_values, zeros_values),
+            jnp.where(branch_mine[:, None], own_values, zeros_values),
+            jnp.where(root_mine[:, None], own_stats, zeros_stats),
+            jnp.where(branch_mine[:, None], own_stats, zeros_stats),
+            jnp.zeros((total_leaves, pad_width), jnp.bfloat16),
+        ],
         -1,
     )
-    zeros = jnp.zeros_like(packet)
-    packet = jnp.stack(
-        [
-            jnp.where(root_mine[:, None], packet, zeros),
-            jnp.where(branch_mine[:, None], packet, zeros),
-        ],
-        1,
-    )
-    width = packet.shape[-1]
-    gathered = scatter_rows(
-        scatter_rows(packet.reshape(total_leaves * 2, width), ("y", "core")), "z"
-    ).reshape(local_leaves, 2, width)
+    gathered = scatter_rows(scatter_rows(packet, ("y", "core")), "z")
     sums = []
     weights = []
     peaks = []
     for part in range(2):
-        piece = gathered[:, part]
         sums.append(
-            piece[:, : group * head_dim].astype(jnp.float32).reshape(local_leaves, group, head_dim)
+            gathered[:, part * group * head_dim : (part + 1) * group * head_dim]
+            .astype(jnp.float32)
+            .reshape(local_leaves, group, head_dim)
         )
-        base = group * head_dim
-        weights.append(join([piece[:, base + k * group : base + (k + 1) * group] for k in range(2)]))
+        base = 2 * group * head_dim + part * stat_width
+        weights.append(join([gathered[:, base + k * group : base + (k + 1) * group] for k in range(2)]))
         base = base + 2 * group
-        peaks.append(join([piece[:, base + k * group : base + (k + 1) * group] for k in range(3)]))
+        peaks.append(join([gathered[:, base + k * group : base + (k + 1) * group] for k in range(3)]))
     sums.append(leaf_sum)
     weights.append(leaf_weight)
     peaks.append(leaf_peak)

time: 170 us -> 159 us (0.935)
  blocking collectives: 29.8 us -> 0 us
  starting transfers between devices: 19.1 us -> 34.3 us
  local copies, waits for them, and re-layouts: 31.2 us -> 16.4 us
  waiting for transfers between devices: 57.9 us -> 69 us
  other arithmetic: 13.4 us -> 19.5 us
    all_to_all x1 -> x0, blocking collectives: 29.8 us -> none  [gather_rows(): received = lax.all_to_all(spread, axes, 0, 0, tiled=False)]
    another operation x3 -> x0, local copies, waits for them, and re-layouts: 18.4 us -> none  [the longest x2 11 us: scatter_rows(): blocks = values.reshape(count, values.shape[0] // count, values.shape[1])]
    all_to_all x1 -> x2, starting transfers between devices: 4.69 us -> 19.9 us  [gather_rows(): received = lax.all_to_all(spread, axes, 0, 0, tiled=False)]
    all_to_all x1 -> x2, waiting for transfers between devices: 10.5 us -> 21.7 us  [gather_rows(): received = lax.all_to_all(spread, axes, 0, 0, tiled=False)]
    unnamed x4 -> x8, other arithmetic: 0.03 us -> 3.81 us
  transfers between devices with their start and end apart: 4 -> 5, of which waited for: 4 -> 5; matrix products, arithmetic and copies ran while one was open for 5% -> 7% of each run, Pallas kernels for 0% -> 0%
where the time goes in v4:
time: 159 us; the launch traced here: 156 us
  waiting for transfers between devices  69 us (43%)
  starting transfers between devices  34.3 us (22%)
  other arithmetic  19.5 us (12%)
  local copies, waits for them, and re-layouts  16.4 us (10%)
  matrix products  14.6 us (9%)
  between operations  2.15 us (1%)
    all_to_all x2, waiting for transfers between devices, scatter_rows(): received = lax.all_to_all(blocks, axes, 0, 0, tiled=False)  42.3 us
    all_to_all x2, waiting for transfers between devices, gather_rows(): received = lax.all_to_all(spread, axes, 0, 0, tiled=False)  21.7 us
    all_to_all x2, starting transfers between devices, gather_rows(): received = lax.all_to_all(spread, axes, 0, 0, tiled=False)  19.9 us
    all_to_all x2, starting transfers between devices, scatter_rows(): received = lax.all_to_all(blocks, axes, 0, 0, tiled=False)  10.1 us
    all_to_all x1, waiting for transfers between devices, local(): lax.all_to_all(term.reshape(local_leaves, tensor_size, term.shape[1] // t...  4.97 us
    dot_general x2, matrix products, soft_part(): jnp.einsum(pattern, weights, value_rows, preferred_element_type=jnp.float32)  4.9 us
    all_to_all x1, starting transfers between devices, local(): lax.all_to_all(term.reshape(local_leaves, tensor_size, term.shape[1] // t...  4.3 us
    reduce_sum x2, other arithmetic, soft_part(): weight_sum = jnp.sum(weights.astype(jnp.float32), -1)  4.22 us
  transfers between devices with their start and end apart: 5, of which 5 were waited for; matrix products, arithmetic and copies ran while one was open for 7% of the time, Pallas kernels for 0%

profile of v4, /device:TPU:24, one launch (start us, length us, event | category | flops | bytes accessed | tf_op | source)
XLA Modules:
  0.0 155.9 jit_solution(1187720080680387820)
XLA Ops:
  0.7 1.0 fusion.11
  1.7 1.3 fusion.20
  3.0 1.2 fusion.22
  4.2 0.1 reshape.352
  4.3 0.1 slice_negate_fusion
  4.4 0.8 dynamic_slice.3
  5.1 0.9 select_reduce_fusion
  6.0 0.8 select_reduce_fusion.1
  6.9 0.7 add_convert_fusion.3
  7.5 0.1 slice_negate_fusion.1
  7.6 0.1 fusion.29
  7.7 0.1 maximum_multiply_fusion
  7.8 0.1 mul.157
  7.9 0.1 mul.153
  8.0 0.7 broadcast_in_dim.204
  8.6 15.2 %all-to-all-start = ((bf16[16,8,512]{2,1,0:T(8,128)(2,1)}), bf16[16,8,512]{2,1,0:T(8,128)(2,1)S(1)}, u32[]{:S(2)}, u32[]{:S(2)}) async-start(bf16[16,8,512]{2,1,0:T(8,128)(2,1)} %broadcast_in_dim.204), calls=%async_computation | async-start | bytes 262144 | tf_op jit(solution)/shard_map/all_to_all | solution.py:60
  23.8 0.8 reshape.351
  24.6 0.1 eq.40
  24.7 1.0 copy.53
  25.7 1.3 select_reduce_fusion.4
  27.0 0.7 fusion.27
  27.8 10.8 %all-to-all-done = bf16[16,8,512]{2,1,0:T(8,128)(2,1)S(1)} async-done(((bf16[16,8,512]{2,1,0:T(8,128)(2,1)}), bf16[16,8,512]{2,1,0:T(8,128)(2,1)S(1)}, u32[]{:S(2)}, u32[]{:S(2)}) %all-to-all-start) | async-done | bytes 131104 | tf_op jit(solution)/shard_map/all_to_all | solution.py:60
  38.6 0.1 copy.51
  38.7 1.2 broadcast_in_dim.206
  39.9 4.7 %all-to-all-start.1 = ((bf16[8,128,512]{1,2,0:T(8,128)(2,1)}), bf16[8,128,512]{1,2,0:T(8,128)(2,1)}, u32[]{:S(2)}, u32[]{:S(2)}) async-start(bf16[8,128,512]{1,2,0:T(8,128)(2,1)} %broadcast_in_dim.206), calls=%async_computation.1 | async-start | bytes 2097152 | tf_op jit(solution)/shard_map/all_to_all | solution.py:60
  44.6 1.3 select_reduce_fusion.3
  45.9 0.1 fusion.8
  47.4 0.3 broadcast_and_fusion
  47.7 10.9 %all-to-all-done.1 = bf16[8,128,512]{1,2,0:T(8,128)(2,1)} async-done(((bf16[8,128,512]{1,2,0:T(8,128)(2,1)}), bf16[8,128,512]{1,2,0:T(8,128)(2,1)}, u32[]{:S(2)}, u32[]{:S(2)}) %all-to-all-start.1) | async-done | bytes 1048608 | tf_op jit(solution)/shard_map/all_to_all | solution.py:60
  58.6 2.9 %copy.52 = bf16[8,128,512]{1,0,2:T(8,128)(2,1)} copy(bf16[8,128,512]{1,2,0:T(8,128)(2,1)} %all-to-all-done.1) | data formatting | bytes 2097152 | tf_op jit(solution)/shard_map/all_to_all | solution.py:60
  61.5 2.3 %reshape_reshape.3 = bf16[1024,8,64]{0,2,1:T(8,128)(2,1)} reshape(bf16[8,128,512]{1,0,2:T(8,128)(2,1)} %copy.52) | data formatting | bytes 2097152 | tf_op jit(solution)/shard_map/reshape;reshape | solution.py:156
  63.8 4.1 %fusion = (f32[1024,8]{0,1:T(8,128)S(1)}, f32[1024,8,512]{0,2,1:T(8,128)S(1)}) fusion(pred[1024,512]{0,1:T(8,128)(4,1)S(1)} %broadcast_and_fusion, bf16[1024,8,64]{0,2,1:T(8,128)(2,1)} %reshape_reshape.3, bf16[512,128]{0,1:T(8,128)(2,1)S(1)} %bitcast.72), kind=kOutput, calls=%fused_computation.3 | convolution fusion | flops 549445632 | bytes 18448384 | tf_op jit(solution)/shard_map/ngd,kd->ngk/dot_general | solution.py:158
  67.9 4.1 %convert_reduce_fusion = f32[1024,8]{0,1:T(8,128)S(1)} fusion(f32[1024,8]{0,1:T(8,128)S(1)} %get-tuple-element.25, f32[1024,8,512]{0,2,1:T(8,128)S(1)} %get-tuple-element.26, pred[1024,512]{0,1:T(8,128)(4,1)S(1)} %broadcast_and_fusion), kind=kLoop, calls=%fused_computation | loop fusion | flops 29351936 | bytes 17367040 | tf_op jit(solution)/shard_map/reduce_sum | solution.py:25
  72.0 4.7 %convolution_convert_fusion = bf16[1024,8,64]{0,2,1:T(8,128)(2,1)S(1)} fusion(bf16[512,128]{0,1:T(8,128)(2,1)S(1)} %bitcast.73, f32[1024,8,512]{0,2,1:T(8,128)S(1)} %get-tuple-element.26, f32[1024,8]{0,1:T(8,128)S(1)} %get-tuple-element.25, pred[1024,512]{0,1:T(8,128)(4,1)S(1)} %broadcast_and_fusion), kind=kOutput, calls=%fused_computation.4 | convolution fusion | flops 558366720 | bytes 18448384 | tf_op jit(solution)/shard_map/ngk,kd->ngd/dot_general | solution.py:24
  76.8 0.3 copy.64
  77.0 1.2 select_dynamic-update-slice_fusion.1
  78.3 1.2 select_dynamic-update-slice_fusion
  79.5 0.7 select_dynamic-update-slice_fusion.3
  80.1 0.7 select_dynamic-update-slice_fusion.2
  80.8 0.7 broadcast_dynamic-update-slice_fusion
  81.4 6.3 %all-to-all-start.2 = ((bf16[8,128,1152]{1,2,0:T(8,128)(2,1)}), bf16[8,128,1152]{1,2,0:T(8,128)(2,1)}, u32[]{:S(2)}, u32[]{:S(2)}) async-start(bf16[8,128,1152]{1,2,0:T(8,128)(2,1)} %broadcast_dynamic-update-slice_fusion), calls=%async_computation.2 | async-start | bytes 4718592 | tf_op jit(solution)/shard_map/all_to_all | solution.py:67
  87.9 0.2 copy.59
  88.0 3.9 %copy.62 = bf16[2048,512]{1,0:T(8,128)(2,1)} copy(bf16[2048,512]{0,1:T(8,128)(2,1)} %bitcast.69) | data formatting | bytes 4194304 | tf_op jit(solution)/shard_map/dot_general | solution.py:211
  92.0 23.8 %all-to-all-done.2 = bf16[8,128,1152]{1,2,0:T(8,128)(2,1)} async-done(((bf16[8,128,1152]{1,2,0:T(8,128)(2,1)}), bf16[8,128,1152]{1,2,0:T(8,128)(2,1)}, u32[]{:S(2)}, u32[]{:S(2)}) %all-to-all-start.2) | async-done | bytes 2359328 | tf_op jit(solution)/shard_map/all_to_all | solution.py:67
  115.8 2.1 %reduce_sum.115 = bf16[128,1152]{0,1:T(8,128)(2,1)S(1)} reduce(bf16[8,128,1152]{1,2,0:T(8,128)(2,1)} %all-to-all-done.2, bf16[]{:T(256)} %constant.50.clone.1), dimensions={0}, to_apply=%region_11.12 | reduce | flops 1032192 | bytes 2654210 | tf_op jit(solution)/shard_map/reduce_sum | solution.py:68
  117.9 0.9 copy.58
  118.8 3.8 %all-to-all-start.3 = ((bf16[16,8,1152]{2,1,0:T(8,128)(2,1)}), bf16[16,8,1152]{2,1,0:T(8,128)(2,1)S(1)}, u32[]{:S(2)}, u32[]{:S(2)}) async-start(bf16[16,8,1152]{2,1,0:T(8,128)(2,1)} %bitcast.9), calls=%async_computation.3 | async-start | bytes 589824 | tf_op jit(solution)/shard_map/all_to_all | solution.py:67
  122.6 0.1 pad_maximum_fusion.1
  122.6 0.1 iota_compare_fusion.2
  122.7 0.2 bitcast_select_fusion
  122.9 0.2 fusion.30
  123.1 0.2 convert_reduce_fusion.1
  123.3 0.1 slice_bitcast_fusion.4
  123.4 18.5 %all-to-all-done.3 = bf16[16,8,1152]{2,1,0:T(8,128)(2,1)S(1)} async-done(((bf16[16,8,1152]{2,1,0:T(8,128)(2,1)}), bf16[16,8,1152]{2,1,0:T(8,128)(2,1)S(1)}, u32[]{:S(2)}, u32[]{:S(2)}) %all-to-all-start.3) | async-done | bytes 294944 | tf_op jit(solution)/shard_map/all_to_all | solution.py:67
  141.9 0.1 multiply_add_fusion
  142.0 0.1 reshape.360
  142.1 0.1 reshape.362
  142.2 0.2 fusion.4
  142.4 0.1 reshape.365
  142.5 2.9 %fusion.31 = f32[8,4,512]{2,0,1:T(8,128)} fusion(bf16[8,512,1]{1,0,2:T(8,128)(2,1)S(1)} %reshape.365, bf16[4,512,512]{2,1,0:T(8,128)(2,1)} %bitcast.68), kind=kOutput, calls=%fused_computation.96 | convolution fusion | flops 16777216 | bytes 2170880 | tf_op jit(solution)/shard_map/dot_general | solution.py:211
  145.4 4.3 %all-to-all-start.4 = ((f32[8,4,512]{2,0,1:T(8,128)}), f32[8,4,512]{2,0,1:T(8,128)S(1)}, u32[]{:S(2)}, u32[]{:S(2)}) async-start(f32[8,4,512]{2,0,1:T(8,128)} %fusion.31), calls=%async_computation.4 | async-start | bytes 131072 | tf_op jit(solution)/shard_map/all_to_all | solution.py:213
  149.7 0.7 pad_maximum_fusion.2
  150.3 5.0 %all-to-all-done.4 = f32[8,4,512]{2,0,1:T(8,128)S(1)} async-done(((f32[8,4,512]{2,0,1:T(8,128)}), f32[8,4,512]{2,0,1:T(8,128)S(1)}, u32[]{:S(2)}, u32[]{:S(2)}) %all-to-all-start.4) | async-done | bytes 65568 | tf_op jit(solution)/shard_map/all_to_all | solution.py:213
  155.3 0.6 reduce_sum.118
  (22 shorter events, 0.3 us)
Async XLA Ops:
  0.6 2.4 %copy-start = (bf16[2048,512]{1,0:T(8,128)(2,1)S(1)}, bf16[2048,512]{1,0:T(8,128)(2,1)}, u32[]{:S(2)}) copy-start(bf16[2048,512]{1,0:T(8,128)(2,1)} %param.16) | copy-start | bytes 6291460
  8.6 30.0 %all-to-all-start = ((bf16[16,8,512]{2,1,0:T(8,128)(2,1)}), bf16[16,8,512]{2,1,0:T(8,128)(2,1)S(1)}, u32[]{:S(2)}, u32[]{:S(2)}) async-start(bf16[16,8,512]{2,1,0:T(8,128)(2,1)} %broadcast_in_dim.204), calls=%async_computation | async-start | bytes 262144 | tf_op jit(solution)/shard_map/all_to_all | solution.py:60
  39.9 18.7 %all-to-all-start.1 = ((bf16[8,128,512]{1,2,0:T(8,128)(2,1)}), bf16[8,128,512]{1,2,0:T(8,128)(2,1)}, u32[]{:S(2)}, u32[]{:S(2)}) async-start(bf16[8,128,512]{1,2,0:T(8,128)(2,1)} %broadcast_in_dim.206), calls=%async_computation.1 | async-start | bytes 2097152 | tf_op jit(solution)/shard_map/all_to_all | solution.py:60
  76.6 11.2 %copy-start.1 = (bf16[8,1,128,128]{3,2,1,0:T(8,128)(2,1)S(1)}, bf16[8,1,128,128]{3,2,1,0:T(8,128)(2,1)}, u32[]{:S(2)}) copy-start(bf16[8,1,128,128]{3,2,1,0:T(8,128)(2,1)} %param.20) | copy-start | bytes 786436
  78.3 44.4 %copy-start.2 = (s32[8]{0:T(128)S(1)}, s32[8]{0:T(128)}, u32[]{:S(2)}) copy-start(s32[8]{0:T(128)} %param.27) | copy-start | bytes 100
  81.4 34.3 %all-to-all-start.2 = ((bf16[8,128,1152]{1,2,0:T(8,128)(2,1)}), bf16[8,128,1152]{1,2,0:T(8,128)(2,1)}, u32[]{:S(2)}, u32[]{:S(2)}) async-start(bf16[8,128,1152]{1,2,0:T(8,128)(2,1)} %broadcast_dynamic-update-slice_fusion), calls=%async_computation.2 | async-start | bytes 4718592 | tf_op jit(solution)/shard_map/all_to_all | solution.py:67
  118.8 23.1 %all-to-all-start.3 = ((bf16[16,8,1152]{2,1,0:T(8,128)(2,1)}), bf16[16,8,1152]{2,1,0:T(8,128)(2,1)S(1)}, u32[]{:S(2)}, u32[]{:S(2)}) async-start(bf16[16,8,1152]{2,1,0:T(8,128)(2,1)} %bitcast.9), calls=%async_computation.3 | async-start | bytes 589824 | tf_op jit(solution)/shard_map/all_to_all | solution.py:67
  145.4 9.9 %all-to-all-start.4 = ((f32[8,4,512]{2,0,1:T(8,128)}), f32[8,4,512]{2,0,1:T(8,128)S(1)}, u32[]{:S(2)}, u32[]{:S(2)}) async-start(f32[8,4,512]{2,0,1:T(8,128)} %fusion.31), calls=%async_computation.4 | async-start | bytes 131072 | tf_op jit(solution)/shard_map/all_to_all | solution.py:213

commit v5 on v4

--- a/solution.py
+++ b/solution.py
@@ -112,8 +112,10 @@
         local_leaves, group, head_dim
     )
     queries = rotate(raw_query, positions[:, None]).astype(jnp.bfloat16)
-    everyone = gather_rows(
-        gather_rows(queries.reshape(local_leaves, group * head_dim), "z"), ("y", "core")
+    everyone = gather_rows(queries.reshape(local_leaves, group * head_dim), "z")
+    node_rows = node_cache[0, 0]
+    slots = gather_rows(node_rows, ("y", "core")).reshape(
+        -1, node_rows.shape[0], node_rows.shape[1]
     )
     raw_entry = jnp.dot(normed, w_keyval, preferred_element_type=jnp.float32)
     new_entry = jnp.concatenate(
@@ -135,51 +137,65 @@
         leaf_scores, leaf_usable, appended[:, :, head_dim:], "lgk,lkd->lgd"
     )
 
-    total_leaves = everyone.shape[0]
+    row_count = everyone.shape[0]
+    slot_count = slots.shape[0]
     z_size = lax.axis_size("z")
-    row_branch = (
-        leaf_branch.reshape(z_size, total_leaves // (z_size * local_leaves), local_leaves)
-        .transpose(1, 0, 2)
-        .reshape(total_leaves)
-    )
+    my_y_core = device % slot_count
+    first_slot = device - my_y_core
+    row_branch = lax.dynamic_slice_in_dim(
+        leaf_branch.reshape(z_size, slot_count * local_leaves),
+        my_y_core * local_leaves,
+        local_leaves,
+        axis=1,
+    ).reshape(row_count)
+    slot_ids = first_slot + jnp.arange(slot_count, dtype=jnp.int32)
     branch_root_hits = branch_root[:, None] == root_ids[None, :]
-    root_mine_by_branch = jnp.any(branch_root_hits & (root_owner == device)[None, :], 1)
+    root_slot_of_branch = jnp.any(
+        branch_root_hits[:, None, :] & (root_owner[None, None, :] == slot_ids[None, :, None]), 2
+    )
+    branch_slot_of_branch = branch_owner[:, None] == slot_ids[None, :]
     row_hits = row_branch[:, None] == branch_ids[None, :]
-    root_mine = jnp.any(row_hits & root_mine_by_branch[None, :], 1)
-    branch_mine = jnp.any(row_hits & (branch_owner == device)[None, :], 1)
+    root_mine = jnp.any(row_hits[:, :, None] & root_slot_of_branch[None, :, :], 1)
+    branch_mine = jnp.any(row_hits[:, :, None] & branch_slot_of_branch[None, :, :], 1)
     mine_all = root_mine | branch_mine
-    my_length = jnp.sum(jnp.where(root_owner == device, root_len, 0)) + jnp.sum(
-        jnp.where(branch_owner == device, branch_len, 0)
-    )
-    node_rows = node_cache[0, 0]
-    node_usable = jnp.arange(node_rows.shape[0], dtype=jnp.int32) < my_length
-    rows_query = everyone.reshape(total_leaves, group, head_dim)
+    slot_length = jnp.sum(
+        jnp.where(root_owner[None, :] == slot_ids[:, None], root_len[None, :], 0), 1
+    ) + jnp.sum(jnp.where(branch_owner[None, :] == slot_ids[:, None], branch_len[None, :], 0), 1)
+    node_usable = (
+        jnp.arange(slots.shape[1], dtype=jnp.int32)[None, :] < slot_length[:, None]
+    )
+    rows_query = everyone.reshape(row_count, group, head_dim)
     scores = (
         jnp.einsum(
-            "ngd,kd->ngk", rows_query, node_rows[:, :head_dim], preferred_element_type=jnp.float32
+            "ngd,skd->nsgk", rows_query, slots[:, :, :head_dim], preferred_element_type=jnp.float32
         )
         * factor
     )
-    usable = mine_all[:, None, None] & node_usable[None, None, :]
-    own_sum, own_weight, own_peak = soft_part(scores, usable, node_rows[:, head_dim:], "ngk,kd->ngd")
-    own_peak = jnp.where(mine_all[:, None], own_peak, 0.0)
-    own_values = own_sum.reshape(total_leaves, group * head_dim).astype(jnp.bfloat16)
-    own_stats = jnp.concatenate(split_two(own_weight) + split_three(own_peak), -1)
-    stat_width = own_stats.shape[1]
+    usable = mine_all[:, :, None, None] & node_usable[None, :, None, :]
+    slot_sum, slot_weight, slot_peak = soft_part(
+        scores, usable, slots[:, :, head_dim:], "nsgk,skd->nsgd"
+    )
+    slot_peak = jnp.where(mine_all[:, :, None], slot_peak, 0.0)
+
+    def pick(mask, values):
+        shape = mask.shape + (1,) * (values.ndim - mask.ndim)
+        return jnp.sum(jnp.where(mask.reshape(shape), values, 0.0), 1)
+
+    parts = [
+        (pick(mask, slot_sum), pick(mask, slot_weight), pick(mask, slot_peak))
+        for mask in (root_mine, branch_mine)
+    ]
+    pieces = []
+    stats = []
+    for part_sum, part_weight, part_peak in parts:
+        pieces.append(part_sum.reshape(row_count, group * head_dim).astype(jnp.bfloat16))
+        stats.append(jnp.concatenate(split_two(part_weight) + split_three(part_peak), -1))
+    stat_width = stats[0].shape[1]
     pad_width = (-(2 * group * head_dim + 2 * stat_width)) % 128
-    zeros_values = jnp.zeros_like(own_values)
-    zeros_stats = jnp.zeros_like(own_stats)
     packet = jnp.concatenate(
-        [
-            jnp.where(root_mine[:, None], own_values, zeros_values),
-            jnp.where(branch_mine[:, None], own_values, zeros_values),
-            jnp.where(root_mine[:, None], own_stats, zeros_stats),
-            jnp.where(branch_mine[:, None], own_stats, zeros_stats),
-            jnp.zeros((total_leaves, pad_width), jnp.bfloat16),
-        ],
-        -1,
-    )
-    gathered = scatter_rows(scatter_rows(packet, ("y", "core")), "z")
+        pieces + stats + [jnp.zeros((row_count, pad_width), jnp.bfloat16)], -1
+    )
+    gathered = scatter_rows(packet, "z")
     sums = []
     weights = []
     peaks = []

time: 159 us -> 119 us (0.75)
  the two profiles are of different devices: /device:TPU:24 before, /device:TPU:32 now
where the time goes in v5:
time: 119 us
  waiting for transfers between devices  44.2 us (37%)
  starting transfers between devices  28.3 us (24%)
  matrix products  15.8 us (13%)
  other arithmetic  15.7 us (13%)
  local copies, waits for them, and re-layouts  13.7 us (12%)
    all_to_all x2, waiting for transfers between devices, gather_rows(): received = lax.all_to_all(spread, axes, 0, 0, tiled=False)  20.7 us
    all_to_all x2, starting transfers between devices, gather_rows(): received = lax.all_to_all(spread, axes, 0, 0, tiled=False)  19.7 us
    all_to_all x1, waiting for transfers between devices, scatter_rows(): received = lax.all_to_all(blocks, axes, 0, 0, tiled=False)  18.5 us
    reduce_sum x2, other arithmetic, soft_part(): weight_sum = jnp.sum(weights.astype(jnp.float32), -1)  7.8 us
    dot_general x2, matrix products, soft_part(): jnp.einsum(pattern, weights, value_rows, preferred_element_type=jnp.float32)  6.35 us
    all_to_all x1, waiting for transfers between devices, local(): lax.all_to_all(term.reshape(local_leaves, tensor_size, term.shape[1] // t...  4.97 us
    all_to_all x1, starting transfers between devices, local(): lax.all_to_all(term.reshape(local_leaves, tensor_size, term.shape[1] // t...  4.36 us
    all_to_all x1, starting transfers between devices, scatter_rows(): received = lax.all_to_all(blocks, axes, 0, 0, tiled=False)  4.31 us
  transfers between devices with their start and end apart: 4, of which 4 were waited for; matrix products, arithmetic and copies ran while one was open for 9% of the time, Pallas kernels for 0%

profile of v5, /device:TPU:32, one launch (start us, length us, event | category | flops | bytes accessed | tf_op | source)
XLA Modules:
  0.0 118.7 jit_solution(1986821233197314440)
XLA Ops:
  0.7 1.0 fusion.15
  1.7 1.3 %fusion.21 = f32[8,128]{1,0:T(8,128)S(1)} fusion(bf16[2048,128]{1,0:T(8,128)(2,1)} %param.17, bf16[8,2048]{1,0:T(8,128)(2,1)} %param.14, f32[2048]{0:T(1024)} %param.15, f32[8]{0:T(128)S(1)} %add_rsqrt_fusion), kind=kOutput, calls=%fused_computation.59 | convolution fusion | flops 4259840 | bytes 569376 | tf_op jit(solution)/shard_map/dot_general | solution.py:120
  3.1 1.2 fusion.23
  4.4 0.8 dynamic_slice.7
  5.2 0.9 select_reduce_fusion.7
  6.1 0.9 select_reduce_fusion.8
  7.0 0.7 add_convert_fusion.3
  7.7 0.1 fusion.28
  8.1 0.7 broadcast_in_dim.216
  8.7 15.2 %all-to-all-start = ((bf16[16,8,512]{2,1,0:T(8,128)(2,1)}), bf16[16,8,512]{2,1,0:T(8,128)(2,1)S(1)}, u32[]{:S(2)}, u32[]{:S(2)}) async-start(bf16[16,8,512]{2,1,0:T(8,128)(2,1)} %broadcast_in_dim.216), calls=%async_computation | async-start | bytes 262144 | tf_op jit(solution)/shard_map/all_to_all | solution.py:60
  23.9 0.8 reshape.434
  24.7 0.7 iota_compare_fusion.6
  25.5 0.1 eq.132
  25.6 1.0 copy.73
  26.6 0.7 broadcast_compare_fusion.1
  27.3 10.8 %all-to-all-done = bf16[16,8,512]{2,1,0:T(8,128)(2,1)S(1)} async-done(((bf16[16,8,512]{2,1,0:T(8,128)(2,1)}), bf16[16,8,512]{2,1,0:T(8,128)(2,1)S(1)}, u32[]{:S(2)}, u32[]{:S(2)}) %all-to-all-start) | async-done | bytes 131104 | tf_op jit(solution)/shard_map/all_to_all | solution.py:60
  38.2 1.1 broadcast_in_dim.218
  39.2 4.5 %all-to-all-start.1 = ((bf16[8,512,128]{1,2,0:T(8,128)(2,1)}), bf16[8,512,128]{1,2,0:T(8,128)(2,1)}, u32[]{:S(2)}, u32[]{:S(2)}) async-start(bf16[8,512,128]{1,2,0:T(8,128)(2,1)} %broadcast_in_dim.218), calls=%async_computation.1 | async-start | bytes 2097152 | tf_op jit(solution)/shard_map/all_to_all | solution.py:60
  43.7 0.1 and_reduce_fusion.2
  43.8 0.1 copy.72
  43.9 1.1 copy.96
  45.0 3.9 %copy.102 = bf16[2048,512]{1,0:T(8,128)(2,1)} copy(bf16[2048,512]{0,1:T(8,128)(2,1)} %bitcast.51) | data formatting | bytes 4194304 | tf_op jit(solution)/shard_map/dot_general | solution.py:227
  49.0 0.2 and_reduce_fusion
  49.4 0.3 broadcast_and_fusion
  49.7 0.2 reshape_reshape.3
  49.9 9.9 %all-to-all-done.1 = bf16[8,512,128]{1,2,0:T(8,128)(2,1)} async-done(((bf16[8,512,128]{1,2,0:T(8,128)(2,1)}), bf16[8,512,128]{1,2,0:T(8,128)(2,1)}, u32[]{:S(2)}, u32[]{:S(2)}) %all-to-all-start.1) | async-done | bytes 1048608 | tf_op jit(solution)/shard_map/all_to_all | solution.py:60
  59.8 3.9 %bitcast_reduce_fusion = (f32[128,8,8]{0,1,2:T(8,128)S(1)}, f32[128,8,8,512]{3,0,2,1:T(8,128)S(1)}) fusion(pred[128,8,512]{2,0,1:T(8,128)(4,1)S(1)} %broadcast_and_fusion, bf16[8,512,128]{1,2,0:T(8,128)(2,1)} %all-to-all-done.1, bf16[128,8,64,1]{2,1,0,3:T(8,128)(2,1)S(1)} %bitcast.52), kind=kOutput, calls=%fused_computation.1 | convolution fusion | flops 549445632 | bytes 17989632 | tf_op jit(solution)/shard_map/ngd,skd->nsgk/dot_general | solution.py:169
  63.6 7.6 %convert_reduce_fusion = (f32[128,8,8]{0,1,2:T(8,128)S(1)}, bf16[128,8,8,512]{3,0,1,2:T(8,128)(2,1)}) fusion(f32[128,8,8]{0,1,2:T(8,128)S(1)} %get-tuple-element.44, f32[128,8,8,512]{3,0,2,1:T(8,128)S(1)} %get-tuple-element.45, pred[128,8,512]{2,0,1:T(8,128)(4,1)S(1)} %broadcast_and_fusion), kind=kLoop, calls=%fused_computation.5 | loop fusion | flops 29351936 | bytes 25755648 | tf_op jit(solution)/shard_map/reduce_sum | solution.py:25
  71.3 0.1 reduce_sum.167
  71.4 0.1 copy.80
  71.5 0.1 copy.88
  71.6 0.1 copy.89
  71.7 0.1 copy.90
  71.8 0.1 reduce_sum.171
  71.9 0.1 copy.84
  72.0 0.1 copy.93
  72.1 0.1 copy.94
  72.2 0.1 copy.95
  72.3 0.1 reduce_sum.165
  72.4 0.1 copy.78
  72.5 0.1 copy.86
  72.6 0.1 copy.87
  72.7 0.1 reduce_sum.169
  72.9 0.1 copy.91
  73.0 0.1 copy.92
  73.1 6.1 %fusion.6 = (bf16[128,8,64]{0,2,1:T(8,128)(2,1)S(1)}, bf16[128,8,64]{0,2,1:T(8,128)(2,1)S(1)}) fusion(pred[128,8]{0,1:T(8,128)(4,1)S(1)} %get-tuple-element.8, pred[128,8]{0,1:T(8,128)(4,1)S(1)} %get-tuple-element.9, bf16[8,512,128]{1,2,0:T(8,128)(2,1)} %all-to-all-done.1, bf16[128,8,8,512]{3,0,1,2:T(8,128)(2,1)} %get-tuple-element.26), kind=kOutput, calls=%fused_computation.12 | convolution fusion | flops 538836992 | bytes 9177088 | tf_op jit(solution)/shard_map/nsgk,skd->nsgd/dot_general | solution.py:24
  79.3 0.2 copy.76
  79.5 0.2 convert_element_type.173
  79.7 0.2 copy.77
  79.9 0.2 convert_element_type.175
  80.1 0.9 concatenate.45
  81.0 4.3 %all-to-all-start.2 = ((bf16[16,8,1152]{2,1,0:T(8,128)(2,1)}), bf16[16,8,1152]{2,1,0:T(8,128)(2,1)S(1)}, u32[]{:S(2)}, u32[]{:S(2)}) async-start(bf16[16,8,1152]{2,1,0:T(8,128)(2,1)} %concatenate.45), calls=%async_computation.2 | async-start | bytes 589824 | tf_op jit(solution)/shard_map/all_to_all | solution.py:67
  85.4 0.2 bitcast_select_fusion.2
  85.6 0.2 fusion.30
  85.9 0.2 convert_reduce_fusion.1
  86.1 18.5 %all-to-all-done.2 = bf16[16,8,1152]{2,1,0:T(8,128)(2,1)S(1)} async-done(((bf16[16,8,1152]{2,1,0:T(8,128)(2,1)}), bf16[16,8,1152]{2,1,0:T(8,128)(2,1)S(1)}, u32[]{:S(2)}, u32[]{:S(2)}) %all-to-all-start.2) | async-done | bytes 294944 | tf_op jit(solution)/shard_map/all_to_all | solution.py:67
  104.6 0.1 multiply_add_fusion
  104.9 0.2 fusion.10
  105.1 0.1 reshape.448
  105.2 2.9 %fusion.31 = f32[8,4,512]{2,0,1:T(8,128)} fusion(bf16[8,512,1]{1,0,2:T(8,128)(2,1)S(1)} %reshape.448, bf16[4,512,512]{2,1,0:T(8,128)(2,1)} %bitcast.50), kind=kOutput, calls=%fused_computation.97 | convolution fusion | flops 16777216 | bytes 2170880 | tf_op jit(solution)/shard_map/dot_general | solution.py:227
  108.1 4.4 %all-to-all-start.3 = ((f32[8,4,512]{2,0,1:T(8,128)}), f32[8,4,512]{2,0,1:T(8,128)S(1)}, u32[]{:S(2)}, u32[]{:S(2)}) async-start(f32[8,4,512]{2,0,1:T(8,128)} %fusion.31), calls=%async_computation.3 | async-start | bytes 131072 | tf_op jit(solution)/shard_map/all_to_all | solution.py:229
  112.4 0.7 pad_maximum_fusion.2
  113.1 5.0 %all-to-all-done.3 = f32[8,4,512]{2,0,1:T(8,128)S(1)} async-done(((f32[8,4,512]{2,0,1:T(8,128)}), f32[8,4,512]{2,0,1:T(8,128)S(1)}, u32[]{:S(2)}, u32[]{:S(2)}) %all-to-all-start.3) | async-done | bytes 65568 | tf_op jit(solution)/shard_map/all_to_all | solution.py:229
  118.1 0.6 reduce_sum.174
  (38 shorter events, 1.4 us)
Async XLA Ops:
  0.6 2.4 %copy-start = (bf16[2048,512]{1,0:T(8,128)(2,1)S(1)}, bf16[2048,512]{1,0:T(8,128)(2,1)}, u32[]{:S(2)}) copy-start(bf16[2048,512]{1,0:T(8,128)(2,1)} %param.16) | copy-start | bytes 6291460
  0.6 48.3 %copy-start.2 = (s32[64]{0:T(128)S(1)}, s32[64]{0:T(128)}, u32[]{:S(2)}) copy-start(s32[64]{0:T(128)} %param.24) | copy-start | bytes 772
  8.7 29.4 %all-to-all-start = ((bf16[16,8,512]{2,1,0:T(8,128)(2,1)}), bf16[16,8,512]{2,1,0:T(8,128)(2,1)S(1)}, u32[]{:S(2)}, u32[]{:S(2)}) async-start(bf16[16,8,512]{2,1,0:T(8,128)(2,1)} %broadcast_in_dim.216), calls=%async_computation | async-start | bytes 262144 | tf_op jit(solution)/shard_map/all_to_all | solution.py:60
  39.2 20.5 %all-to-all-start.1 = ((bf16[8,512,128]{1,2,0:T(8,128)(2,1)}), bf16[8,512,128]{1,2,0:T(8,128)(2,1)}, u32[]{:S(2)}, u32[]{:S(2)}) async-start(bf16[8,512,128]{1,2,0:T(8,128)(2,1)} %broadcast_in_dim.218), calls=%async_computation.1 | async-start | bytes 2097152 | tf_op jit(solution)/shard_map/all_to_all | solution.py:60
  73.1 12.2 %copy-start.1 = (s32[8]{0:T(128)S(1)}, s32[8]{0:T(128)}, u32[]{:S(2)}) copy-start(s32[8]{0:T(128)} %param.27) | copy-start | bytes 100
  81.0 23.6 %all-to-all-start.2 = ((bf16[16,8,1152]{2,1,0:T(8,128)(2,1)}), bf16[16,8,1152]{2,1,0:T(8,128)(2,1)S(1)}, u32[]{:S(2)}, u32[]{:S(2)}) async-start(bf16[16,8,1152]{2,1,0:T(8,128)(2,1)} %concatenate.45), calls=%async_computation.2 | async-start | bytes 589824 | tf_op jit(solution)/shard_map/all_to_all | solution.py:67
  108.1 10.0 %all-to-all-start.3 = ((f32[8,4,512]{2,0,1:T(8,128)}), f32[8,4,512]{2,0,1:T(8,128)S(1)}, u32[]{:S(2)}, u32[]{:S(2)}) async-start(f32[8,4,512]{2,0,1:T(8,128)} %fusion.31), calls=%async_computation.3 | async-start | bytes 131072 | tf_op jit(solution)/shard_map/all_to_all | solution.py:229

commit v6 on v5

--- a/solution.py
+++ b/solution.py
@@ -112,11 +112,9 @@
         local_leaves, group, head_dim
     )
     queries = rotate(raw_query, positions[:, None]).astype(jnp.bfloat16)
-    everyone = gather_rows(queries.reshape(local_leaves, group * head_dim), "z")
+    everyone = gather_rows(queries.reshape(local_leaves, group * head_dim), ("y", "core"))
     node_rows = node_cache[0, 0]
-    slots = gather_rows(node_rows, ("y", "core")).reshape(
-        -1, node_rows.shape[0], node_rows.shape[1]
-    )
+    slots = gather_rows(node_rows, "z").reshape(-1, node_rows.shape[0], node_rows.shape[1])
     raw_entry = jnp.dot(normed, w_keyval, preferred_element_type=jnp.float32)
     new_entry = jnp.concatenate(
         [rotate(raw_entry[:, :head_dim], positions), raw_entry[:, head_dim:]], -1
@@ -139,16 +137,12 @@
 
     row_count = everyone.shape[0]
     slot_count = slots.shape[0]
-    z_size = lax.axis_size("z")
-    my_y_core = device % slot_count
-    first_slot = device - my_y_core
+    y_core_size = row_count // local_leaves
+    my_y_core = device % y_core_size
     row_branch = lax.dynamic_slice_in_dim(
-        leaf_branch.reshape(z_size, slot_count * local_leaves),
-        my_y_core * local_leaves,
-        local_leaves,
-        axis=1,
-    ).reshape(row_count)
-    slot_ids = first_slot + jnp.arange(slot_count, dtype=jnp.int32)
+        leaf_branch, (device - my_y_core) * local_leaves, row_count
+    )
+    slot_ids = my_y_core + y_core_size * jnp.arange(slot_count, dtype=jnp.int32)
     branch_root_hits = branch_root[:, None] == root_ids[None, :]
     root_slot_of_branch = jnp.any(
         branch_root_hits[:, None, :] & (root_owner[None, None, :] == slot_ids[None, :, None]), 2
@@ -195,7 +189,7 @@
     packet = jnp.concatenate(
         pieces + stats + [jnp.zeros((row_count, pad_width), jnp.bfloat16)], -1
     )
-    gathered = scatter_rows(packet, "z")
+    gathered = scatter_rows(packet, ("y", "core"))
     sums = []
     weights = []
     peaks = []

time: 119 us -> 177 us (1.49)
  the two profiles are of different devices: /device:TPU:32 before, /device:TPU:24 now
where the time goes in v6:
time: 177 us; the launch traced here: 175 us
  waiting for transfers between devices  97.6 us (55%)
  starting transfers between devices  29.6 us (17%)
  other arithmetic  19 us (11%)
  matrix products  17 us (10%)
  local copies, waits for them, and re-layouts  11 us (6%)
    all_to_all x2, waiting for transfers between devices, gather_rows(): received = lax.all_to_all(spread, axes, 0, 0, tiled=False)  92.6 us
    all_to_all x2, starting transfers between devices, gather_rows(): received = lax.all_to_all(spread, axes, 0, 0, tiled=False)  20 us
    reduce_sum x2, other arithmetic, soft_part(): weight_sum = jnp.sum(weights.astype(jnp.float32), -1)  9.51 us
    dot_general x2, matrix products, soft_part(): jnp.einsum(pattern, weights, value_rows, preferred_element_type=jnp.float32)  5.96 us
    dot_general x1, matrix products, local(): jnp.einsum('ngd,skd->nsgk', rows_query, slots[:, :, :head_dim], preferred...  5.5 us
    all_to_all x1, starting transfers between devices, scatter_rows(): received = lax.all_to_all(blocks, axes, 0, 0, tiled=False)  5.37 us
    all_to_all x1, waiting for transfers between devices, local(): lax.all_to_all(term.reshape(local_leaves, tensor_size, term.shape[1] // t...  4.97 us
    all_to_all x1, starting transfers between devices, local(): lax.all_to_all(term.reshape(local_leaves, tensor_size, term.shape[1] // t...  4.3 us
  transfers between devices with their start and end apart: 4, of which 3 were waited for; matrix products, arithmetic and copies ran while one was open for 6% of the time, Pallas kernels for 0%

profile of v6, /device:TPU:24, one launch (start us, length us, event | category | flops | bytes accessed | tf_op | source)
XLA Modules:
  0.0 175.3 jit_solution(16338950212005063904)
XLA Ops:
  0.6 0.0 copy-start
  0.8 1.0 fusion.15
  1.8 1.3 fusion.23
  3.1 1.2 fusion.25
  4.3 0.1 reshape.431
  4.4 0.1 slice_negate_fusion
  4.4 0.8 dynamic_slice.7
  5.2 0.9 select_reduce_fusion.5
  6.1 0.8 select_reduce_fusion.6
  6.9 0.7 add_convert_fusion.3
  7.6 0.1 slice_negate_fusion.1
  7.7 0.1 fusion.30
  7.8 0.1 maximum_multiply_fusion
  7.9 0.1 mul.178
  8.0 0.1 mul.174
  8.0 0.6 broadcast_in_dim.237
  8.7 8.9 %all-to-all-start = ((bf16[8,8,512]{2,1,0:T(8,128)(2,1)}), bf16[8,8,512]{2,1,0:T(8,128)(2,1)S(1)}, u32[]{:S(2)}, u32[]{:S(2)}) async-start(bf16[8,8,512]{2,1,0:T(8,128)(2,1)} %broadcast_in_dim.237), calls=%async_computation | async-start | bytes 131072 | tf_op jit(solution)/shard_map/all_to_all | solution.py:60
  17.5 1.0 copy.26
  18.5 2.5 %all-to-all-done = bf16[8,8,512]{2,1,0:T(8,128)(2,1)S(1)} async-done(((bf16[8,8,512]{2,1,0:T(8,128)(2,1)}), bf16[8,8,512]{2,1,0:T(8,128)(2,1)S(1)}, u32[]{:S(2)}, u32[]{:S(2)}) %all-to-all-start) | async-done | bytes 65568 | tf_op jit(solution)/shard_map/all_to_all | solution.py:60
  21.1 1.6 broadcast_in_dim.239
  22.6 11.1 %all-to-all-start.1 = ((bf16[16,512,128]{1,2,0:T(8,128)(2,1)}), bf16[16,512,128]{1,2,0:T(8,128)(2,1)}, u32[]{:S(2)}, u32[]{:S(2)}) async-start(bf16[16,512,128]{1,2,0:T(8,128)(2,1)} %broadcast_in_dim.239), calls=%async_computation.1 | async-start | bytes 4194304 | tf_op jit(solution)/shard_map/all_to_all | solution.py:60
  33.8 0.8 dynamic_slice.6
  34.5 0.1 broadcast_compare_fusion.1
  34.6 0.1 copy.24
  34.7 0.1 and_reduce_fusion.2
  34.8 0.1 broadcast_compare_fusion
  34.9 0.1 iota_compare_fusion.1
  35.0 2.3 %and_reduce_fusion = (pred[64,16]{1,0:T(8,128)(4,1)S(1)}, pred[64,16]{1,0:T(8,128)(4,1)S(1)}) fusion(pred[64,16]{0,1:T(8,128)(4,1)S(1)} %broadcast_compare_fusion, pred[64,64]{1,0:T(8,128)(4,1)S(1)} %iota_compare_fusion.1, pred[64,16]{0,1:T(8,128)(4,1)S(1)} %and_reduce_fusion.2), kind=kLoop, calls=%fused_computation.27 | loop fusion | flops 260096 | bytes 8192 | tf_op jit(solution)/shard_map/reduce_or | solution.py:153
  37.2 0.1 copy.25
  37.3 0.1 copy.28
  37.4 0.1 slice.138
  37.5 0.2 copy.29
  37.7 0.2 select_reduce_fusion.4
  37.9 0.1 select_reduce_fusion.8
  38.0 0.1 pad_maximum_fusion.1
  38.1 0.1 iota_compare_fusion.3
  38.1 0.1 iota_compare_fusion
  38.2 0.2 bitcast_select_fusion.2
  38.4 0.2 fusion.32
  38.6 0.3 broadcast_and_fusion
  39.0 0.1 reshape.441
  39.1 90.1 %all-to-all-done.1 = bf16[16,512,128]{1,2,0:T(8,128)(2,1)} async-done(((bf16[16,512,128]{1,2,0:T(8,128)(2,1)}), bf16[16,512,128]{1,2,0:T(8,128)(2,1)}, u32[]{:S(2)}, u32[]{:S(2)}) %all-to-all-start.1) | async-done | bytes 2097184 | tf_op jit(solution)/shard_map/all_to_all | solution.py:60
  129.2 5.5 %bitcast_reduce_fusion = (f32[64,16,8]{2,1,0:T(8,128)S(1)}, f32[64,8,16,512]{3,1,2,0:T(8,128)S(1)}) fusion(pred[64,16,512]{2,1,0:T(8,128)(4,1)S(1)} %broadcast_and_fusion, bf16[16,512,128]{1,2,0:T(8,128)(2,1)} %all-to-all-done.1, bf16[64,8,64,1]{2,1,0,3:T(8,128)(2,1)S(1)} %reshape.441), kind=kOutput, calls=%fused_computation.1 | convolution fusion | flops 549445632 | bytes 18448384 | tf_op jit(solution)/shard_map/ngd,skd->nsgk/dot_general | solution.py:163
  134.7 9.4 %convert_reduce_fusion = (f32[64,16,8]{2,1,0:T(8,128)S(1)}, bf16[64,16,8,512]{3,2,1,0:T(8,128)(2,1)}) fusion(f32[64,16,8]{2,1,0:T(8,128)S(1)} %get-tuple-element.39, f32[64,8,16,512]{3,1,2,0:T(8,128)S(1)} %get-tuple-element.40, pred[64,16,512]{2,1,0:T(8,128)(4,1)S(1)} %broadcast_and_fusion), kind=kLoop, calls=%fused_computation.5 | loop fusion | flops 29351936 | bytes 25755648 | tf_op jit(solution)/shard_map/reduce_sum | solution.py:25
  144.1 0.7 select_reduce_fusion.1
  144.8 5.7 %fusion.6 = (bf16[64,8,64]{2,1,0:T(8,128)(2,1)S(1)}, bf16[64,8,64]{2,1,0:T(8,128)(2,1)S(1)}) fusion(pred[64,16]{0,1:T(8,128)(4,1)S(1)} %copy.28, pred[64,16]{0,1:T(8,128)(4,1)S(1)} %copy.25, bf16[16,512,128]{1,2,0:T(8,128)(2,1)} %all-to-all-done.1, bf16[64,16,8,512]{3,2,1,0:T(8,128)(2,1)} %get-tuple-element.23), kind=kOutput, calls=%fused_computation.12 | convolution fusion | flops 538902528 | bytes 9570304 | tf_op jit(solution)/shard_map/nsgk,skd->nsgd/dot_general | solution.py:24
  150.6 0.1 convert_element_type.173
  150.7 0.1 convert_element_type.175
  150.9 0.8 concatenate.45
  151.7 5.4 %all-to-all-start.2 = ((bf16[8,8,1152]{2,1,0:T(8,128)(2,1)}), bf16[8,8,1152]{2,1,0:T(8,128)(2,1)S(1)}, u32[]{:S(2)}, u32[]{:S(2)}) async-start(bf16[8,8,1152]{2,1,0:T(8,128)(2,1)} %concatenate.45), calls=%async_computation.2 | async-start | bytes 294912 | tf_op jit(solution)/shard_map/all_to_all | solution.py:67
  157.0 0.1 slice_bitcast_fusion.4
  157.1 3.9 %copy.33 = bf16[2048,512]{1,0:T(8,128)(2,1)} copy(bf16[2048,512]{0,1:T(8,128)(2,1)} %bitcast.85) | data formatting | bytes 4194304 | tf_op jit(solution)/shard_map/dot_general | solution.py:221
  161.0 0.2 convert_reduce_fusion.1
  161.2 0.0 all-to-all-done.2
  161.3 0.1 multiply_add_fusion
  161.4 0.1 reshape.438
  161.4 0.1 reshape.440
  161.5 0.2 fusion.10
  161.8 0.1 reshape.444
  161.9 2.9 %fusion.33 = f32[8,4,512]{2,0,1:T(8,128)} fusion(bf16[8,512,1]{1,0,2:T(8,128)(2,1)S(1)} %reshape.444, bf16[4,512,512]{2,1,0:T(8,128)(2,1)} %bitcast.84), kind=kOutput, calls=%fused_computation.102 | convolution fusion | flops 16777216 | bytes 2170880 | tf_op jit(solution)/shard_map/dot_general | solution.py:221
  164.7 4.3 %all-to-all-start.3 = ((f32[8,4,512]{2,0,1:T(8,128)}), f32[8,4,512]{2,0,1:T(8,128)S(1)}, u32[]{:S(2)}, u32[]{:S(2)}) async-start(f32[8,4,512]{2,0,1:T(8,128)} %fusion.33), calls=%async_computation.3 | async-start | bytes 131072 | tf_op jit(solution)/shard_map/all_to_all | solution.py:223
  169.0 0.7 pad_maximum_fusion.2
  169.7 5.0 %all-to-all-done.3 = f32[8,4,512]{2,0,1:T(8,128)S(1)} async-done(((f32[8,4,512]{2,0,1:T(8,128)}), f32[8,4,512]{2,0,1:T(8,128)S(1)}, u32[]{:S(2)}, u32[]{:S(2)}) %all-to-all-start.3) | async-done | bytes 65568 | tf_op jit(solution)/shard_map/all_to_all | solution.py:223
  174.6 0.6 reduce_sum.174
  (32 shorter events, 0.2 us)
Async XLA Ops:
  0.6 2.5 %copy-start = (bf16[2048,512]{1,0:T(8,128)(2,1)S(1)}, bf16[2048,512]{1,0:T(8,128)(2,1)}, u32[]{:S(2)}) copy-start(bf16[2048,512]{1,0:T(8,128)(2,1)} %param.16) | copy-start | bytes 6291460
  0.6 34.0 %copy-start.6 = (s32[64]{0:T(128)S(1)}, s32[64]{0:T(128)}, u32[]{:S(2)}) copy-start(s32[64]{0:T(128)} %param.22) | copy-start | bytes 772
  0.7 37.0 %copy-start.2 = (s32[64]{0:T(128)S(1)}, s32[64]{0:T(128)}, u32[]{:S(2)}) copy-start(s32[64]{0:T(128)} %param.26) | copy-start | bytes 772
  0.7 37.2 %copy-start.7 = (s32[8]{0:T(128)S(1)}, s32[8]{0:T(128)}, u32[]{:S(2)}) copy-start(s32[8]{0:T(128)} %param.25) | copy-start | bytes 100
  0.7 37.4 %copy-start.3 = (s32[8]{0:T(128)S(1)}, s32[8]{0:T(128)}, u32[]{:S(2)}) copy-start(s32[8]{0:T(128)} %param.27) | copy-start | bytes 100
  0.7 33.8 %copy-start.5 = (s32[8]{0:T(128)S(1)}, s32[8]{0:T(128)}, u32[]{:S(2)}) copy-start(s32[8]{0:T(128)} %param.23) | copy-start | bytes 100
  0.7 34.1 %copy-start.4 = (s32[64]{0:T(128)S(1)}, s32[64]{0:T(128)}, u32[]{:S(2)}) copy-start(s32[64]{0:T(128)} %param.24) | copy-start | bytes 772
  0.7 36.8 %copy-start.1 = (bf16[8,1,128,128]{3,2,1,0:T(8,128)(2,1)S(1)}, bf16[8,1,128,128]{3,2,1,0:T(8,128)(2,1)}, u32[]{:S(2)}) copy-start(bf16[8,1,128,128]{3,2,1,0:T(8,128)(2,1)} %param.20) | copy-start | bytes 786436
  8.7 12.4 %all-to-all-start = ((bf16[8,8,512]{2,1,0:T(8,128)(2,1)}), bf16[8,8,512]{2,1,0:T(8,128)(2,1)S(1)}, u32[]{:S(2)}, u32[]{:S(2)}) async-start(bf16[8,8,512]{2,1,0:T(8,128)(2,1)} %broadcast_in_dim.237), calls=%async_computation | async-start | bytes 131072 | tf_op jit(solution)/shard_map/all_to_all | solution.py:60
  22.6 106.6 %all-to-all-start.1 = ((bf16[16,512,128]{1,2,0:T(8,128)(2,1)}), bf16[16,512,128]{1,2,0:T(8,128)(2,1)}, u32[]{:S(2)}, u32[]{:S(2)}) async-start(bf16[16,512,128]{1,2,0:T(8,128)(2,1)} %broadcast_in_dim.239), calls=%async_computation.1 | async-start | bytes 4194304 | tf_op jit(solution)/shard_map/all_to_all | solution.py:60
  151.7 9.6 %all-to-all-start.2 = ((bf16[8,8,1152]{2,1,0:T(8,128)(2,1)}), bf16[8,8,1152]{2,1,0:T(8,128)(2,1)S(1)}, u32[]{:S(2)}, u32[]{:S(2)}) async-start(bf16[8,8,1152]{2,1,0:T(8,128)(2,1)} %concatenate.45), calls=%async_computation.2 | async-start | bytes 294912 | tf_op jit(solution)/shard_map/all_to_all | solution.py:67
  164.7 9.9 %all-to-all-start.3 = ((f32[8,4,512]{2,0,1:T(8,128)}), f32[8,4,512]{2,0,1:T(8,128)S(1)}, u32[]{:S(2)}, u32[]{:S(2)}) async-start(f32[8,4,512]{2,0,1:T(8,128)} %fusion.33), calls=%async_computation.3 | async-start | bytes 131072 | tf_op jit(solution)/shard_map/all_to_all | solution.py:223

commit v7 on v5

--- a/solution.py
+++ b/solution.py
@@ -114,8 +114,17 @@
     queries = rotate(raw_query, positions[:, None]).astype(jnp.bfloat16)
     everyone = gather_rows(queries.reshape(local_leaves, group * head_dim), "z")
     node_rows = node_cache[0, 0]
-    slots = gather_rows(node_rows, ("y", "core")).reshape(
-        -1, node_rows.shape[0], node_rows.shape[1]
+    slot_count = lax.axis_size("y") * lax.axis_size("core")
+    slots = jnp.stack(
+        [node_rows]
+        + [
+            lax.ppermute(
+                node_rows,
+                ("y", "core"),
+                [(source, (source + shift) % slot_count) for source in range(slot_count)],
+            )
+            for shift in range(1, slot_count)
+        ]
     )
     raw_entry = jnp.dot(normed, w_keyval, preferred_element_type=jnp.float32)
     new_entry = jnp.concatenate(
@@ -138,7 +147,6 @@
     )
 
     row_count = everyone.shape[0]
-    slot_count = slots.shape[0]
     z_size = lax.axis_size("z")
     my_y_core = device % slot_count
     first_slot = device - my_y_core
@@ -148,7 +156,7 @@
         local_leaves,
         axis=1,
     ).reshape(row_count)
-    slot_ids = first_slot + jnp.arange(slot_count, dtype=jnp.int32)
+    slot_ids = first_slot + (my_y_core - jnp.arange(slot_count, dtype=jnp.int32)) % slot_count
     branch_root_hits = branch_root[:, None] == root_ids[None, :]
     root_slot_of_branch = jnp.any(
         branch_root_hits[:, None, :] & (root_owner[None, None, :] == slot_ids[None, :, None]), 2

time: 119 us -> 125 us (1.050)
  starting transfers between devices: 28.3 us -> 49.9 us
  waiting for transfers between devices: 44.2 us -> 23.7 us
  local copies, waits for them, and re-layouts: 13.7 us -> 21 us
  other arithmetic: 15.7 us -> 13 us
    all_to_all x2 -> x1, waiting for transfers between devices: 20.7 us -> 0.01 us  [gather_rows(): received = lax.all_to_all(spread, axes, 0, 0, tiled=False)]
    ppermute x0 -> x7, starting transfers between devices: none -> 18.4 us  [local(): lax.ppermute(node_rows, ('y', 'core'), [(source, (source + shift) % slot_...]
    unnamed x7 -> x13, local copies, waits for them, and re-layouts: 1.14 us -> 9.6 us
    all_to_all x1, starting transfers between devices: 4.31 us -> 12 us  [scatter_rows(): received = lax.all_to_all(blocks, axes, 0, 0, tiled=False)]
    all_to_all x2 -> x1, starting transfers between devices: 19.7 us -> 15.2 us  [gather_rows(): received = lax.all_to_all(spread, axes, 0, 0, tiled=False)]
    reduce_sum x2, other arithmetic: 7.8 us -> 4.24 us  [soft_part(): weight_sum = jnp.sum(weights.astype(jnp.float32), -1)]
    broadcast_in_dim x3 -> x1, local copies, waits for them, and re-layouts: 2.74 us -> 0.67 us  [gather_rows(): spread = jnp.broadcast_to(values[None], (count,) + values.shape)]
  transfers between devices with their start and end apart: 4 -> 10, of which waited for: 4 -> 2; matrix products, arithmetic and copies ran while one was open for 9% -> 22% of each run, Pallas kernels for 0% -> 0%
where the time goes in v7:
time: 125 us; the launch traced here: 124 us
  starting transfers between devices  49.9 us (40%)
  waiting for transfers between devices  23.7 us (19%)
  local copies, waits for them, and re-layouts  21 us (17%)
  matrix products  14.8 us (12%)
  other arithmetic  13 us (10%)
    all_to_all x1, waiting for transfers between devices, scatter_rows(): received = lax.all_to_all(blocks, axes, 0, 0, tiled=False)  18.7 us
    ppermute x7, starting transfers between devices, local(): lax.ppermute(node_rows, ('y', 'core'), [(source, (source + shift) % slot_...  18.4 us
    all_to_all x1, starting transfers between devices, gather_rows(): received = lax.all_to_all(spread, axes, 0, 0, tiled=False)  15.2 us
    all_to_all x1, starting transfers between devices, scatter_rows(): received = lax.all_to_all(blocks, axes, 0, 0, tiled=False)  12 us
    unnamed x13, local copies, waits for them, and re-layouts  9.6 us
    dot_general x2, matrix products, soft_part(): jnp.einsum(pattern, weights, value_rows, preferred_element_type=jnp.float32)  5.63 us
    all_to_all x1, waiting for transfers between devices, local(): lax.all_to_all(term.reshape(local_leaves, tensor_size, term.shape[1] // t...  4.97 us
    all_to_all x1, starting transfers between devices, local(): lax.all_to_all(term.reshape(local_leaves, tensor_size, term.shape[1] // t...  4.29 us
  transfers between devices with their start and end apart: 10, of which 2 were waited for; matrix products, arithmetic and copies ran while one was open for 22% of the time, Pallas kernels for 0%

profile of v7, /device:TPU:32, one launch (start us, length us, event | category | flops | bytes accessed | tf_op | source)
XLA Modules:
  0.0 123.5 jit_solution(8875012673476791011)
XLA Ops:
  0.6 1.2 copy.78
  1.8 3.5 %collective-permute-start.1 = (bf16[512,128]{0,1:T(8,128)(2,1)S(1)}, bf16[512,128]{0,1:T(8,128)(2,1)}, u32[]{:S(2)}, u32[]{:S(2)}) collective-permute-start(bf16[512,128]{0,1:T(8,128)(2,1)S(1)} %bitcast.76), channel_id=1, source_target_pairs={{0,2},{1,3},{2,4},{3,5},{4,6},{5,7},{6,0},{7,1},{8,10},{9,11},{10,... | collective-permute-start | bytes 393224 | tf_op jit(solution)/shard_map/ppermute | solution.py:121
  5.3 4.2 %collective-permute-start.2 = (bf16[512,128]{0,1:T(8,128)(2,1)S(1)}, bf16[512,128]{0,1:T(8,128)(2,1)}, u32[]{:S(2)}, u32[]{:S(2)}) collective-permute-start(bf16[512,128]{0,1:T(8,128)(2,1)S(1)} %bitcast.77), channel_id=1, source_target_pairs={{0,3},{1,4},{2,5},{3,6},{4,7},{5,0},{6,1},{7,2},{8,11},{9,12},{10,... | collective-permute-start | bytes 393224 | tf_op jit(solution)/shard_map/ppermute | solution.py:121
  9.5 3.7 %collective-permute-start.3 = (bf16[512,128]{0,1:T(8,128)(2,1)S(1)}, bf16[512,128]{0,1:T(8,128)(2,1)S(1)}, u32[]{:S(2)}, u32[]{:S(2)}) collective-permute-start(bf16[512,128]{0,1:T(8,128)(2,1)S(1)} %bitcast.78), channel_id=1, source_target_pairs={{0,4},{1,5},{2,6},{3,7},{4,0},{5,1},{6,2},{7,3},{8,12},{9,13},{10,... | collective-permute-start | bytes 393224 | tf_op jit(solution)/shard_map/ppermute | solution.py:121
  13.3 3.7 %collective-permute-start.4 = (bf16[512,128]{0,1:T(8,128)(2,1)S(1)}, bf16[512,128]{0,1:T(8,128)(2,1)S(1)}, u32[]{:S(2)}, u32[]{:S(2)}) collective-permute-start(bf16[512,128]{0,1:T(8,128)(2,1)S(1)} %bitcast.79), channel_id=1, source_target_pairs={{0,5},{1,6},{2,7},{3,0},{4,1},{5,2},{6,3},{7,4},{8,13},{9,14},{10,... | collective-permute-start | bytes 393224 | tf_op jit(solution)/shard_map/ppermute | solution.py:121
  17.0 0.9 fusion.12
  17.9 1.3 %fusion.18 = f32[8,128]{1,0:T(8,128)S(1)} fusion(bf16[2048,128]{1,0:T(8,128)(2,1)} %param.17, bf16[8,2048]{1,0:T(8,128)(2,1)} %param.14, f32[2048]{0:T(1024)} %param.15, f32[8]{0:T(128)S(1)} %add_rsqrt_fusion), kind=kOutput, calls=%fused_computation.63 | convolution fusion | flops 4259840 | bytes 569376 | tf_op jit(solution)/shard_map/dot_general | solution.py:129
  19.2 1.2 fusion.20
  20.6 0.8 dynamic_slice.7
  21.3 0.9 select_reduce_fusion.7
  22.2 0.9 select_reduce_fusion.8
  23.1 0.7 add_convert_fusion.3
  23.9 0.1 fusion.25
  24.2 0.7 broadcast_in_dim.206
  24.9 15.2 %all-to-all-start = ((bf16[16,8,512]{2,1,0:T(8,128)(2,1)}), bf16[16,8,512]{2,1,0:T(8,128)(2,1)S(1)}, u32[]{:S(2)}, u32[]{:S(2)}) async-start(bf16[16,8,512]{2,1,0:T(8,128)(2,1)} %broadcast_in_dim.206), calls=%async_computation | async-start | bytes 262144 | tf_op jit(solution)/shard_map/all_to_all | solution.py:60
  40.2 0.7 broadcast_compare_fusion
  40.9 0.8 reshape.469
  41.7 0.7 broadcast_compare_fusion.1
  42.4 0.7 iota_compare_fusion.6
  43.1 1.1 copy.102
  44.5 0.1 copy.77
  44.7 3.9 %copy.107 = bf16[2048,512]{1,0:T(8,128)(2,1)} copy(bf16[2048,512]{0,1:T(8,128)(2,1)} %bitcast.74) | data formatting | bytes 4194304 | tf_op jit(solution)/shard_map/dot_general | solution.py:235
  48.6 0.2 and_reduce_fusion
  48.8 0.7 broadcast_and_fusion
  49.6 0.7 bitcast_dynamic-update-slice_fusion.7
  50.2 3.2 %collective-permute-start.5 = (bf16[512,128]{0,1:T(8,128)(2,1)S(1)}, bf16[512,128]{0,1:T(8,128)(2,1)S(1)}, u32[]{:S(2)}, u32[]{:S(2)}) collective-permute-start(bf16[512,128]{0,1:T(8,128)(2,1)S(1)} %bitcast.80), channel_id=1, source_target_pairs={{0,6},{1,7},{2,0},{3,1},{4,2},{5,3},{6,4},{7,5},{8,14},{9,15},{10,... | collective-permute-start | bytes 393224 | tf_op jit(solution)/shard_map/ppermute | solution.py:121
  53.5 1.6 %bitcast_dynamic-update-slice_fusion.6 = bf16[8,512,128]{1,2,0:T(8,128)(2,1)} fusion(bf16[8,512,128]{1,2,0:T(8,128)(2,1)} %bitcast_dynamic-update-slice_fusion.7, bf16[512,128]{0,1:T(8,128)(2,1)} %collective-permute-done), kind=kLoop, calls=%fused_computation.31 | loop fusion | bytes 262144
  55.0 1.6 %bitcast_dynamic-update-slice_fusion.5 = bf16[8,512,128]{1,2,0:T(8,128)(2,1)} fusion(bf16[8,512,128]{1,2,0:T(8,128)(2,1)} %bitcast_dynamic-update-slice_fusion.6, bf16[512,128]{0,1:T(8,128)(2,1)} %collective-permute-done.1), kind=kLoop, calls=%fused_computation.30 | loop fusion | bytes 262144
  56.6 1.6 %bitcast_dynamic-update-slice_fusion.4 = bf16[8,512,128]{1,2,0:T(8,128)(2,1)} fusion(bf16[8,512,128]{1,2,0:T(8,128)(2,1)} %bitcast_dynamic-update-slice_fusion.5, bf16[512,128]{0,1:T(8,128)(2,1)} %collective-permute-done.2), kind=kLoop, calls=%fused_computation.29 | loop fusion | bytes 262144
  58.2 0.6 bitcast_dynamic-update-slice_fusion.3
  58.8 0.7 bitcast_dynamic-update-slice_fusion.2
  59.5 0.7 bitcast_dynamic-update-slice_fusion.1
  60.1 0.7 bitcast_dynamic-update-slice_fusion
  60.8 0.2 reshape_reshape.3
  61.0 0.2 copy.80
  61.2 3.6 %fusion = (f32[128,8,8]{0,2,1:T(8,128)S(1)}, f32[8,512,128,8]{2,1,3,0:T(8,128)S(1)}) fusion(pred[128,8,512]{0,2,1:T(8,128)(4,1)S(1)} %broadcast_and_fusion, bf16[128,8,64]{0,2,1:T(8,128)(2,1)S(1)} %copy.80, bf16[8,512,128]{1,2,0:T(8,128)(2,1)} %bitcast_dynamic-update-slice_fusion), kind=kOutput, calls=%fused_computation.3 | convolution fusion | flops 549445632 | bytes 17989632 | tf_op jit(solution)/shard_map/ngd,skd->nsgk/dot_general | solution.py:177
  64.8 5.4 %fusion.2 = (bf16[128,8,64]{0,2,1:T(8,128)(2,1)S(1)}, bf16[128,8,64]{0,2,1:T(8,128)(2,1)S(1)}) fusion(pred[128,8]{0,1:T(8,128)(4,1)S(1)} %get-tuple-element.8, pred[128,8]{0,1:T(8,128)(4,1)S(1)} %get-tuple-element.9, f32[8,512,128,8]{2,1,3,0:T(8,128)S(1)} %get-tuple-element.43, f32[128,8,8]{0,2,1:T(8,128)S(1)} %get-tuple-element.42, ...), kind=kOutput, calls=%fused_computation.7 | convolution fusion | flops 559808512 | bytes 18122752 | tf_op jit(solution)/shard_map/nsgk,skd->nsgd/dot_general | solution.py:24
  70.2 4.1 %convert_reduce_fusion = f32[128,8,8]{0,2,1:T(8,128)S(1)} fusion(f32[128,8,8]{0,2,1:T(8,128)S(1)} %get-tuple-element.42, f32[8,512,128,8]{2,1,3,0:T(8,128)S(1)} %get-tuple-element.43, pred[128,8,512]{0,2,1:T(8,128)(4,1)S(1)} %broadcast_and_fusion), kind=kLoop, calls=%fused_computation.1 | loop fusion | flops 29351936 | bytes 17367040 | tf_op jit(solution)/shard_map/reduce_sum | solution.py:25
  74.3 0.2 copy.82
  74.5 0.2 convert_element_type.173
  74.7 0.2 copy.83
  74.9 0.2 convert_element_type.175
  75.4 0.1 copy.92
  75.5 0.1 copy.93
  75.8 0.1 copy.94
  75.9 0.1 copy.95
  76.0 0.1 copy.96
  76.3 0.1 copy.97
  76.4 0.1 copy.98
  76.7 0.1 copy.99
  76.8 0.1 copy.100
  76.9 0.1 copy.101
  77.0 0.9 concatenate.45
  77.9 12.0 %all-to-all-start.1 = ((bf16[16,8,1152]{2,1,0:T(8,128)(2,1)}), bf16[16,8,1152]{2,1,0:T(8,128)(2,1)S(1)}, u32[]{:S(2)}, u32[]{:S(2)}) async-start(bf16[16,8,1152]{2,1,0:T(8,128)(2,1)} %concatenate.45), calls=%async_computation.1 | async-start | bytes 589824 | tf_op jit(solution)/shard_map/all_to_all | solution.py:67
  90.1 0.2 bitcast_select_fusion.3
  90.3 0.2 fusion.28
  90.5 0.2 convert_reduce_fusion.1
  90.7 18.7 %all-to-all-done.1 = bf16[16,8,1152]{2,1,0:T(8,128)(2,1)S(1)} async-done(((bf16[16,8,1152]{2,1,0:T(8,128)(2,1)}), bf16[16,8,1152]{2,1,0:T(8,128)(2,1)S(1)}, u32[]{:S(2)}, u32[]{:S(2)}) %all-to-all-start.1) | async-done | bytes 294944 | tf_op jit(solution)/shard_map/all_to_all | solution.py:67
  109.8 0.2 fusion.6
  110.1 2.9 %fusion.29 = f32[8,4,512]{2,0,1:T(8,128)} fusion(bf16[8,512,1]{1,0,2:T(8,128)(2,1)S(1)} %reshape.483, bf16[4,512,512]{2,1,0:T(8,128)(2,1)} %bitcast.73), kind=kOutput, calls=%fused_computation.105 | convolution fusion | flops 16777216 | bytes 2170880 | tf_op jit(solution)/shard_map/dot_general | solution.py:235
  113.0 4.3 %all-to-all-start.2 = ((f32[8,4,512]{2,0,1:T(8,128)}), f32[8,4,512]{2,0,1:T(8,128)S(1)}, u32[]{:S(2)}, u32[]{:S(2)}) async-start(f32[8,4,512]{2,0,1:T(8,128)} %fusion.29), calls=%async_computation.2 | async-start | bytes 131072 | tf_op jit(solution)/shard_map/all_to_all | solution.py:237
  117.3 0.7 pad_maximum_fusion.2
  117.9 5.0 %all-to-all-done.2 = f32[8,4,512]{2,0,1:T(8,128)S(1)} async-done(((f32[8,4,512]{2,0,1:T(8,128)}), f32[8,4,512]{2,0,1:T(8,128)S(1)}, u32[]{:S(2)}, u32[]{:S(2)}) %all-to-all-start.2) | async-done | bytes 65568 | tf_op jit(solution)/shard_map/all_to_all | solution.py:237
  122.9 0.6 reduce_sum.174
  (56 shorter events, 2.3 us)
Async XLA Ops:
  0.6 18.6 %copy-start = (bf16[2048,512]{1,0:T(8,128)(2,1)S(1)}, bf16[2048,512]{1,0:T(8,128)(2,1)}, u32[]{:S(2)}) copy-start(bf16[2048,512]{1,0:T(8,128)(2,1)} %param.16) | copy-start | bytes 6291460
  1.8 48.4 %collective-permute-start = (bf16[512,128]{0,1:T(8,128)(2,1)S(1)}, bf16[512,128]{0,1:T(8,128)(2,1)}, u32[]{:S(2)}, u32[]{:S(2)}) collective-permute-start(bf16[512,128]{0,1:T(8,128)(2,1)S(1)} %bitcast.75), channel_id=1, source_target_pairs={{0,1},{1,2},{2,3},{3,4},{4,5},{5,6},{6,7},{7,0},{8,9},{9,10},{10,1... | collective-permute-start | bytes 393224 | tf_op jit(solution)/shard_map/ppermute | solution.py:121
  1.8 53.2 %collective-permute-start.1 = (bf16[512,128]{0,1:T(8,128)(2,1)S(1)}, bf16[512,128]{0,1:T(8,128)(2,1)}, u32[]{:S(2)}, u32[]{:S(2)}) collective-permute-start(bf16[512,128]{0,1:T(8,128)(2,1)S(1)} %bitcast.76), channel_id=1, source_target_pairs={{0,2},{1,3},{2,4},{3,5},{4,6},{5,7},{6,0},{7,1},{8,10},{9,11},{10,... | collective-permute-start | bytes 393224 | tf_op jit(solution)/shard_map/ppermute | solution.py:121
  5.3 51.3 %collective-permute-start.2 = (bf16[512,128]{0,1:T(8,128)(2,1)S(1)}, bf16[512,128]{0,1:T(8,128)(2,1)}, u32[]{:S(2)}, u32[]{:S(2)}) collective-permute-start(bf16[512,128]{0,1:T(8,128)(2,1)S(1)} %bitcast.77), channel_id=1, source_target_pairs={{0,3},{1,4},{2,5},{3,6},{4,7},{5,0},{6,1},{7,2},{8,11},{9,12},{10,... | collective-permute-start | bytes 393224 | tf_op jit(solution)/shard_map/ppermute | solution.py:121
  9.5 48.6 %collective-permute-start.3 = (bf16[512,128]{0,1:T(8,128)(2,1)S(1)}, bf16[512,128]{0,1:T(8,128)(2,1)S(1)}, u32[]{:S(2)}, u32[]{:S(2)}) collective-permute-start(bf16[512,128]{0,1:T(8,128)(2,1)S(1)} %bitcast.78), channel_id=1, source_target_pairs={{0,4},{1,5},{2,6},{3,7},{4,0},{5,1},{6,2},{7,3},{8,12},{9,13},{10,... | collective-permute-start | bytes 393224 | tf_op jit(solution)/shard_map/ppermute | solution.py:121
  13.3 45.5 %collective-permute-start.4 = (bf16[512,128]{0,1:T(8,128)(2,1)S(1)}, bf16[512,128]{0,1:T(8,128)(2,1)S(1)}, u32[]{:S(2)}, u32[]{:S(2)}) collective-permute-start(bf16[512,128]{0,1:T(8,128)(2,1)S(1)} %bitcast.79), channel_id=1, source_target_pairs={{0,5},{1,6},{2,7},{3,0},{4,1},{5,2},{6,3},{7,4},{8,13},{9,14},{10,... | collective-permute-start | bytes 393224 | tf_op jit(solution)/shard_map/ppermute | solution.py:121
  24.9 35.9 %all-to-all-start = ((bf16[16,8,512]{2,1,0:T(8,128)(2,1)}), bf16[16,8,512]{2,1,0:T(8,128)(2,1)S(1)}, u32[]{:S(2)}, u32[]{:S(2)}) async-start(bf16[16,8,512]{2,1,0:T(8,128)(2,1)} %broadcast_in_dim.206), calls=%async_computation | async-start | bytes 262144 | tf_op jit(solution)/shard_map/all_to_all | solution.py:60
  50.2 9.3 %collective-permute-start.5 = (bf16[512,128]{0,1:T(8,128)(2,1)S(1)}, bf16[512,128]{0,1:T(8,128)(2,1)S(1)}, u32[]{:S(2)}, u32[]{:S(2)}) collective-permute-start(bf16[512,128]{0,1:T(8,128)(2,1)S(1)} %bitcast.80), channel_id=1, source_target_pairs={{0,6},{1,7},{2,0},{3,1},{4,2},{5,3},{6,4},{7,5},{8,14},{9,15},{10,... | collective-permute-start | bytes 393224 | tf_op jit(solution)/shard_map/ppermute | solution.py:121
  55.0 5.1 %collective-permute-start.6 = (bf16[512,128]{0,1:T(8,128)(2,1)S(1)}, bf16[512,128]{0,1:T(8,128)(2,1)S(1)}, u32[]{:S(2)}, u32[]{:S(2)}) collective-permute-start(bf16[512,128]{0,1:T(8,128)(2,1)S(1)} %bitcast.81), channel_id=1, source_target_pairs={{0,7},{1,0},{2,1},{3,2},{4,3},{5,4},{6,5},{7,6},{8,15},{9,8},{10,9... | collective-permute-start | bytes 393224 | tf_op jit(solution)/shard_map/ppermute | solution.py:121
  70.2 19.8 %copy-start.1 = (s32[8]{0:T(128)S(1)}, s32[8]{0:T(128)}, u32[]{:S(2)}) copy-start(s32[8]{0:T(128)} %param.27) | copy-start | bytes 100
  77.9 31.6 %all-to-all-start.1 = ((bf16[16,8,1152]{2,1,0:T(8,128)(2,1)}), bf16[16,8,1152]{2,1,0:T(8,128)(2,1)S(1)}, u32[]{:S(2)}, u32[]{:S(2)}) async-start(bf16[16,8,1152]{2,1,0:T(8,128)(2,1)} %concatenate.45), calls=%async_computation.1 | async-start | bytes 589824 | tf_op jit(solution)/shard_map/all_to_all | solution.py:67
  113.0 9.9 %all-to-all-start.2 = ((f32[8,4,512]{2,0,1:T(8,128)}), f32[8,4,512]{2,0,1:T(8,128)S(1)}, u32[]{:S(2)}, u32[]{:S(2)}) async-start(f32[8,4,512]{2,0,1:T(8,128)} %fusion.29), calls=%async_computation.2 | async-start | bytes 131072 | tf_op jit(solution)/shard_map/all_to_all | solution.py:237

commit v8 on v5

--- a/solution.py
+++ b/solution.py
@@ -112,11 +112,12 @@
         local_leaves, group, head_dim
     )
     queries = rotate(raw_query, positions[:, None]).astype(jnp.bfloat16)
-    everyone = gather_rows(queries.reshape(local_leaves, group * head_dim), "z")
     node_rows = node_cache[0, 0]
     slots = gather_rows(node_rows, ("y", "core")).reshape(
         -1, node_rows.shape[0], node_rows.shape[1]
     )
+    queries, slots = lax.optimization_barrier((queries, slots))
+    everyone = gather_rows(queries.reshape(local_leaves, group * head_dim), "z")
     raw_entry = jnp.dot(normed, w_keyval, preferred_element_type=jnp.float32)
     new_entry = jnp.concatenate(
         [rotate(raw_entry[:, :head_dim], positions), raw_entry[:, head_dim:]], -1

time: 119 us -> 110 us (0.924)
  the two profiles are of different devices: /device:TPU:32 before, /device:TPU:64 now
where the time goes in v8:
time: 110 us; the launch traced here: 109 us
  starting transfers between devices  31.5 us (29%)
  waiting for transfers between devices  31.3 us (28%)
  other arithmetic  16.5 us (15%)
  local copies, waits for them, and re-layouts  15.3 us (14%)
  matrix products  13.9 us (13%)
    all_to_all x2, starting transfers between devices, gather_rows(): received = lax.all_to_all(spread, axes, 0, 0, tiled=False)  19.2 us
    all_to_all x1, waiting for transfers between devices, scatter_rows(): received = lax.all_to_all(blocks, axes, 0, 0, tiled=False)  18.2 us
    all_to_all x2, waiting for transfers between devices, gather_rows(): received = lax.all_to_all(spread, axes, 0, 0, tiled=False)  8.08 us
    all_to_all x1, starting transfers between devices, scatter_rows(): received = lax.all_to_all(blocks, axes, 0, 0, tiled=False)  8 us
    all_to_all x1, waiting for transfers between devices, local(): lax.all_to_all(term.reshape(local_leaves, tensor_size, term.shape[1] // t...  4.97 us
    dot_general x2, matrix products, soft_part(): jnp.einsum(pattern, weights, value_rows, preferred_element_type=jnp.float32)  4.64 us
    all_to_all x1, starting transfers between devices, local(): lax.all_to_all(term.reshape(local_leaves, tensor_size, term.shape[1] // t...  4.27 us
    reduce_sum x2, other arithmetic, soft_part(): weight_sum = jnp.sum(weights.astype(jnp.float32), -1)  4.24 us
  transfers between devices with their start and end apart: 4, of which 4 were waited for; matrix products, arithmetic and copies ran while one was open for 20% of the time, Pallas kernels for 0%

profile of v8, /device:TPU:64, one launch (start us, length us, event | category | flops | bytes accessed | tf_op | source)
XLA Modules:
  0.0 109.4 jit_solution(5450262537313780796)
XLA Ops:
  0.6 1.2 %copy.73 = bf16[512,128]{0,1:T(8,128)(2,1)S(1)} copy(bf16[512,128]{1,0:T(8,128)(2,1)} %bitcast.60) | data formatting | bytes 262144 | tf_op jit(solution)/shard_map/broadcast_in_dim | solution.py:59
  1.8 1.1 broadcast_in_dim.215
  2.9 4.5 %all-to-all-start = ((bf16[8,512,128]{1,2,0:T(8,128)(2,1)}), bf16[8,512,128]{1,2,0:T(8,128)(2,1)S(1)}, u32[]{:S(2)}, u32[]{:S(2)}) async-start(bf16[8,512,128]{1,2,0:T(8,128)(2,1)} %broadcast_in_dim.215), calls=%async_computation | async-start | bytes 2097152 | tf_op jit(solution)/shard_map/all_to_all | solution.py:60
  7.4 0.9 fusion.16
  8.3 0.8 reshape.418
  9.0 0.8 dynamic_slice.7
  9.9 0.1 eq.132
  10.0 0.7 broadcast_compare_fusion
  10.7 0.7 broadcast_compare_fusion.1
  11.4 0.7 iota_compare_fusion.6
  12.1 1.3 %fusion.23 = f32[8,128]{1,0:T(8,128)S(1)} fusion(bf16[2048,128]{1,0:T(8,128)(2,1)} %param.17, bf16[8,2048]{1,0:T(8,128)(2,1)} %param.14, f32[2048]{0:T(1024)} %param.15, f32[8]{0:T(128)S(1)} %add_rsqrt_fusion), kind=kOutput, calls=%fused_computation.56 | convolution fusion | flops 4259840 | bytes 569376 | tf_op jit(solution)/shard_map/dot_general | solution.py:121
  13.4 1.2 %fusion.25 = f32[8,512]{1,0:T(8,128)S(1)} fusion(bf16[2048,512]{1,0:T(8,128)(2,1)S(1)} %copy-done, bf16[8,2048]{1,0:T(8,128)(2,1)} %param.14, f32[2048]{0:T(1024)} %param.15, f32[8]{0:T(128)S(1)} %add_rsqrt_fusion), kind=kOutput, calls=%fused_computation.57 | convolution fusion | flops 16842752 | bytes 2154528 | tf_op jit(solution)/shard_map/dot_general | solution.py:111
  14.6 1.4 %select_reduce_fusion.4 = (s32[8]{0:T(128)}, s32[8]{0:T(128)S(1)}, s32[8]{0:T(128)S(1)}) fusion(s32[64]{0:T(128)} %param.24, s32[64]{0:T(128)} %param.26, s32[8]{0:T(128)S(1)} %iota_add_fusion, s32[8]{0:T(128)S(1)} %dynamic_slice.7, s32[64]{0:T(128)} %param.22), kind=kLoop, calls=%fused_computation.73 | loop fusion | flops 4072 | bytes 928 | tf_op jit(solution)/shard_map/reduce_sum | solution.py:164
  16.0 1.4 %select_reduce_fusion.5 = (s32[8]{0:T(128)}, s32[8]{0:T(128)S(1)}) fusion(s32[8]{0:T(128)} %param.25, s32[8]{0:T(128)S(1)} %iota_add_fusion, s32[8]{0:T(128)} %param.23, s32[8]{0:T(128)S(1)} %get-tuple-element.18), kind=kLoop, calls=%fused_computation.74 | loop fusion | flops 368 | bytes 192 | tf_op jit(solution)/shard_map/reduce_sum | solution.py:162
  17.4 0.1 and_reduce_fusion.2
  17.5 0.7 add_convert_fusion
  18.2 0.1 copy.72
  18.4 0.7 fusion.30
  19.2 0.1 fusion.20
  19.3 4.0 %all-to-all-done = bf16[8,512,128]{1,2,0:T(8,128)(2,1)S(1)} async-done(((bf16[8,512,128]{1,2,0:T(8,128)(2,1)}), bf16[8,512,128]{1,2,0:T(8,128)(2,1)S(1)}, u32[]{:S(2)}, u32[]{:S(2)}) %all-to-all-start) | async-done | bytes 1048608 | tf_op jit(solution)/shard_map/all_to_all | solution.py:60
  23.3 0.1 broadcast_in_dim.217
  23.4 0.8 broadcast_in_dim.218
  24.2 14.8 %all-to-all-start.1 = ((bf16[16,8,512]{2,1,0:T(8,128)(2,1)}), bf16[16,8,512]{2,1,0:T(8,128)(2,1)S(1)}, u32[]{:S(2)}, u32[]{:S(2)}) async-start(bf16[16,8,512]{2,1,0:T(8,128)(2,1)} %broadcast_in_dim.218), calls=%async_computation.1 | async-start | bytes 262144 | tf_op jit(solution)/shard_map/all_to_all | solution.py:60
  38.9 0.8 and_reduce_fusion
  39.7 0.6 slice.140
  40.4 1.1 %copy.96 = bf16[8,1,128,128]{2,3,0,1:T(8,128)(2,1)S(1)} copy(bf16[8,1,128,128]{3,2,1,0:T(8,128)(2,1)} %param.20) | data formatting | bytes 524288 | tf_op args[6]
  41.5 3.9 %copy.101 = bf16[2048,512]{1,0:T(8,128)(2,1)} copy(bf16[2048,512]{0,1:T(8,128)(2,1)} %bitcast.59) | data formatting | bytes 4194304 | tf_op jit(solution)/shard_map/dot_general | solution.py:228
  45.4 0.7 add.102
  46.1 0.7 or.11
  46.8 0.5 copy-done.6
  47.3 0.7 broadcast_and_fusion
  48.0 4.0 %all-to-all-done.1 = bf16[16,8,512]{2,1,0:T(8,128)(2,1)S(1)} async-done(((bf16[16,8,512]{2,1,0:T(8,128)(2,1)}), bf16[16,8,512]{2,1,0:T(8,128)(2,1)S(1)}, u32[]{:S(2)}, u32[]{:S(2)}) %all-to-all-start.1) | async-done | bytes 131104 | tf_op jit(solution)/shard_map/all_to_all | solution.py:60
  52.1 0.2 reshape_reshape.3
  52.3 0.2 copy.74
  52.5 3.7 %fusion = (f32[128,8,8]{0,2,1:T(8,128)S(1)}, f32[8,512,128,8]{2,1,3,0:T(8,128)S(1)}) fusion(pred[128,8,512]{0,2,1:T(8,128)(4,1)S(1)} %broadcast_and_fusion, bf16[128,8,64]{0,2,1:T(8,128)(2,1)S(1)} %copy.74, bf16[8,512,128]{1,2,0:T(8,128)(2,1)} %copy-done.1), kind=kOutput, calls=%fused_computation.3 | convolution fusion | flops 549445632 | bytes 17989632 | tf_op jit(solution)/shard_map/ngd,skd->nsgk/dot_general | solution.py:170
  56.2 4.4 %fusion.2 = (bf16[128,8,64]{0,2,1:T(8,128)(2,1)S(1)}, bf16[128,8,64]{0,2,1:T(8,128)(2,1)S(1)}) fusion(pred[128,8]{0,1:T(8,128)(4,1)S(1)} %copy-done.8, pred[128,8]{0,1:T(8,128)(4,1)S(1)} %copy-done.9, f32[8,512,128,8]{2,1,3,0:T(8,128)S(1)} %get-tuple-element.47, f32[128,8,8]{0,2,1:T(8,128)S(1)} %get-tuple-element.46, ...), kind=kOutput, calls=%fused_computation.7 | convolution fusion | flops 559808512 | bytes 18122752 | tf_op jit(solution)/shard_map/nsgk,skd->nsgd/dot_general | solution.py:24
  60.7 4.1 %convert_reduce_fusion = f32[128,8,8]{0,2,1:T(8,128)S(1)} fusion(f32[128,8,8]{0,2,1:T(8,128)S(1)} %get-tuple-element.46, f32[8,512,128,8]{2,1,3,0:T(8,128)S(1)} %get-tuple-element.47, pred[128,8,512]{0,2,1:T(8,128)(4,1)S(1)} %broadcast_and_fusion), kind=kLoop, calls=%fused_computation.1 | loop fusion | flops 29351936 | bytes 17367040 | tf_op jit(solution)/shard_map/reduce_sum | solution.py:25
  64.8 0.2 copy.76
  65.0 0.2 convert_element_type.169
  65.2 0.2 copy.77
  65.4 0.2 convert_element_type.171
  65.8 0.1 copy.86
  65.9 0.1 copy.87
  66.2 0.1 copy.88
  66.3 0.1 copy.89
  66.4 0.1 copy.90
  66.7 0.1 copy.91
  66.8 0.1 copy.92
  67.1 0.1 copy.93
  67.2 0.1 copy.94
  67.3 0.1 copy.95
  67.4 0.9 concatenate.45
  68.3 8.0 %all-to-all-start.2 = ((bf16[16,8,1152]{2,1,0:T(8,128)(2,1)}), bf16[16,8,1152]{2,1,0:T(8,128)(2,1)S(1)}, u32[]{:S(2)}, u32[]{:S(2)}) async-start(bf16[16,8,1152]{2,1,0:T(8,128)(2,1)} %concatenate.45), calls=%async_computation.2 | async-start | bytes 589824 | tf_op jit(solution)/shard_map/all_to_all | solution.py:67
  76.6 0.2 bitcast_select_fusion.3
  76.8 0.2 fusion.31
  77.0 0.2 convert_reduce_fusion.1
  77.2 18.2 %all-to-all-done.2 = bf16[16,8,1152]{2,1,0:T(8,128)(2,1)S(1)} async-done(((bf16[16,8,1152]{2,1,0:T(8,128)(2,1)}), bf16[16,8,1152]{2,1,0:T(8,128)(2,1)S(1)}, u32[]{:S(2)}, u32[]{:S(2)}) %all-to-all-start.2) | async-done | bytes 294944 | tf_op jit(solution)/shard_map/all_to_all | solution.py:67
  95.7 0.2 fusion.6
  96.0 0.1 reshape.432
  96.0 2.9 %fusion.32 = f32[8,4,512]{2,0,1:T(8,128)} fusion(bf16[8,512,1]{1,0,2:T(8,128)(2,1)S(1)} %reshape.432, bf16[4,512,512]{2,1,0:T(8,128)(2,1)} %bitcast.58), kind=kOutput, calls=%fused_computation.94 | convolution fusion | flops 16777216 | bytes 2170880 | tf_op jit(solution)/shard_map/dot_general | solution.py:228
  98.9 4.3 %all-to-all-start.3 = ((f32[8,4,512]{2,0,1:T(8,128)}), f32[8,4,512]{2,0,1:T(8,128)S(1)}, u32[]{:S(2)}, u32[]{:S(2)}) async-start(f32[8,4,512]{2,0,1:T(8,128)} %fusion.32), calls=%async_computation.3 | async-start | bytes 131072 | tf_op jit(solution)/shard_map/all_to_all | solution.py:230
  103.2 0.7 pad_maximum_fusion.2
  103.8 5.0 %all-to-all-done.3 = f32[8,4,512]{2,0,1:T(8,128)S(1)} async-done(((f32[8,4,512]{2,0,1:T(8,128)}), f32[8,4,512]{2,0,1:T(8,128)S(1)}, u32[]{:S(2)}, u32[]{:S(2)}) %all-to-all-start.3) | async-done | bytes 65568 | tf_op jit(solution)/shard_map/all_to_all | solution.py:230
  108.8 0.6 reduce_sum.174
  (54 shorter events, 1.7 us)
Async XLA Ops:
  0.6 12.8 %copy-start = (bf16[2048,512]{1,0:T(8,128)(2,1)S(1)}, bf16[2048,512]{1,0:T(8,128)(2,1)}, u32[]{:S(2)}) copy-start(bf16[2048,512]{1,0:T(8,128)(2,1)} %param.16) | copy-start | bytes 6291460
  2.9 20.4 %all-to-all-start = ((bf16[8,512,128]{1,2,0:T(8,128)(2,1)}), bf16[8,512,128]{1,2,0:T(8,128)(2,1)S(1)}, u32[]{:S(2)}, u32[]{:S(2)}) async-start(bf16[8,512,128]{1,2,0:T(8,128)(2,1)} %broadcast_in_dim.215), calls=%async_computation | async-start | bytes 2097152 | tf_op jit(solution)/shard_map/all_to_all | solution.py:60
  13.4 26.3 %copy-start.3 = (f32[8,128]{1,0:T(8,128)}, f32[8,128]{1,0:T(8,128)S(1)}, u32[]{:S(2)}) copy-start(f32[8,128]{1,0:T(8,128)S(1)} %fusion.23) | copy-start | bytes 12292
  23.3 23.5 %copy-start.1 = (bf16[8,512,128]{1,2,0:T(8,128)(2,1)}, bf16[8,512,128]{1,2,0:T(8,128)(2,1)S(1)}, u32[]{:S(2)}) copy-start(bf16[8,512,128]{1,2,0:T(8,128)(2,1)S(1)} %all-to-all-done) | copy-start | bytes 3145732
  24.2 27.9 %all-to-all-start.1 = ((bf16[16,8,512]{2,1,0:T(8,128)(2,1)}), bf16[16,8,512]{2,1,0:T(8,128)(2,1)S(1)}, u32[]{:S(2)}, u32[]{:S(2)}) async-start(bf16[16,8,512]{2,1,0:T(8,128)(2,1)} %broadcast_in_dim.218), calls=%async_computation.1 | async-start | bytes 262144 | tf_op jit(solution)/shard_map/all_to_all | solution.py:60
  46.8 0.5 copy-start.6
  47.3 8.9 %copy-start.8 = (pred[128,8]{0,1:T(8,128)(4,1)S(1)}, pred[128,8]{0,1:T(8,128)(4,1)}, u32[]{:S(2)}) copy-start(pred[128,8]{0,1:T(8,128)(4,1)} %get-tuple-element.12) | copy-start | bytes 3076
  47.3 8.9 %copy-start.9 = (pred[128,8]{0,1:T(8,128)(4,1)S(1)}, pred[128,8]{0,1:T(8,128)(4,1)}, u32[]{:S(2)}) copy-start(pred[128,8]{0,1:T(8,128)(4,1)} %get-tuple-element.13) | copy-start | bytes 3076
  52.5 3.7 %copy-start.2 = (bf16[8,512,128]{1,2,0:T(8,128)(2,1)S(1)}, bf16[8,512,128]{1,2,0:T(8,128)(2,1)}, u32[]{:S(2)}) copy-start(bf16[8,512,128]{1,2,0:T(8,128)(2,1)} %copy-done.1) | copy-start | bytes 3145732
  60.6 5.0 %copy-start.7 = (pred[128,8]{0,1:T(8,128)(4,1)S(1)}, pred[128,8]{0,1:T(8,128)(4,1)}, u32[]{:S(2)}) copy-start(pred[128,8]{0,1:T(8,128)(4,1)} %copy-done.6) | copy-start | bytes 3076
  60.6 15.7 %copy-start.5 = (bf16[8,64]{1,0:T(8,128)(2,1)S(1)}, bf16[8,64]{1,0:T(8,128)(2,1)}, u32[]{:S(2)}) copy-start(bf16[8,64]{1,0:T(8,128)(2,1)} %get-tuple-element.40) | copy-start | bytes 3076
  60.6 15.7 %copy-start.10 = (bf16[8,64]{1,0:T(8,128)(2,1)S(1)}, bf16[8,64]{1,0:T(8,128)(2,1)}, u32[]{:S(2)}) copy-start(bf16[8,64]{1,0:T(8,128)(2,1)} %slice.140) | copy-start | bytes 3076
  60.6 15.8 %copy-start.11 = (s32[8]{0:T(128)S(1)}, s32[8]{0:T(128)}, u32[]{:S(2)}) copy-start(s32[8]{0:T(128)} %param.27) | copy-start | bytes 100
  60.7 15.9 %copy-start.4 = (f32[8,128]{1,0:T(8,128)S(1)}, f32[8,128]{1,0:T(8,128)}, u32[]{:S(2)}) copy-start(f32[8,128]{1,0:T(8,128)} %copy-done.3) | copy-start | bytes 12292
  68.3 27.1 %all-to-all-start.2 = ((bf16[16,8,1152]{2,1,0:T(8,128)(2,1)}), bf16[16,8,1152]{2,1,0:T(8,128)(2,1)S(1)}, u32[]{:S(2)}, u32[]{:S(2)}) async-start(bf16[16,8,1152]{2,1,0:T(8,128)(2,1)} %concatenate.45), calls=%async_computation.2 | async-start | bytes 589824 | tf_op jit(solution)/shard_map/all_to_all | solution.py:67
  98.9 9.9 %all-to-all-start.3 = ((f32[8,4,512]{2,0,1:T(8,128)}), f32[8,4,512]{2,0,1:T(8,128)S(1)}, u32[]{:S(2)}, u32[]{:S(2)}) async-start(f32[8,4,512]{2,0,1:T(8,128)} %fusion.32), calls=%async_computation.3 | async-start | bytes 131072 | tf_op jit(solution)/shard_map/all_to_all | solution.py:230

commit v9 on v8

--- a/solution.py
+++ b/solution.py
@@ -89,7 +89,8 @@
     group = w_query.shape[1] // head_dim
     factor = head_dim ** (-0.5)
     device = (
-        lax.axis_index("z") * (lax.axis_size("y") * lax.axis_size("core"))
+        (lax.axis_index("zh") * lax.axis_size("zl") + lax.axis_index("zl"))
+        * (lax.axis_size("y") * lax.axis_size("core"))
         + lax.axis_index("y") * lax.axis_size("core")
         + lax.axis_index("core")
     )
@@ -117,7 +118,9 @@
         -1, node_rows.shape[0], node_rows.shape[1]
     )
     queries, slots = lax.optimization_barrier((queries, slots))
-    everyone = gather_rows(queries.reshape(local_leaves, group * head_dim), "z")
+    everyone = gather_rows(
+        gather_rows(queries.reshape(local_leaves, group * head_dim), "zl"), "zh"
+    )
     raw_entry = jnp.dot(normed, w_keyval, preferred_element_type=jnp.float32)
     new_entry = jnp.concatenate(
         [rotate(raw_entry[:, :head_dim], positions), raw_entry[:, head_dim:]], -1
@@ -140,7 +143,7 @@
 
     row_count = everyone.shape[0]
     slot_count = slots.shape[0]
-    z_size = lax.axis_size("z")
+    z_size = lax.axis_size("zh") * lax.axis_size("zl")
     my_y_core = device % slot_count
     first_slot = device - my_y_core
     row_branch = lax.dynamic_slice_in_dim(
@@ -196,7 +199,7 @@
     packet = jnp.concatenate(
         pieces + stats + [jnp.zeros((row_count, pad_width), jnp.bfloat16)], -1
     )
-    gathered = scatter_rows(packet, "z")
+    gathered = scatter_rows(scatter_rows(packet, "zh"), "zl")
     sums = []
     weights = []
     peaks = []
@@ -244,11 +247,12 @@
     core_size = 2
     y_size = 4
     z_size = request_size // (y_size * core_size)
+    z_low = 4
     fine = Mesh(
-        mesh.devices.reshape(tensor_size, z_size, y_size, core_size),
-        ("tensor", "z", "y", "core"),
-    )
-    request = ("z", "y", "core")
+        mesh.devices.reshape(tensor_size, z_size // z_low, z_low, y_size, core_size),
+        ("tensor", "zh", "zl", "y", "core"),
+    )
+    request = ("zh", "zl", "y", "core")
     in_specs = (
         P(request, None),
         P(),

time: 110 us -> 124 us (1.13)
  the two profiles are of different devices: /device:TPU:64 before, /device:TPU:24 now
where the time goes in v9:
time: 124 us; the launch traced here: 122 us
  waiting for transfers between devices  45.7 us (37%)
  starting transfers between devices  34.7 us (28%)
  matrix products  13.9 us (11%)
  local copies, waits for them, and re-layouts  13.6 us (11%)
  other arithmetic  13.6 us (11%)
    all_to_all x3, starting transfers between devices, gather_rows(): received = lax.all_to_all(spread, axes, 0, 0, tiled=False)  23.1 us
    all_to_all x3, waiting for transfers between devices, gather_rows(): received = lax.all_to_all(spread, axes, 0, 0, tiled=False)  21.3 us
    all_to_all x2, waiting for transfers between devices, scatter_rows(): received = lax.all_to_all(blocks, axes, 0, 0, tiled=False)  19.5 us
    all_to_all x2, starting transfers between devices, scatter_rows(): received = lax.all_to_all(blocks, axes, 0, 0, tiled=False)  7.22 us
    all_to_all x1, waiting for transfers between devices, local(): lax.all_to_all(term.reshape(local_leaves, tensor_size, term.shape[1] // t...  4.97 us
    dot_general x2, matrix products, soft_part(): jnp.einsum(pattern, weights, value_rows, preferred_element_type=jnp.float32)  4.64 us
    all_to_all x1, starting transfers between devices, local(): lax.all_to_all(term.reshape(local_leaves, tensor_size, term.shape[1] // t...  4.4 us
    reduce_sum x2, other arithmetic, soft_part(): weight_sum = jnp.sum(weights.astype(jnp.float32), -1)  4.24 us
  transfers between devices with their start and end apart: 6, of which 6 were waited for; matrix products, arithmetic and copies ran while one was open for 14% of the time, Pallas kernels for 0%

profile of v9, /device:TPU:24, one launch (start us, length us, event | category | flops | bytes accessed | tf_op | source)
XLA Modules:
  0.0 122.4 jit_solution(14990714237343783035)
XLA Ops:
  0.6 1.2 copy.76
  1.8 1.1 broadcast_in_dim.222
  2.9 9.1 %all-to-all-start = ((bf16[8,512,128]{1,2,0:T(8,128)(2,1)}), bf16[8,512,128]{1,2,0:T(8,128)(2,1)S(1)}, u32[]{:S(2)}, u32[]{:S(2)}) async-start(bf16[8,512,128]{1,2,0:T(8,128)(2,1)} %broadcast_in_dim.222), calls=%async_computation | async-start | bytes 2097152 | tf_op jit(solution)/shard_map/all_to_all | solution.py:60
  11.9 0.9 fusion.16
  12.9 0.8 reshape.422
  13.6 0.8 dynamic_slice.7
  14.6 0.7 broadcast_compare_fusion
  15.3 0.7 broadcast_compare_fusion.1
  16.0 0.7 iota_compare_fusion.6
  16.7 1.3 %fusion.23 = f32[8,128]{1,0:T(8,128)S(1)} fusion(bf16[2048,128]{1,0:T(8,128)(2,1)} %param.17, bf16[8,2048]{1,0:T(8,128)(2,1)} %param.14, f32[2048]{0:T(1024)} %param.15, f32[8]{0:T(128)S(1)} %add_rsqrt_fusion), kind=kOutput, calls=%fused_computation.60 | convolution fusion | flops 4259840 | bytes 569376 | tf_op jit(solution)/shard_map/dot_general | solution.py:124
  18.0 1.2 fusion.25
  19.2 0.9 select_reduce_fusion.4
  20.1 0.9 select_reduce_fusion.5
  21.0 0.1 and_reduce_fusion.2
  21.1 0.7 add_convert_fusion
  21.7 0.1 copy.75
  22.0 0.1 fusion.30
  22.3 3.5 %all-to-all-done = bf16[8,512,128]{1,2,0:T(8,128)(2,1)S(1)} async-done(((bf16[8,512,128]{1,2,0:T(8,128)(2,1)}), bf16[8,512,128]{1,2,0:T(8,128)(2,1)S(1)}, u32[]{:S(2)}, u32[]{:S(2)}) %all-to-all-start) | async-done | bytes 1048608 | tf_op jit(solution)/shard_map/all_to_all | solution.py:60
  25.8 0.1 broadcast_in_dim.224
  25.9 0.7 broadcast_in_dim.225
  26.6 3.3 %all-to-all-start.1 = ((bf16[4,8,512]{2,1,0:T(8,128)(2,1)}), bf16[4,8,512]{2,1,0:T(8,128)(2,1)S(1)}, u32[]{:S(2)}, u32[]{:S(2)}) async-start(bf16[4,8,512]{2,1,0:T(8,128)(2,1)} %broadcast_in_dim.225), calls=%async_computation.1 | async-start | bytes 65536 | tf_op jit(solution)/shard_map/all_to_all | solution.py:60
  29.9 0.2 and_reduce_fusion
  30.1 5.4 %all-to-all-done.1 = bf16[4,8,512]{2,1,0:T(8,128)(2,1)S(1)} async-done(((bf16[4,8,512]{2,1,0:T(8,128)(2,1)}), bf16[4,8,512]{2,1,0:T(8,128)(2,1)S(1)}, u32[]{:S(2)}, u32[]{:S(2)}) %all-to-all-start.1) | async-done | bytes 32800 | tf_op jit(solution)/shard_map/all_to_all | solution.py:60
  35.5 0.7 broadcast_in_dim.227
  36.2 10.7 %all-to-all-start.2 = ((bf16[4,32,512]{2,1,0:T(8,128)(2,1)}), bf16[4,32,512]{2,1,0:T(8,128)(2,1)S(1)}, u32[]{:S(2)}, u32[]{:S(2)}) async-start(bf16[4,32,512]{2,1,0:T(8,128)(2,1)} %broadcast_in_dim.227), calls=%async_computation.2 | async-start | bytes 262144 | tf_op jit(solution)/shard_map/all_to_all | solution.py:60
  47.0 0.7 broadcast_and_fusion
  47.7 12.4 %all-to-all-done.2 = bf16[4,32,512]{2,1,0:T(8,128)(2,1)S(1)} async-done(((bf16[4,32,512]{2,1,0:T(8,128)(2,1)}), bf16[4,32,512]{2,1,0:T(8,128)(2,1)S(1)}, u32[]{:S(2)}, u32[]{:S(2)}) %all-to-all-start.2) | async-done | bytes 131104 | tf_op jit(solution)/shard_map/all_to_all | solution.py:60
  60.1 0.2 reshape_reshape.3
  60.3 0.2 copy.77
  60.5 3.7 %fusion = (f32[128,8,8]{0,2,1:T(8,128)S(1)}, f32[8,512,128,8]{2,1,3,0:T(8,128)S(1)}) fusion(pred[128,8,512]{0,2,1:T(8,128)(4,1)S(1)} %broadcast_and_fusion, bf16[128,8,64]{0,2,1:T(8,128)(2,1)S(1)} %copy.77, bf16[8,512,128]{1,2,0:T(8,128)(2,1)} %copy-done.1), kind=kOutput, calls=%fused_computation.3 | convolution fusion | flops 549445632 | bytes 17989632 | tf_op jit(solution)/shard_map/ngd,skd->nsgk/dot_general | solution.py:173
  64.2 4.4 %fusion.2 = (bf16[128,8,64]{0,2,1:T(8,128)(2,1)S(1)}, bf16[128,8,64]{0,2,1:T(8,128)(2,1)S(1)}) fusion(pred[128,8]{0,1:T(8,128)(4,1)S(1)} %get-tuple-element.12, pred[128,8]{0,1:T(8,128)(4,1)S(1)} %get-tuple-element.13, f32[8,512,128,8]{2,1,3,0:T(8,128)S(1)} %get-tuple-element.41, f32[128,8,8]{0,2,1:T(8,128)S(1)} %get-tuple-element.40, ...), kind=kOutput, calls=%fused_computation.7 | convolution fusion | flops 559808512 | bytes 18122752 | tf_op jit(solution)/shard_map/nsgk,skd->nsgd/dot_general | solution.py:24
  68.6 4.1 %convert_reduce_fusion = f32[128,8,8]{0,2,1:T(8,128)S(1)} fusion(f32[128,8,8]{0,2,1:T(8,128)S(1)} %get-tuple-element.40, f32[8,512,128,8]{2,1,3,0:T(8,128)S(1)} %get-tuple-element.41, pred[128,8,512]{0,2,1:T(8,128)(4,1)S(1)} %broadcast_and_fusion), kind=kLoop, calls=%fused_computation.1 | loop fusion | flops 29351936 | bytes 17367040 | tf_op jit(solution)/shard_map/reduce_sum | solution.py:25
  73.1 0.2 copy.79
  73.3 0.2 convert_element_type.171
  73.5 0.2 copy.80
  73.7 0.2 convert_element_type.173
  73.9 0.1 copy.89
  74.0 0.1 copy.90
  74.1 0.1 copy.91
  74.2 0.1 copy.92
  74.4 0.1 copy.93
  74.5 0.1 copy.94
  74.6 0.1 copy.95
  74.7 0.1 copy.96
  74.8 0.1 copy.97
  74.9 0.1 copy.98
  75.0 0.9 concatenate.45
  75.9 3.9 %all-to-all-start.3 = ((bf16[4,32,1152]{2,1,0:T(8,128)(2,1)}), bf16[4,32,1152]{2,1,0:T(8,128)(2,1)S(1)}, u32[]{:S(2)}, u32[]{:S(2)}) async-start(bf16[4,32,1152]{2,1,0:T(8,128)(2,1)} %concatenate.45), calls=%async_computation.3 | async-start | bytes 589824 | tf_op jit(solution)/shard_map/all_to_all | solution.py:67
  79.9 0.2 copy.99
  80.1 3.9 %copy.104 = bf16[2048,512]{1,0:T(8,128)(2,1)} copy(bf16[2048,512]{0,1:T(8,128)(2,1)} %bitcast.61) | data formatting | bytes 4194304 | tf_op jit(solution)/shard_map/dot_general | solution.py:231
  84.3 0.2 bitcast_select_fusion.3
  84.5 14.1 %all-to-all-done.3 = bf16[4,32,1152]{2,1,0:T(8,128)(2,1)S(1)} async-done(((bf16[4,32,1152]{2,1,0:T(8,128)(2,1)}), bf16[4,32,1152]{2,1,0:T(8,128)(2,1)S(1)}, u32[]{:S(2)}, u32[]{:S(2)}) %all-to-all-start.3) | async-done | bytes 294944 | tf_op jit(solution)/shard_map/all_to_all | solution.py:67
  98.6 0.7 reduce_sum.184
  99.3 3.3 %all-to-all-start.4 = ((bf16[4,8,1152]{2,1,0:T(8,128)(2,1)}), bf16[4,8,1152]{2,1,0:T(8,128)(2,1)S(1)}, u32[]{:S(2)}, u32[]{:S(2)}) async-start(bf16[4,8,1152]{2,1,0:T(8,128)(2,1)} %bitcast.9), calls=%async_computation.4 | async-start | bytes 147456 | tf_op jit(solution)/shard_map/all_to_all | solution.py:67
  102.6 0.2 fusion.31
  102.8 0.2 convert_reduce_fusion.1
  103.0 5.3 %all-to-all-done.4 = bf16[4,8,1152]{2,1,0:T(8,128)(2,1)S(1)} async-done(((bf16[4,8,1152]{2,1,0:T(8,128)(2,1)}), bf16[4,8,1152]{2,1,0:T(8,128)(2,1)S(1)}, u32[]{:S(2)}, u32[]{:S(2)}) %all-to-all-start.4) | async-done | bytes 73760 | tf_op jit(solution)/shard_map/all_to_all | solution.py:67
  108.6 0.2 fusion.6
  108.8 0.1 reshape.437
  108.9 2.9 %fusion.32 = f32[8,4,512]{2,0,1:T(8,128)} fusion(bf16[8,512,1]{1,0,2:T(8,128)(2,1)S(1)} %reshape.437, bf16[4,512,512]{2,1,0:T(8,128)(2,1)} %bitcast.60), kind=kOutput, calls=%fused_computation.98 | convolution fusion | flops 16777216 | bytes 2170880 | tf_op jit(solution)/shard_map/dot_general | solution.py:231
  111.8 4.4 %all-to-all-start.5 = ((f32[8,4,512]{2,0,1:T(8,128)}), f32[8,4,512]{2,0,1:T(8,128)S(1)}, u32[]{:S(2)}, u32[]{:S(2)}) async-start(f32[8,4,512]{2,0,1:T(8,128)} %fusion.32), calls=%async_computation.5 | async-start | bytes 131072 | tf_op jit(solution)/shard_map/all_to_all | solution.py:233
  116.2 0.7 pad_maximum_fusion.2
  116.8 5.0 %all-to-all-done.5 = f32[8,4,512]{2,0,1:T(8,128)S(1)} async-done(((f32[8,4,512]{2,0,1:T(8,128)}), f32[8,4,512]{2,0,1:T(8,128)S(1)}, u32[]{:S(2)}, u32[]{:S(2)}) %all-to-all-start.5) | async-done | bytes 65568 | tf_op jit(solution)/shard_map/all_to_all | solution.py:233
  121.8 0.6 reduce_sum.187
  (46 shorter events, 1.6 us)
Async XLA Ops:
  0.6 17.4 %copy-start = (bf16[2048,512]{1,0:T(8,128)(2,1)S(1)}, bf16[2048,512]{1,0:T(8,128)(2,1)}, u32[]{:S(2)}) copy-start(bf16[2048,512]{1,0:T(8,128)(2,1)} %param.16) | copy-start | bytes 6291460
  2.9 22.9 %all-to-all-start = ((bf16[8,512,128]{1,2,0:T(8,128)(2,1)}), bf16[8,512,128]{1,2,0:T(8,128)(2,1)S(1)}, u32[]{:S(2)}, u32[]{:S(2)}) async-start(bf16[8,512,128]{1,2,0:T(8,128)(2,1)} %broadcast_in_dim.222), calls=%async_computation | async-start | bytes 2097152 | tf_op jit(solution)/shard_map/all_to_all | solution.py:60
  25.8 21.1 %copy-start.1 = (bf16[8,512,128]{1,2,0:T(8,128)(2,1)}, bf16[8,512,128]{1,2,0:T(8,128)(2,1)S(1)}, u32[]{:S(2)}) copy-start(bf16[8,512,128]{1,2,0:T(8,128)(2,1)S(1)} %all-to-all-done) | copy-start | bytes 3145732
  26.6 8.9 %all-to-all-start.1 = ((bf16[4,8,512]{2,1,0:T(8,128)(2,1)}), bf16[4,8,512]{2,1,0:T(8,128)(2,1)S(1)}, u32[]{:S(2)}, u32[]{:S(2)}) async-start(bf16[4,8,512]{2,1,0:T(8,128)(2,1)} %broadcast_in_dim.225), calls=%async_computation.1 | async-start | bytes 65536 | tf_op jit(solution)/shard_map/all_to_all | solution.py:60
  36.2 23.9 %all-to-all-start.2 = ((bf16[4,32,512]{2,1,0:T(8,128)(2,1)}), bf16[4,32,512]{2,1,0:T(8,128)(2,1)S(1)}, u32[]{:S(2)}, u32[]{:S(2)}) async-start(bf16[4,32,512]{2,1,0:T(8,128)(2,1)} %broadcast_in_dim.227), calls=%async_computation.2 | async-start | bytes 262144 | tf_op jit(solution)/shard_map/all_to_all | solution.py:60
  60.5 3.7 %copy-start.2 = (bf16[8,512,128]{1,2,0:T(8,128)(2,1)S(1)}, bf16[8,512,128]{1,2,0:T(8,128)(2,1)}, u32[]{:S(2)}) copy-start(bf16[8,512,128]{1,2,0:T(8,128)(2,1)} %copy-done.1) | copy-start | bytes 3145732
  68.6 11.3 %copy-start.3 = (bf16[8,1,128,128]{3,2,1,0:T(8,128)(2,1)S(1)}, bf16[8,1,128,128]{3,2,1,0:T(8,128)(2,1)}, u32[]{:S(2)}) copy-start(bf16[8,1,128,128]{3,2,1,0:T(8,128)(2,1)} %param.20) | copy-start | bytes 786436
  68.6 15.5 %copy-start.4 = (s32[8]{0:T(128)S(1)}, s32[8]{0:T(128)}, u32[]{:S(2)}) copy-start(s32[8]{0:T(128)} %param.27) | copy-start | bytes 100
  75.9 22.7 %all-to-all-start.3 = ((bf16[4,32,1152]{2,1,0:T(8,128)(2,1)}), bf16[4,32,1152]{2,1,0:T(8,128)(2,1)S(1)}, u32[]{:S(2)}, u32[]{:S(2)}) async-start(bf16[4,32,1152]{2,1,0:T(8,128)(2,1)} %concatenate.45), calls=%async_computation.3 | async-start | bytes 589824 | tf_op jit(solution)/shard_map/all_to_all | solution.py:67
  99.3 9.0 %all-to-all-start.4 = ((bf16[4,8,1152]{2,1,0:T(8,128)(2,1)}), bf16[4,8,1152]{2,1,0:T(8,128)(2,1)S(1)}, u32[]{:S(2)}, u32[]{:S(2)}) async-start(bf16[4,8,1152]{2,1,0:T(8,128)(2,1)} %bitcast.9), calls=%async_computation.4 | async-start | bytes 147456 | tf_op jit(solution)/shard_map/all_to_all | solution.py:67
  111.8 10.0 %all-to-all-start.5 = ((f32[8,4,512]{2,0,1:T(8,128)}), f32[8,4,512]{2,0,1:T(8,128)S(1)}, u32[]{:S(2)}, u32[]{:S(2)}) async-start(f32[8,4,512]{2,0,1:T(8,128)} %fusion.32), calls=%async_computation.5 | async-start | bytes 131072 | tf_op jit(solution)/shard_map/all_to_all | solution.py:233

commit v10 on v8

--- a/solution.py
+++ b/solution.py
@@ -173,19 +173,19 @@
         * factor
     )
     usable = mine_all[:, :, None, None] & node_usable[None, :, None, :]
-    slot_sum, slot_weight, slot_peak = soft_part(
-        scores, usable, slots[:, :, head_dim:], "nsgk,skd->nsgd"
-    )
+    scores = jnp.where(usable, scores, FLOOR)
+    slot_peak = jnp.max(scores, -1)
+    weights = jnp.where(usable, jnp.exp(scores - slot_peak[..., None]), 0.0).astype(jnp.bfloat16)
     slot_peak = jnp.where(mine_all[:, :, None], slot_peak, 0.0)
-
-    def pick(mask, values):
-        shape = mask.shape + (1,) * (values.ndim - mask.ndim)
-        return jnp.sum(jnp.where(mask.reshape(shape), values, 0.0), 1)
-
-    parts = [
-        (pick(mask, slot_sum), pick(mask, slot_weight), pick(mask, slot_peak))
-        for mask in (root_mine, branch_mine)
-    ]
+    parts = []
+    for mask in (root_mine, branch_mine):
+        part_weights = jnp.where(mask[:, :, None, None], weights, jnp.zeros_like(weights))
+        part_sum = jnp.einsum(
+            "nsgk,skd->ngd", part_weights, slots[:, :, head_dim:], preferred_element_type=jnp.float32
+        )
+        part_weight = jnp.sum(part_weights.astype(jnp.float32), (1, 3))
+        part_peak = jnp.sum(jnp.where(mask[:, :, None], slot_peak, 0.0), 1)
+        parts.append((part_sum, part_weight, part_peak))
     pieces = []
     stats = []
     for part_sum, part_weight, part_peak in parts:

time: 110 us -> 111 us (level)
  the two profiles are of different devices: /device:TPU:64 before, /device:TPU:24 now
where the time goes in v10:
time: 111 us; the launch traced here: 109 us
  waiting for transfers between devices  30.9 us (28%)
  starting transfers between devices  30.5 us (27%)
  other arithmetic  18.8 us (17%)
  local copies, waits for them, and re-layouts  14.8 us (13%)
  matrix products  12.6 us (11%)
    all_to_all x2, starting transfers between devices, gather_rows(): received = lax.all_to_all(spread, axes, 0, 0, tiled=False)  19.9 us
    all_to_all x1, waiting for transfers between devices, scatter_rows(): received = lax.all_to_all(blocks, axes, 0, 0, tiled=False)  18.3 us
    all_to_all x2, waiting for transfers between devices, gather_rows(): received = lax.all_to_all(spread, axes, 0, 0, tiled=False)  7.67 us
    reduce_sum x1, other arithmetic, local(): part_weight = jnp.sum(part_weights.astype(jnp.float32), (1, 3))  6.39 us
    all_to_all x1, starting transfers between devices, scatter_rows(): received = lax.all_to_all(blocks, axes, 0, 0, tiled=False)  6.28 us
    all_to_all x1, waiting for transfers between devices, local(): lax.all_to_all(term.reshape(local_leaves, tensor_size, term.shape[1] // t...  4.97 us
    all_to_all x1, starting transfers between devices, local(): lax.all_to_all(term.reshape(local_leaves, tensor_size, term.shape[1] // t...  4.29 us
    dot_general x1, local copies, waits for them, and re-layouts, local(): term = jnp.dot(attended, w_output, preferred_element_type=jnp.float32)  3.94 us
  transfers between devices with their start and end apart: 4, of which 4 were waited for; matrix products, arithmetic and copies ran while one was open for 20% of the time, Pallas kernels for 0%

profile of v10, /device:TPU:24, one launch (start us, length us, event | category | flops | bytes accessed | tf_op | source)
XLA Modules:
  0.0 108.7 jit_solution(11576843734387720286)
XLA Ops:
  0.6 1.2 %copy.56 = bf16[512,128]{0,1:T(8,128)(2,1)S(1)} copy(bf16[512,128]{1,0:T(8,128)(2,1)} %bitcast.57) | data formatting | bytes 262144 | tf_op jit(solution)/shard_map/broadcast_in_dim | solution.py:59
  1.8 1.1 broadcast_in_dim.207
  2.9 9.1 %all-to-all-start = ((bf16[8,512,128]{1,2,0:T(8,128)(2,1)}), bf16[8,512,128]{1,2,0:T(8,128)(2,1)S(1)}, u32[]{:S(2)}, u32[]{:S(2)}) async-start(bf16[8,512,128]{1,2,0:T(8,128)(2,1)} %broadcast_in_dim.207), calls=%async_computation | async-start | bytes 2097152 | tf_op jit(solution)/shard_map/all_to_all | solution.py:60
  11.9 0.8 reshape.412
  12.7 0.8 dynamic_slice.7
  13.5 0.9 fusion.23
  14.4 1.3 %fusion.30 = f32[8,128]{1,0:T(8,128)S(1)} fusion(bf16[2048,128]{1,0:T(8,128)(2,1)} %param.17, bf16[8,2048]{1,0:T(8,128)(2,1)} %param.14, f32[2048]{0:T(1024)} %param.15, f32[8]{0:T(128)S(1)} %add_rsqrt_fusion), kind=kOutput, calls=%fused_computation.62 | convolution fusion | flops 4259840 | bytes 569376 | tf_op jit(solution)/shard_map/dot_general | solution.py:121
  15.7 1.2 %fusion.32 = f32[8,512]{1,0:T(8,128)S(1)} fusion(bf16[2048,512]{1,0:T(8,128)(2,1)S(1)} %copy-done, bf16[8,2048]{1,0:T(8,128)(2,1)} %param.14, f32[2048]{0:T(1024)} %param.15, f32[8]{0:T(128)S(1)} %add_rsqrt_fusion), kind=kOutput, calls=%fused_computation.63 | convolution fusion | flops 16842752 | bytes 2154528 | tf_op jit(solution)/shard_map/dot_general | solution.py:111
  16.9 0.1 eq.132
  17.1 0.7 iota_compare_fusion.6
  17.7 0.7 broadcast_compare_fusion.1
  18.4 0.7 broadcast_compare_fusion
  19.2 1.4 %select_reduce_fusion.5 = (s32[8]{0:T(128)}, s32[8]{0:T(128)S(1)}, s32[8]{0:T(128)S(1)}) fusion(s32[64]{0:T(128)} %param.26, s32[64]{0:T(128)} %param.24, s32[8]{0:T(128)S(1)} %iota_add_fusion, s32[8]{0:T(128)S(1)} %dynamic_slice.7, s32[64]{0:T(128)} %param.22), kind=kLoop, calls=%fused_computation.84 | loop fusion | flops 4072 | bytes 928 | tf_op jit(solution)/shard_map/reduce_sum | solution.py:164
  20.6 1.4 %select_reduce_fusion.6 = (s32[8]{0:T(128)}, s32[8]{0:T(128)S(1)}) fusion(s32[8]{0:T(128)} %param.25, s32[8]{0:T(128)S(1)} %iota_add_fusion, s32[8]{0:T(128)} %param.23, s32[8]{0:T(128)S(1)} %get-tuple-element.14), kind=kLoop, calls=%fused_computation.85 | loop fusion | flops 368 | bytes 192 | tf_op jit(solution)/shard_map/reduce_sum | solution.py:162
  22.0 0.1 and_reduce_fusion.2
  22.1 0.7 add_convert_fusion
  22.9 0.1 copy.55
  23.0 0.7 fusion.37
  23.8 0.1 fusion.27
  23.9 1.9 %all-to-all-done = bf16[8,512,128]{1,2,0:T(8,128)(2,1)S(1)} async-done(((bf16[8,512,128]{1,2,0:T(8,128)(2,1)}), bf16[8,512,128]{1,2,0:T(8,128)(2,1)S(1)}, u32[]{:S(2)}, u32[]{:S(2)}) %all-to-all-start) | async-done | bytes 1048608 | tf_op jit(solution)/shard_map/all_to_all | solution.py:60
  25.8 0.1 broadcast_in_dim.208
  25.9 0.8 broadcast_in_dim.209
  26.7 10.8 %all-to-all-start.1 = ((bf16[16,8,512]{2,1,0:T(8,128)(2,1)}), bf16[16,8,512]{2,1,0:T(8,128)(2,1)S(1)}, u32[]{:S(2)}, u32[]{:S(2)}) async-start(bf16[16,8,512]{2,1,0:T(8,128)(2,1)} %broadcast_in_dim.209), calls=%async_computation.1 | async-start | bytes 262144 | tf_op jit(solution)/shard_map/all_to_all | solution.py:60
  37.5 0.8 and_reduce_fusion
  38.3 0.6 slice.145
  39.0 1.1 %copy.80 = bf16[8,1,128,128]{2,3,0,1:T(8,128)(2,1)S(1)} copy(bf16[8,1,128,128]{3,2,1,0:T(8,128)(2,1)} %param.20) | data formatting | bytes 524288 | tf_op args[6]
  40.1 3.9 %copy.86 = bf16[2048,512]{1,0:T(8,128)(2,1)} copy(bf16[2048,512]{0,1:T(8,128)(2,1)} %bitcast.56) | data formatting | bytes 4194304 | tf_op jit(solution)/shard_map/dot_general | solution.py:228
  44.0 0.7 or.11
  44.7 0.7 add.97
  45.5 0.7 broadcast_and_fusion
  46.2 5.7 %all-to-all-done.1 = bf16[16,8,512]{2,1,0:T(8,128)(2,1)S(1)} async-done(((bf16[16,8,512]{2,1,0:T(8,128)(2,1)}), bf16[16,8,512]{2,1,0:T(8,128)(2,1)S(1)}, u32[]{:S(2)}, u32[]{:S(2)}) %all-to-all-start.1) | async-done | bytes 131104 | tf_op jit(solution)/shard_map/all_to_all | solution.py:60
  51.9 0.2 reshape_reshape.3
  52.1 0.2 copy.57
  52.3 3.6 %fusion = (f32[128,8,8]{0,2,1:T(8,128)S(1)}, f32[8,512,128,8]{2,1,3,0:T(8,128)S(1)}) fusion(pred[128,8,512]{0,2,1:T(8,128)(4,1)S(1)} %broadcast_and_fusion, bf16[128,8,64]{0,2,1:T(8,128)(2,1)S(1)} %copy.57, bf16[8,512,128]{1,2,0:T(8,128)(2,1)} %copy-done.1), kind=kOutput, calls=%fused_computation.4 | convolution fusion | flops 549445632 | bytes 17989632 | tf_op jit(solution)/shard_map/ngd,skd->nsgk/dot_general | solution.py:170
  56.0 6.4 %convert_reduce_fusion = (f32[128,8]{0,1:T(8,128)S(1)}, f32[128,8]{0,1:T(8,128)S(1)}, bf16[128,8,8,512]{0,3,2,1:T(8,128)(2,1)S(1)}) fusion(pred[128,8]{0,1:T(8,128)(4,1)S(1)} %copy-done.6, pred[128,8]{0,1:T(8,128)(4,1)S(1)} %copy-done.7, f32[128,8,8]{0,2,1:T(8,128)S(1)} %get-tuple-element.43, f32[8,512,128,8]{2,1,3,0:T(8,128)S(1)} %get-tuple-element.44, ...), kind=kLoop, calls=%fused_computation.1 | loop fusion | flops 46135296 | bytes 25733120 | tf_op jit(solution)/shard_map/reduce_sum | solution.py:186
  62.4 1.6 %fusion.8 = bf16[128,8,64]{0,2,1:T(8,128)(2,1)S(1)} fusion(bf16[128,8,8,512]{0,3,2,1:T(8,128)(2,1)S(1)} %get-tuple-element.25, pred[128,8]{0,1:T(8,128)(4,1)S(1)} %copy-done.6, bf16[8,512,128]{1,2,0:T(8,128)(2,1)S(1)} %copy-done.2), kind=kOutput, calls=%fused_computation.14 | convolution fusion | flops 541130752 | bytes 9044992 | tf_op jit(solution)/shard_map/nsgk,skd->ngd/dot_general | solution.py:183
  64.0 1.6 %fusion.7 = bf16[128,8,64]{0,2,1:T(8,128)(2,1)S(1)} fusion(bf16[128,8,8,512]{0,3,2,1:T(8,128)(2,1)S(1)} %get-tuple-element.25, pred[128,8]{0,1:T(8,128)(4,1)S(1)} %copy-done.7, bf16[8,512,128]{1,2,0:T(8,128)(2,1)S(1)} %copy-done.2), kind=kOutput, calls=%fused_computation.13 | convolution fusion | flops 541130752 | bytes 9044992 | tf_op jit(solution)/shard_map/nsgk,skd->ngd/dot_general | solution.py:183
  65.7 0.2 copy.61
  65.9 0.2 convert_element_type.174
  66.1 0.2 copy.59
  66.3 0.2 convert_element_type.172
  66.7 0.1 copy.70
  66.8 0.1 copy.71
  67.1 0.1 copy.75
  67.2 0.1 copy.76
  67.5 0.1 copy.72
  67.6 0.1 copy.73
  67.7 0.1 copy.74
  68.0 0.1 copy.77
  68.1 0.1 copy.78
  68.2 0.1 copy.79
  68.3 0.9 concatenate.45
  69.2 6.3 %all-to-all-start.2 = ((bf16[16,8,1152]{2,1,0:T(8,128)(2,1)}), bf16[16,8,1152]{2,1,0:T(8,128)(2,1)S(1)}, u32[]{:S(2)}, u32[]{:S(2)}) async-start(bf16[16,8,1152]{2,1,0:T(8,128)(2,1)} %concatenate.45), calls=%async_computation.2 | async-start | bytes 589824 | tf_op jit(solution)/shard_map/all_to_all | solution.py:67
  75.7 0.2 bitcast_select_fusion.1
  75.9 0.2 fusion.40
  76.2 0.2 convert_reduce_fusion.2
  76.3 18.3 %all-to-all-done.2 = bf16[16,8,1152]{2,1,0:T(8,128)(2,1)S(1)} async-done(((bf16[16,8,1152]{2,1,0:T(8,128)(2,1)}), bf16[16,8,1152]{2,1,0:T(8,128)(2,1)S(1)}, u32[]{:S(2)}, u32[]{:S(2)}) %all-to-all-start.2) | async-done | bytes 294944 | tf_op jit(solution)/shard_map/all_to_all | solution.py:67
  94.9 0.2 fusion.12
  95.2 0.1 reshape.428
  95.3 2.9 %fusion.41 = f32[8,4,512]{2,0,1:T(8,128)} fusion(bf16[8,512,1]{1,0,2:T(8,128)(2,1)S(1)} %reshape.428, bf16[4,512,512]{2,1,0:T(8,128)(2,1)} %bitcast.55), kind=kOutput, calls=%fused_computation.102 | convolution fusion | flops 16777216 | bytes 2170880 | tf_op jit(solution)/shard_map/dot_general | solution.py:228
  98.1 4.3 %all-to-all-start.3 = ((f32[8,4,512]{2,0,1:T(8,128)}), f32[8,4,512]{2,0,1:T(8,128)S(1)}, u32[]{:S(2)}, u32[]{:S(2)}) async-start(f32[8,4,512]{2,0,1:T(8,128)} %fusion.41), calls=%async_computation.3 | async-start | bytes 131072 | tf_op jit(solution)/shard_map/all_to_all | solution.py:230
  102.4 0.7 pad_maximum_fusion.2
  103.1 5.0 %all-to-all-done.3 = f32[8,4,512]{2,0,1:T(8,128)S(1)} async-done(((f32[8,4,512]{2,0,1:T(8,128)}), f32[8,4,512]{2,0,1:T(8,128)S(1)}, u32[]{:S(2)}, u32[]{:S(2)}) %all-to-all-start.3) | async-done | bytes 65568 | tf_op jit(solution)/shard_map/all_to_all | solution.py:230
  108.1 0.6 reduce_sum.144
  (55 shorter events, 1.7 us)
Async XLA Ops:
  0.6 15.0 %copy-start = (bf16[2048,512]{1,0:T(8,128)(2,1)S(1)}, bf16[2048,512]{1,0:T(8,128)(2,1)}, u32[]{:S(2)}) copy-start(bf16[2048,512]{1,0:T(8,128)(2,1)} %param.16) | copy-start | bytes 6291460
  2.9 22.9 %all-to-all-start = ((bf16[8,512,128]{1,2,0:T(8,128)(2,1)}), bf16[8,512,128]{1,2,0:T(8,128)(2,1)S(1)}, u32[]{:S(2)}, u32[]{:S(2)}) async-start(bf16[8,512,128]{1,2,0:T(8,128)(2,1)} %broadcast_in_dim.207), calls=%async_computation | async-start | bytes 2097152 | tf_op jit(solution)/shard_map/all_to_all | solution.py:60
  15.7 22.6 %copy-start.3 = (f32[8,128]{1,0:T(8,128)}, f32[8,128]{1,0:T(8,128)S(1)}, u32[]{:S(2)}) copy-start(f32[8,128]{1,0:T(8,128)S(1)} %fusion.30) | copy-start | bytes 12292
  25.8 19.6 %copy-start.1 = (bf16[8,512,128]{1,2,0:T(8,128)(2,1)}, bf16[8,512,128]{1,2,0:T(8,128)(2,1)S(1)}, u32[]{:S(2)}) copy-start(bf16[8,512,128]{1,2,0:T(8,128)(2,1)S(1)} %all-to-all-done) | copy-start | bytes 3145732
  26.7 25.2 %all-to-all-start.1 = ((bf16[16,8,512]{2,1,0:T(8,128)(2,1)}), bf16[16,8,512]{2,1,0:T(8,128)(2,1)S(1)}, u32[]{:S(2)}, u32[]{:S(2)}) async-start(bf16[16,8,512]{2,1,0:T(8,128)(2,1)} %broadcast_in_dim.209), calls=%async_computation.1 | async-start | bytes 262144 | tf_op jit(solution)/shard_map/all_to_all | solution.py:60
  44.7 0.8 copy-start.8
  52.3 3.7 %copy-start.6 = (pred[128,8]{0,1:T(8,128)(4,1)S(1)}, pred[128,8]{0,1:T(8,128)(4,1)}, u32[]{:S(2)}) copy-start(pred[128,8]{0,1:T(8,128)(4,1)} %get-tuple-element.10) | copy-start | bytes 3076
  52.3 3.7 %copy-start.7 = (pred[128,8]{0,1:T(8,128)(4,1)S(1)}, pred[128,8]{0,1:T(8,128)(4,1)}, u32[]{:S(2)}) copy-start(pred[128,8]{0,1:T(8,128)(4,1)} %get-tuple-element.11) | copy-start | bytes 3076
  56.0 6.4 %copy-start.2 = (bf16[8,512,128]{1,2,0:T(8,128)(2,1)S(1)}, bf16[8,512,128]{1,2,0:T(8,128)(2,1)}, u32[]{:S(2)}) copy-start(bf16[8,512,128]{1,2,0:T(8,128)(2,1)} %copy-done.1) | copy-start | bytes 3145732
  64.0 1.6 %copy-start.9 = (pred[128,8]{0,1:T(8,128)(4,1)S(1)}, pred[128,8]{0,1:T(8,128)(4,1)}, u32[]{:S(2)}) copy-start(pred[128,8]{0,1:T(8,128)(4,1)} %copy-done.8) | copy-start | bytes 3076
  64.0 11.5 %copy-start.5 = (bf16[8,64]{1,0:T(8,128)(2,1)S(1)}, bf16[8,64]{1,0:T(8,128)(2,1)}, u32[]{:S(2)}) copy-start(bf16[8,64]{1,0:T(8,128)(2,1)} %get-tuple-element.37) | copy-start | bytes 3076
  64.0 11.5 %copy-start.10 = (bf16[8,64]{1,0:T(8,128)(2,1)S(1)}, bf16[8,64]{1,0:T(8,128)(2,1)}, u32[]{:S(2)}) copy-start(bf16[8,64]{1,0:T(8,128)(2,1)} %slice.145) | copy-start | bytes 3076
  64.0 11.6 %copy-start.11 = (s32[8]{0:T(128)S(1)}, s32[8]{0:T(128)}, u32[]{:S(2)}) copy-start(s32[8]{0:T(128)} %param.27) | copy-start | bytes 100
  64.0 11.6 %copy-start.4 = (f32[8,128]{1,0:T(8,128)S(1)}, f32[8,128]{1,0:T(8,128)}, u32[]{:S(2)}) copy-start(f32[8,128]{1,0:T(8,128)} %copy-done.3) | copy-start | bytes 12292
  69.2 25.4 %all-to-all-start.2 = ((bf16[16,8,1152]{2,1,0:T(8,128)(2,1)}), bf16[16,8,1152]{2,1,0:T(8,128)(2,1)S(1)}, u32[]{:S(2)}, u32[]{:S(2)}) async-start(bf16[16,8,1152]{2,1,0:T(8,128)(2,1)} %concatenate.45), calls=%async_computation.2 | async-start | bytes 589824 | tf_op jit(solution)/shard_map/all_to_all | solution.py:67
  98.1 9.9 %all-to-all-start.3 = ((f32[8,4,512]{2,0,1:T(8,128)}), f32[8,4,512]{2,0,1:T(8,128)S(1)}, u32[]{:S(2)}, u32[]{:S(2)}) async-start(f32[8,4,512]{2,0,1:T(8,128)} %fusion.41), calls=%async_computation.3 | async-start | bytes 131072 | tf_op jit(solution)/shard_map/all_to_all | solution.py:230

commit v11 on v8

--- a/solution.py
+++ b/solution.py
@@ -228,13 +228,13 @@
     term = jnp.dot(attended, w_output, preferred_element_type=jnp.float32)
     tensor_size = lax.axis_size("tensor")
     pieces = lax.all_to_all(
-        term.reshape(local_leaves, tensor_size, term.shape[1] // tensor_size),
+        term.reshape(local_leaves, tensor_size, term.shape[1] // tensor_size).astype(jnp.bfloat16),
         "tensor",
         1,
         1,
         tiled=False,
     )
-    mixed = jnp.sum(pieces, 1).astype(jnp.bfloat16)
+    mixed = jnp.sum(pieces.astype(jnp.float32), 1).astype(jnp.bfloat16)
     return (mixed, new_entry[:, None, :])
 
 

time: 110 us -> 110 us (level)
  no operation moved by 1% of the time
where the time goes in v11:
time: 110 us; the launch traced here: 109 us
  starting transfers between devices  31.5 us (29%)
  waiting for transfers between devices  31.1 us (28%)
  other arithmetic  16.5 us (15%)
  local copies, waits for them, and re-layouts  15.3 us (14%)
  matrix products  13.9 us (13%)
    all_to_all x2, starting transfers between devices, gather_rows(): received = lax.all_to_all(spread, axes, 0, 0, tiled=False)  19.2 us
    all_to_all x1, waiting for transfers between devices, scatter_rows(): received = lax.all_to_all(blocks, axes, 0, 0, tiled=False)  18.2 us
    all_to_all x2, waiting for transfers between devices, gather_rows(): received = lax.all_to_all(spread, axes, 0, 0, tiled=False)  8.08 us
    all_to_all x1, starting transfers between devices, scatter_rows(): received = lax.all_to_all(blocks, axes, 0, 0, tiled=False)  8 us
    all_to_all x1, waiting for transfers between devices, local(): lax.all_to_all(term.reshape(local_leaves, tensor_size, term.shape[1] // t...  4.8 us
    dot_general x2, matrix products, soft_part(): jnp.einsum(pattern, weights, value_rows, preferred_element_type=jnp.float32)  4.64 us
    all_to_all x1, starting transfers between devices, local(): lax.all_to_all(term.reshape(local_leaves, tensor_size, term.shape[1] // t...  4.27 us
    reduce_sum x2, other arithmetic, soft_part(): weight_sum = jnp.sum(weights.astype(jnp.float32), -1)  4.24 us
  transfers between devices with their start and end apart: 4, of which 4 were waited for; matrix products, arithmetic and copies ran while one was open for 20% of the time, Pallas kernels for 0%

profile of v11, /device:TPU:64, one launch (start us, length us, event | category | flops | bytes accessed | tf_op | source)
XLA Modules:
  0.0 109.2 jit_solution(16728215150828721573)
XLA Ops:
  0.6 1.2 %copy.73 = bf16[512,128]{0,1:T(8,128)(2,1)S(1)} copy(bf16[512,128]{1,0:T(8,128)(2,1)} %bitcast.60) | data formatting | bytes 262144 | tf_op jit(solution)/shard_map/broadcast_in_dim | solution.py:59
  1.8 1.1 broadcast_in_dim.215
  2.9 4.5 %all-to-all-start = ((bf16[8,512,128]{1,2,0:T(8,128)(2,1)}), bf16[8,512,128]{1,2,0:T(8,128)(2,1)S(1)}, u32[]{:S(2)}, u32[]{:S(2)}) async-start(bf16[8,512,128]{1,2,0:T(8,128)(2,1)} %broadcast_in_dim.215), calls=%async_computation | async-start | bytes 2097152 | tf_op jit(solution)/shard_map/all_to_all | solution.py:60
  7.4 0.9 fusion.16
  8.3 0.8 reshape.418
  9.0 0.8 dynamic_slice.7
  9.9 0.1 eq.132
  10.0 0.7 broadcast_compare_fusion
  10.7 0.7 broadcast_compare_fusion.1
  11.4 0.7 iota_compare_fusion.6
  12.1 1.3 %fusion.23 = f32[8,128]{1,0:T(8,128)S(1)} fusion(bf16[2048,128]{1,0:T(8,128)(2,1)} %param.17, bf16[8,2048]{1,0:T(8,128)(2,1)} %param.14, f32[2048]{0:T(1024)} %param.15, f32[8]{0:T(128)S(1)} %add_rsqrt_fusion), kind=kOutput, calls=%fused_computation.57 | convolution fusion | flops 4259840 | bytes 569376 | tf_op jit(solution)/shard_map/dot_general | solution.py:121
  13.4 1.2 %fusion.25 = f32[8,512]{1,0:T(8,128)S(1)} fusion(bf16[2048,512]{1,0:T(8,128)(2,1)S(1)} %copy-done, bf16[8,2048]{1,0:T(8,128)(2,1)} %param.14, f32[2048]{0:T(1024)} %param.15, f32[8]{0:T(128)S(1)} %add_rsqrt_fusion), kind=kOutput, calls=%fused_computation.58 | convolution fusion | flops 16842752 | bytes 2154528 | tf_op jit(solution)/shard_map/dot_general | solution.py:111
  14.6 1.4 %select_reduce_fusion.4 = (s32[8]{0:T(128)}, s32[8]{0:T(128)S(1)}, s32[8]{0:T(128)S(1)}) fusion(s32[64]{0:T(128)} %param.24, s32[64]{0:T(128)} %param.26, s32[8]{0:T(128)S(1)} %iota_add_fusion, s32[8]{0:T(128)S(1)} %dynamic_slice.7, s32[64]{0:T(128)} %param.22), kind=kLoop, calls=%fused_computation.74 | loop fusion | flops 4072 | bytes 928 | tf_op jit(solution)/shard_map/reduce_sum | solution.py:164
  16.0 1.4 %select_reduce_fusion.5 = (s32[8]{0:T(128)}, s32[8]{0:T(128)S(1)}) fusion(s32[8]{0:T(128)} %param.25, s32[8]{0:T(128)S(1)} %iota_add_fusion, s32[8]{0:T(128)} %param.23, s32[8]{0:T(128)S(1)} %get-tuple-element.18), kind=kLoop, calls=%fused_computation.75 | loop fusion | flops 368 | bytes 192 | tf_op jit(solution)/shard_map/reduce_sum | solution.py:162
  17.4 0.1 and_reduce_fusion.2
  17.5 0.7 add_convert_fusion
  18.2 0.1 copy.72
  18.4 0.7 fusion.30
  19.2 0.1 fusion.20
  19.3 4.0 %all-to-all-done = bf16[8,512,128]{1,2,0:T(8,128)(2,1)S(1)} async-done(((bf16[8,512,128]{1,2,0:T(8,128)(2,1)}), bf16[8,512,128]{1,2,0:T(8,128)(2,1)S(1)}, u32[]{:S(2)}, u32[]{:S(2)}) %all-to-all-start) | async-done | bytes 1048608 | tf_op jit(solution)/shard_map/all_to_all | solution.py:60
  23.3 0.1 broadcast_in_dim.217
  23.4 0.8 broadcast_in_dim.218
  24.2 14.8 %all-to-all-start.1 = ((bf16[16,8,512]{2,1,0:T(8,128)(2,1)}), bf16[16,8,512]{2,1,0:T(8,128)(2,1)S(1)}, u32[]{:S(2)}, u32[]{:S(2)}) async-start(bf16[16,8,512]{2,1,0:T(8,128)(2,1)} %broadcast_in_dim.218), calls=%async_computation.1 | async-start | bytes 262144 | tf_op jit(solution)/shard_map/all_to_all | solution.py:60
  38.9 0.8 and_reduce_fusion
  39.7 0.6 slice.140
  40.4 1.1 %copy.96 = bf16[8,1,128,128]{2,3,0,1:T(8,128)(2,1)S(1)} copy(bf16[8,1,128,128]{3,2,1,0:T(8,128)(2,1)} %param.20) | data formatting | bytes 524288 | tf_op args[6]
  41.5 3.9 %copy.101 = bf16[2048,512]{1,0:T(8,128)(2,1)} copy(bf16[2048,512]{0,1:T(8,128)(2,1)} %bitcast.59) | data formatting | bytes 4194304 | tf_op jit(solution)/shard_map/dot_general | solution.py:228
  45.4 0.7 add.102
  46.1 0.7 or.11
  46.8 0.5 copy-done.6
  47.3 0.7 broadcast_and_fusion
  48.0 4.0 %all-to-all-done.1 = bf16[16,8,512]{2,1,0:T(8,128)(2,1)S(1)} async-done(((bf16[16,8,512]{2,1,0:T(8,128)(2,1)}), bf16[16,8,512]{2,1,0:T(8,128)(2,1)S(1)}, u32[]{:S(2)}, u32[]{:S(2)}) %all-to-all-start.1) | async-done | bytes 131104 | tf_op jit(solution)/shard_map/all_to_all | solution.py:60
  52.1 0.2 reshape_reshape.3
  52.3 0.2 copy.74
  52.5 3.7 %fusion = (f32[128,8,8]{0,2,1:T(8,128)S(1)}, f32[8,512,128,8]{2,1,3,0:T(8,128)S(1)}) fusion(pred[128,8,512]{0,2,1:T(8,128)(4,1)S(1)} %broadcast_and_fusion, bf16[128,8,64]{0,2,1:T(8,128)(2,1)S(1)} %copy.74, bf16[8,512,128]{1,2,0:T(8,128)(2,1)} %copy-done.1), kind=kOutput, calls=%fused_computation.3 | convolution fusion | flops 549445632 | bytes 17989632 | tf_op jit(solution)/shard_map/ngd,skd->nsgk/dot_general | solution.py:170
  56.2 4.4 %fusion.2 = (bf16[128,8,64]{0,2,1:T(8,128)(2,1)S(1)}, bf16[128,8,64]{0,2,1:T(8,128)(2,1)S(1)}) fusion(pred[128,8]{0,1:T(8,128)(4,1)S(1)} %copy-done.8, pred[128,8]{0,1:T(8,128)(4,1)S(1)} %copy-done.9, f32[8,512,128,8]{2,1,3,0:T(8,128)S(1)} %get-tuple-element.47, f32[128,8,8]{0,2,1:T(8,128)S(1)} %get-tuple-element.46, ...), kind=kOutput, calls=%fused_computation.7 | convolution fusion | flops 559808512 | bytes 18122752 | tf_op jit(solution)/shard_map/nsgk,skd->nsgd/dot_general | solution.py:24
  60.7 4.1 %convert_reduce_fusion = f32[128,8,8]{0,2,1:T(8,128)S(1)} fusion(f32[128,8,8]{0,2,1:T(8,128)S(1)} %get-tuple-element.46, f32[8,512,128,8]{2,1,3,0:T(8,128)S(1)} %get-tuple-element.47, pred[128,8,512]{0,2,1:T(8,128)(4,1)S(1)} %broadcast_and_fusion), kind=kLoop, calls=%fused_computation.1 | loop fusion | flops 29351936 | bytes 17367040 | tf_op jit(solution)/shard_map/reduce_sum | solution.py:25
  64.8 0.2 copy.76
  65.0 0.2 convert_element_type.171
  65.2 0.2 copy.77
  65.4 0.2 convert_element_type.173
  65.8 0.1 copy.86
  65.9 0.1 copy.87
  66.2 0.1 copy.88
  66.3 0.1 copy.89
  66.4 0.1 copy.90
  66.7 0.1 copy.91
  66.8 0.1 copy.92
  67.1 0.1 copy.93
  67.2 0.1 copy.94
  67.3 0.1 copy.95
  67.4 0.9 concatenate.45
  68.3 8.0 %all-to-all-start.2 = ((bf16[16,8,1152]{2,1,0:T(8,128)(2,1)}), bf16[16,8,1152]{2,1,0:T(8,128)(2,1)S(1)}, u32[]{:S(2)}, u32[]{:S(2)}) async-start(bf16[16,8,1152]{2,1,0:T(8,128)(2,1)} %concatenate.45), calls=%async_computation.2 | async-start | bytes 589824 | tf_op jit(solution)/shard_map/all_to_all | solution.py:67
  76.6 0.2 bitcast_select_fusion.3
  76.8 0.2 fusion.31
  77.0 0.2 convert_reduce_fusion.1
  77.2 18.2 %all-to-all-done.2 = bf16[16,8,1152]{2,1,0:T(8,128)(2,1)S(1)} async-done(((bf16[16,8,1152]{2,1,0:T(8,128)(2,1)}), bf16[16,8,1152]{2,1,0:T(8,128)(2,1)S(1)}, u32[]{:S(2)}, u32[]{:S(2)}) %all-to-all-start.2) | async-done | bytes 294944 | tf_op jit(solution)/shard_map/all_to_all | solution.py:67
  95.7 0.2 fusion.6
  96.0 0.1 reshape.432
  96.0 2.9 %convolution_convert_fusion = bf16[8,4,512]{2,0,1:T(8,128)(2,1)} fusion(bf16[8,512,1]{1,0,2:T(8,128)(2,1)S(1)} %reshape.432, bf16[4,512,512]{2,1,0:T(8,128)(2,1)} %bitcast.58), kind=kOutput, calls=%fused_computation.8 | convolution fusion | flops 16793600 | bytes 2138112 | tf_op jit(solution)/shard_map/dot_general | solution.py:228
  98.9 4.3 %all-to-all-start.3 = ((bf16[8,4,512]{2,0,1:T(8,128)(2,1)}), bf16[8,4,512]{2,0,1:T(8,128)(2,1)S(1)}, u32[]{:S(2)}, u32[]{:S(2)}) async-start(bf16[8,4,512]{2,0,1:T(8,128)(2,1)} %convolution_convert_fusion), calls=%async_computation.3 | async-start | bytes 65536 | tf_op jit(solution)/shard_map/all_to_all | solution.py:230
  103.2 0.7 pad_maximum_fusion.2
  103.8 4.8 %all-to-all-done.3 = bf16[8,4,512]{2,0,1:T(8,128)(2,1)S(1)} async-done(((bf16[8,4,512]{2,0,1:T(8,128)(2,1)}), bf16[8,4,512]{2,0,1:T(8,128)(2,1)S(1)}, u32[]{:S(2)}, u32[]{:S(2)}) %all-to-all-start.3) | async-done | bytes 32800 | tf_op jit(solution)/shard_map/all_to_all | solution.py:230
  108.6 0.6 reduce_sum.177
  (54 shorter events, 1.7 us)
Async XLA Ops:
  0.6 12.8 %copy-start = (bf16[2048,512]{1,0:T(8,128)(2,1)S(1)}, bf16[2048,512]{1,0:T(8,128)(2,1)}, u32[]{:S(2)}) copy-start(bf16[2048,512]{1,0:T(8,128)(2,1)} %param.16) | copy-start | bytes 6291460
  2.9 20.4 %all-to-all-start = ((bf16[8,512,128]{1,2,0:T(8,128)(2,1)}), bf16[8,512,128]{1,2,0:T(8,128)(2,1)S(1)}, u32[]{:S(2)}, u32[]{:S(2)}) async-start(bf16[8,512,128]{1,2,0:T(8,128)(2,1)} %broadcast_in_dim.215), calls=%async_computation | async-start | bytes 2097152 | tf_op jit(solution)/shard_map/all_to_all | solution.py:60
  13.4 26.3 %copy-start.3 = (f32[8,128]{1,0:T(8,128)}, f32[8,128]{1,0:T(8,128)S(1)}, u32[]{:S(2)}) copy-start(f32[8,128]{1,0:T(8,128)S(1)} %fusion.23) | copy-start | bytes 12292
  23.3 23.5 %copy-start.1 = (bf16[8,512,128]{1,2,0:T(8,128)(2,1)}, bf16[8,512,128]{1,2,0:T(8,128)(2,1)S(1)}, u32[]{:S(2)}) copy-start(bf16[8,512,128]{1,2,0:T(8,128)(2,1)S(1)} %all-to-all-done) | copy-start | bytes 3145732
  24.2 27.9 %all-to-all-start.1 = ((bf16[16,8,512]{2,1,0:T(8,128)(2,1)}), bf16[16,8,512]{2,1,0:T(8,128)(2,1)S(1)}, u32[]{:S(2)}, u32[]{:S(2)}) async-start(bf16[16,8,512]{2,1,0:T(8,128)(2,1)} %broadcast_in_dim.218), calls=%async_computation.1 | async-start | bytes 262144 | tf_op jit(solution)/shard_map/all_to_all | solution.py:60
  46.8 0.5 copy-start.6
  47.3 8.9 %copy-start.8 = (pred[128,8]{0,1:T(8,128)(4,1)S(1)}, pred[128,8]{0,1:T(8,128)(4,1)}, u32[]{:S(2)}) copy-start(pred[128,8]{0,1:T(8,128)(4,1)} %get-tuple-element.12) | copy-start | bytes 3076
  47.3 8.9 %copy-start.9 = (pred[128,8]{0,1:T(8,128)(4,1)S(1)}, pred[128,8]{0,1:T(8,128)(4,1)}, u32[]{:S(2)}) copy-start(pred[128,8]{0,1:T(8,128)(4,1)} %get-tuple-element.13) | copy-start | bytes 3076
  52.5 3.7 %copy-start.2 = (bf16[8,512,128]{1,2,0:T(8,128)(2,1)S(1)}, bf16[8,512,128]{1,2,0:T(8,128)(2,1)}, u32[]{:S(2)}) copy-start(bf16[8,512,128]{1,2,0:T(8,128)(2,1)} %copy-done.1) | copy-start | bytes 3145732
  60.6 5.0 %copy-start.7 = (pred[128,8]{0,1:T(8,128)(4,1)S(1)}, pred[128,8]{0,1:T(8,128)(4,1)}, u32[]{:S(2)}) copy-start(pred[128,8]{0,1:T(8,128)(4,1)} %copy-done.6) | copy-start | bytes 3076
  60.6 15.7 %copy-start.5 = (bf16[8,64]{1,0:T(8,128)(2,1)S(1)}, bf16[8,64]{1,0:T(8,128)(2,1)}, u32[]{:S(2)}) copy-start(bf16[8,64]{1,0:T(8,128)(2,1)} %get-tuple-element.40) | copy-start | bytes 3076
  60.6 15.7 %copy-start.10 = (bf16[8,64]{1,0:T(8,128)(2,1)S(1)}, bf16[8,64]{1,0:T(8,128)(2,1)}, u32[]{:S(2)}) copy-start(bf16[8,64]{1,0:T(8,128)(2,1)} %slice.140) | copy-start | bytes 3076
  60.6 15.8 %copy-start.11 = (s32[8]{0:T(128)S(1)}, s32[8]{0:T(128)}, u32[]{:S(2)}) copy-start(s32[8]{0:T(128)} %param.27) | copy-start | bytes 100
  60.7 15.9 %copy-start.4 = (f32[8,128]{1,0:T(8,128)S(1)}, f32[8,128]{1,0:T(8,128)}, u32[]{:S(2)}) copy-start(f32[8,128]{1,0:T(8,128)} %copy-done.3) | copy-start | bytes 12292
  68.3 27.1 %all-to-all-start.2 = ((bf16[16,8,1152]{2,1,0:T(8,128)(2,1)}), bf16[16,8,1152]{2,1,0:T(8,128)(2,1)S(1)}, u32[]{:S(2)}, u32[]{:S(2)}) async-start(bf16[16,8,1152]{2,1,0:T(8,128)(2,1)} %concatenate.45), calls=%async_computation.2 | async-start | bytes 589824 | tf_op jit(solution)/shard_map/all_to_all | solution.py:67
  98.9 9.7 %all-to-all-start.3 = ((bf16[8,4,512]{2,0,1:T(8,128)(2,1)}), bf16[8,4,512]{2,0,1:T(8,128)(2,1)S(1)}, u32[]{:S(2)}, u32[]{:S(2)}) async-start(bf16[8,4,512]{2,0,1:T(8,128)(2,1)} %convolution_convert_fusion), calls=%async_computation.3 | async-start | bytes 65536 | tf_op jit(solution)/shard_map/all_to_all | solution.py:230
